TPU v7x, 32 devices: a whole 2x2x4 slice. The times are simulated.
32 devices in a mesh: dp: 4 (over z), expert: 8 (over y, x, core).
Axes of the slice: x: 2, y: 2, z: 4, core: 2. Of those that a mesh axis runs over, the one named last changes fastest.
Arguments:
- hidden: bfloat16 [3072, 2880], P('expert', 'dp'), may hold values from -6 to 6
- segments: int32 [8, 384], P('expert'), may hold values from 0 to 3, never falling along the last dimension, each value on 1 to 192 neighbouring positions
- request_adapter: int32 [8, 4], P('expert'), may hold values from 0 to 7
- routes: int32 [8, 384, 4], P('expert', 'dp'), may hold values from 0 to 7, all different within a row; in each aligned block of 96 rows (0 to 95, 96 to 191, ..., all dimensions but the last counted through in order) at most 64 rows name the same one
- expert_gates: bfloat16 [8, 384, 4], P('expert', 'dp'), may hold values from 0.049804688 to 0.59765625
- attention_gain: float32 [2880], replicated, may hold values from 0.25 to 1.75
- joined_weight: bfloat16 [2880, 4, 640], P(None, 'dp'), may hold values from -0.109375 to 0.109375
- sinks: float32 [32], P('dp'), may hold values from 0 to 3
- attention_out_weight: bfloat16 [2048, 2880], P('dp'), may hold values from -0.125 to 0.125
- joined_down_maps: bfloat16 [2880, 128], replicated, may hold values from -0.109375 to 0.109375
- joined_up_maps: bfloat16 [128, 4, 640], P(None, 'dp'), may hold values from -0.375 to 0.375
- output_down_maps: bfloat16 [2048, 128], P('dp'), may hold values from -0.125 to 0.125
- output_up_maps: bfloat16 [128, 2880], P(None, 'dp'), may hold values from -0.75 to 0.75
- expert_norm_gain: float32 [2880], replicated, may hold values from 0.25 to 1.75
- expert_gate_weight: bfloat16 [8, 2880, 2880], P('expert', None, 'dp'), may hold values from -0.109375 to 0.109375
- expert_up_weight: bfloat16 [8, 2880, 2880], P('expert', None, 'dp'), may hold values from -0.109375 to 0.109375
- expert_down_weight: bfloat16 [8, 2880, 2880], P('expert', 'dp'), may hold values from -0.109375 to 0.109375
- closing_gain: float32 [2880], replicated, may hold values from 0.25 to 1.75
- vocabulary_weight: bfloat16 [2880, 25600], P(None, ('dp', 'expert')), may hold values from -0.109375 to 0.109375
Outputs:
- hidden_out: bfloat16 [3072, 2880], P('expert', 'dp')
- logits: float32 [32, 25600], P(None, ('dp', 'expert'))
Inputs may be any that keep to these rules, and one draw needn't show every extreme that they name: `segments`: in each column the ids do not fall; each of the 4 requests has 1 to 192 tokens, and one has exactly 192. `routes`: the 4 experts of a token differ. Within the rows of one device (96 consecutive tokens, aligned blocks) no expert is named more than 64 times, and in some blocks one expert is named exactly 64 times.
All inputs are finite; a program needn't handle non-finite values.
Results may differ from a plain program's by a relative error of at most 0.02.
Values may be sent and summed in bfloat16 or wider, within the bound.
No kernel may reach another device: no remote copies, remote signals or barrier semaphores. Data moves between devices by JAX's collectives and lax.ppermute only.
A program may use at most 128 MiB of HBM per device.

v0:
```python
import jax
import jax.numpy as jnp
from jax import lax
from jax.sharding import PartitionSpec as P

HEAD_SIZE = 64
QUERY_GROUP = 8
TOP = 4
ADAPTER_RANK = 16
REQS = 4


epsilon = 1e-05
theta_base = 150000.0
adapter_scale = 2.0
glu_alpha = 1.702


def rms_scale(values, gain_row):
    mean_square = jnp.mean(values * values, axis=-1, keepdims=True)
    return values * lax.rsqrt(mean_square + epsilon) * gain_row


def positions_of(segment_row):
    counter = jnp.arange(segment_row.shape[0], dtype=jnp.int32)
    starting = jnp.concatenate(
        [jnp.ones((1,), dtype=jnp.bool_), segment_row[1:] != segment_row[:-1]]
    )
    first_index = lax.cummax(jnp.where(starting, counter, 0), axis=0)
    return counter - first_index


def adapter_per_token(segment_row, adapter_row):
    hits = segment_row[:, None] == jnp.arange(adapter_row.shape[0], dtype=jnp.int32)[None, :]
    return jnp.sum(jnp.where(hits, adapter_row[None, :], 0), axis=1)


def rotate_heads(values, positions):
    head_dim = values.shape[-1]
    half_dim = head_dim // 2
    frequency = theta_base ** (-2.0 * jnp.arange(half_dim, dtype=jnp.float32) / head_dim)
    angles = positions.astype(jnp.float32)[:, None] * frequency[None, :]
    cosine = jnp.cos(angles)[:, None, :]
    sine_part = jnp.sin(angles)[:, None, :]
    first_half = values[..., :half_dim]
    second_half = values[..., half_dim:]
    return jnp.concatenate(
        [
            first_half * cosine - second_half * sine_part,
            second_half * cosine + first_half * sine_part,
        ],
        axis=-1,
    )


def attend_heads(queries, key_heads, value_heads, segment_row, sink_row):
    tokens_now, kv_now, group_now, head_dim = queries.shape
    scores = jnp.einsum(
        "tkgh,skh->kgts", queries, key_heads, preferred_element_type=jnp.float32
    ) * head_dim ** (-0.5)
    counter = jnp.arange(tokens_now, dtype=jnp.int32)
    allowed = (segment_row[:, None] == segment_row[None, :]) & (
        counter[None, :] <= counter[:, None]
    )
    weights = jnp.where(allowed[None, None], jnp.exp(scores), 0.0)
    totals = jnp.sum(weights, axis=-1, keepdims=True) + jnp.exp(sink_row).reshape(
        kv_now, group_now, 1, 1
    )
    probs = (weights / totals).astype(jnp.bfloat16)
    blended_hidden = jnp.einsum(
        "kgts,skh->tkgh", probs, value_heads, preferred_element_type=jnp.float32
    )
    return blended_hidden.astype(jnp.bfloat16).reshape(tokens_now, kv_now * group_now * head_dim)


def shards(
    hidden,
    segments,
    request_adapter,
    routes,
    expert_gates,
    attention_gain,
    joined_weight,
    sinks,
    attention_out_weight,
    joined_down_maps,
    joined_up_maps,
    output_down_maps,
    output_up_maps,
    expert_norm_gain,
    expert_gate_weight,
    expert_up_weight,
    expert_down_weight,
    closing_gain,
    vocabulary_weight,
):
    groups = lax.axis_size("dp")
    columns = lax.axis_size("expert")
    position_dp = lax.axis_index("dp")
    segment_row = segments[0]
    adapter_row = request_adapter[0]
    col_tokens = segment_row.shape[0]
    gathered_rows = lax.all_gather(hidden, "dp", axis=1, tiled=True)
    width = gathered_rows.shape[1]
    normalized_hidden = rms_scale(gathered_rows.astype(jnp.float32), attention_gain).astype(
        jnp.bfloat16
    )
    joined_projection = jnp.dot(
        normalized_hidden, joined_weight.reshape(width, -1), preferred_element_type=jnp.float32
    )
    reduced_every_adapter = joined_down_maps.shape[1]
    reduced_hidden = jnp.dot(
        normalized_hidden, joined_down_maps, preferred_element_type=jnp.float32
    ).astype(jnp.bfloat16)
    rank_owner = jnp.arange(reduced_every_adapter, dtype=jnp.int32) // ADAPTER_RANK
    adapter_mask = adapter_per_token(segment_row, adapter_row)[:, None] == rank_owner[None, :]
    selected_reduced = jnp.where(adapter_mask, reduced_hidden, jnp.zeros_like(reduced_hidden))
    joined_projection = joined_projection + adapter_scale * jnp.dot(
        selected_reduced,
        joined_up_maps.reshape(reduced_every_adapter, -1),
        preferred_element_type=jnp.float32,
    )
    kv_here = joined_weight.shape[1]
    joined_projection = joined_projection.reshape(col_tokens, kv_here, QUERY_GROUP + 2, HEAD_SIZE)
    positions = positions_of(segment_row)
    queries = rotate_heads(
        joined_projection[:, :, :QUERY_GROUP].reshape(col_tokens, kv_here * QUERY_GROUP, HEAD_SIZE),
        positions,
    )
    queries = queries.astype(jnp.bfloat16).reshape(col_tokens, kv_here, QUERY_GROUP, HEAD_SIZE)
    key_heads = rotate_heads(joined_projection[:, :, QUERY_GROUP], positions).astype(jnp.bfloat16)
    value_heads = joined_projection[:, :, QUERY_GROUP + 1].astype(jnp.bfloat16)
    blended_hidden = attend_heads(queries, key_heads, value_heads, segment_row, sinks)
    partial_out = jnp.dot(blended_hidden, attention_out_weight, preferred_element_type=jnp.float32)
    mine_out = lax.psum_scatter(
        partial_out.astype(jnp.bfloat16), "dp", scatter_dimension=1, tiled=True
    ).astype(jnp.float32)
    output_reduced = lax.psum(
        jnp.dot(blended_hidden, output_down_maps, preferred_element_type=jnp.float32).astype(
            jnp.bfloat16
        ),
        "dp",
    )
    selected_output = jnp.where(adapter_mask, output_reduced, jnp.zeros_like(output_reduced))
    adapter_delta = adapter_scale * jnp.dot(
        selected_output, output_up_maps, preferred_element_type=jnp.float32
    )
    resid = (hidden.astype(jnp.float32) + mine_out + adapter_delta).astype(jnp.bfloat16)
    share = col_tokens // groups
    column_full = lax.all_gather(resid, "dp", axis=1, tiled=True)
    own_rows = lax.dynamic_slice_in_dim(column_full, position_dp * share, share, 0)
    moe_in = rms_scale(
        lax.optimization_barrier(own_rows).astype(jnp.float32), expert_norm_gain
    ).astype(jnp.bfloat16)
    experts = expert_gate_weight.shape[0] * columns
    capacity = 4 * share * TOP // (3 * experts)
    route_flat = routes[0].reshape(-1)
    one_hot = (route_flat[:, None] == jnp.arange(experts, dtype=jnp.int32)[None, :]).astype(
        jnp.int32
    )
    slot_rows = jnp.sum((jnp.cumsum(one_hot, axis=0) - one_hot) * one_hot, axis=1)
    target = route_flat * capacity + slot_rows
    source_rows = jnp.arange(route_flat.shape[0], dtype=jnp.int32) // TOP
    table = jnp.full((experts * capacity,), share, jnp.int32).at[target].set(source_rows)
    padded = jnp.concatenate([moe_in, jnp.zeros((1, width), jnp.bfloat16)], axis=0)
    outgoing = jnp.take(padded, table, axis=0).reshape(experts, capacity, width)
    gate_weight = expert_gate_weight[0]
    up_weight = expert_up_weight[0]
    down_weight = expert_down_weight[0]
    copies = jnp.tile(outgoing, (groups, 1, 1))
    arrived = lax.all_to_all(copies, ("dp", "expert"), split_axis=0, concat_axis=0, tiled=True)
    senders = arrived.shape[0]
    slots_now = arrived.shape[1]
    rows_in = arrived.reshape(-1, width)
    gate_part = jnp.dot(rows_in, gate_weight, preferred_element_type=jnp.float32)
    up_part = jnp.dot(rows_in, up_weight, preferred_element_type=jnp.float32)
    activated = (gate_part * jax.nn.sigmoid(glu_alpha * gate_part) * (up_part + 1.0)).astype(
        jnp.bfloat16
    )
    shares_out = (
        jnp.dot(activated, down_weight, preferred_element_type=jnp.float32)
        .astype(jnp.bfloat16)
        .reshape(senders, slots_now, width)
    )
    answers = lax.all_to_all(shares_out, ("dp", "expert"), split_axis=0, concat_axis=0, tiled=True)
    merged = jnp.sum(
        answers.reshape(groups, columns, capacity, width).astype(jnp.float32), axis=0
    ).astype(jnp.bfloat16)
    picked_out = jnp.take(merged.reshape(experts * capacity, width), target, axis=0).reshape(
        share, TOP, width
    )
    mixture = jnp.einsum(
        "tk,tkd->td", expert_gates[0], picked_out, preferred_element_type=jnp.float32
    )
    moe_rounded = lax.optimization_barrier(mixture.astype(jnp.bfloat16))
    finished = (own_rows.astype(jnp.float32) + moe_rounded.astype(jnp.float32)).astype(jnp.bfloat16)
    hidden_out = lax.all_to_all(finished, "dp", split_axis=1, concat_axis=0, tiled=True)
    counter = jnp.arange(col_tokens, dtype=jnp.int32)
    request_ids = jnp.arange(REQS, dtype=jnp.int32)
    last_index = jnp.max(
        jnp.where(segment_row[None, :] == request_ids[:, None], counter[None, :], -1), axis=1
    )
    local_index = last_index - position_dp * share
    inside = (local_index >= 0) & (local_index < share)
    chosen = jnp.take(finished, jnp.clip(local_index, 0, share - 1), axis=0)
    chosen = jnp.where(inside[:, None], chosen, jnp.zeros_like(chosen))
    ends = rms_scale(chosen.astype(jnp.float32), closing_gain).astype(jnp.bfloat16)
    spread_rows = lax.all_gather(ends, ("dp", "expert"), axis=0, tiled=True)
    tail_rows = jnp.sum(
        spread_rows.reshape(groups, columns * REQS, width).astype(jnp.float32), axis=0
    ).astype(jnp.bfloat16)
    logits = jnp.dot(tail_rows, vocabulary_weight, preferred_element_type=jnp.float32)
    return (hidden_out, logits)


def solution(mesh):
    in_specs = (
        P("expert", "dp"),
        P("expert", None),
        P("expert", None),
        P("expert", "dp", None),
        P("expert", "dp", None),
        P(),
        P(None, "dp", None),
        P("dp"),
        P("dp", None),
        P(),
        P(None, "dp", None),
        P("dp", None),
        P(None, "dp"),
        P(),
        P("expert", None, "dp"),
        P("expert", None, "dp"),
        P("expert", "dp", None),
        P(),
        P(None, ("dp", "expert")),
    )
    out_specs = (P("expert", "dp"), P(None, ("dp", "expert")))
    return jax.shard_map(shards, mesh=mesh, in_specs=in_specs, out_specs=out_specs, check_vma=False)
```

profile of v0, /device:TPU:0, one launch (start us, length us, event | category | flops | bytes accessed | tf_op | source)
XLA Modules:
  0.0 916.7 jit_solution(5084641404369946867)
XLA Ops:
  7.2 0.7 all-gather.4.cloned.1.call-update
  8.0 0.8 reduce.4
  8.8 0.8 compare_reduce_fusion
  9.7 0.3 reduce-window.15
  10.1 0.7 exp.18
  10.8 0.1 slice_reduce_fusion.1
  10.9 0.7 select_reduce_fusion.1
  11.7 0.3 multiply_cosine_fusion
  12.0 0.1 fusion.30
  12.1 48.3 %all-gather.4.cloned.1.call-done = bf16[384,2880]{0,1:T(8,128)(2,1)} async-done(((bf16[384,720]{0,1:T(8,128)(2,1)}), bf16[384,2880]{0,1:T(8,128)(2,1)}) %all-gather.4.cloned.1.call-update) | async-done | bytes 2211856 | tf_op jit(solution)/shard_map/all_gather | solution.py:103
  60.4 2.2 fusion
  62.6 5.9 fusion.11
  68.5 4.8 fusion.21
  73.3 2.5 copy.59
  75.8 1.2 slice_bitcast_fusion
  77.0 0.9 slice_bitcast_fusion.1
  77.9 0.3 fusion.59
  78.1 0.1 subtract_convert_fusion
  78.3 1.3 fusion.10
  79.6 2.2 fusion.23
  81.9 0.7 copy-done.3
  82.6 1.0 convolution_convert_fusion.2
  83.7 4.1 convolution_convert_fusion.1
  87.9 29.0 %all-reduce.3.cloned.1.call-done = bf16[384,128]{1,0:T(8,128)(2,1)} async-done(((bf16[384,128]{1,0:T(8,128)(2,1)}), bf16[384,128]{1,0:T(8,128)(2,1)}) %all-reduce.3.cloned.1.call-update) | async-done | bytes 98320 | tf_op jit(solution)/shard_map/psum | solution.py:138
  116.8 48.0 %reduce-scatter.2.cloned.1.call-done = bf16[384,720]{0,1:T(8,128)(2,1)} async-done(((bf16[384,2880]{0,1:T(8,128)(2,1)}), bf16[384,720]{0,1:T(8,128)(2,1)}) %reduce-scatter.2.cloned.1.call-update) | async-done | bytes 552976 | tf_op jit(solution)/shard_map/reduce_scatter | solution.py:135
  164.9 2.4 fusion.22
  167.6 0.1 reshape_squeeze.3
  167.7 0.9 reduce-window.19
  168.6 0.2 slice_reduce_fusion
  168.8 0.1 copy.65
  169.0 0.1 mul.232
  169.2 3.1 scatter_custom_fusion
  172.4 42.6 %all-gather.6.cloned.1.call-done = bf16[384,2880]{0,1:T(8,128)(2,1)} async-done(((bf16[384,720]{0,1:T(8,128)(2,1)}), bf16[384,2880]{0,1:T(8,128)(2,1)}) %all-gather.6.cloned.1.call-update) | async-done | bytes 2211856 | tf_op jit(solution)/shard_map/all_gather | solution.py:150
  215.0 1.7 constant_dynamic-slice_fusion
  216.7 0.4 fusion.17
  217.1 0.4 fusion.19
  217.5 0.3 copy.77
  217.9 3.7 gather_fusion
  221.6 2.2 broadcast_select_fusion
  223.8 6.0 tile.8
  229.8 266.5 %all_to_all.29 = bf16[32,64,2880]{2,1,0:T(8,128)(2,1)} all-to-all(bf16[32,64,2880]{2,1,0:T(8,128)(2,1)} %bitcast.115), channel_id=1, replica_groups=mesh['dp'=4,'expert'=8] {'dp','expert'}, dimensions={0} | all-to-all | bytes 23592960 | tf_op jit(solution)/shard_map/all_to_all | solution.py:171
  496.3 15.1 %fusion.4 = f32[2048,720]{0,1:T(8,128)} fusion(bf16[2048,2880]{1,0:T(8,128)(2,1)} %bitcast.26, bf16[1,2880,720]{1,2,0:T(8,128)(2,1)} %param.34), kind=kOutput, calls=%fused_computation.15 | convolution fusion | flops 8493465600 | bytes 21841920 | tf_op jit(solution)/shard_map/dot_general | solution.py:176
  511.4 26.6 %convolution_convert_fusion = bf16[2048,2880]{0,1:T(8,128)(2,1)} fusion(bf16[1,720,2880]{2,1,0:T(8,128)(2,1)} %param.35, f32[2048,720]{0,1:T(8,128)} %fusion.4, bf16[2048,2880]{1,0:T(8,128)(2,1)} %bitcast.26, bf16[1,2880,720]{1,2,0:T(8,128)(2,1)} %param.33), kind=kOutput, calls=%fused_computation.4 | convolution fusion | flops 17004625920 | bytes 37785600 | tf_op jit(solution)/shard_map/dot_general | solution.py:181
  538.0 16.3 %copy.67 = bf16[2048,2880]{1,0:T(8,128)(2,1)} copy(bf16[2048,2880]{0,1:T(8,128)(2,1)} %convolution_convert_fusion) | data formatting | bytes 23592960 | tf_op jit(solution)/shard_map/convert_element_type | solution.py:182
  554.4 4.1 all-to-all-start.1
  558.7 0.1 copy.64
  558.9 0.1 select_reduce_fusion
  559.1 266.6 %all-to-all-done.1 = bf16[32,64,2880]{2,1,0:T(8,128)(2,1)} async-done(((bf16[32,64,2880]{2,1,0:T(8,128)(2,1)}), bf16[32,64,2880]{2,1,0:T(8,128)(2,1)}, u32[]{:S(2)}, u32[]{:S(2)}) %all-to-all-start.1) | async-done | bytes 11796512 | tf_op jit(solution)/shard_map/all_to_all | solution.py:185
  825.7 6.8 reduce_sum.89
  832.5 3.5 gather_fusion.1
  836.0 2.6 gather.19
  838.6 4.7 multiply_reduce_fusion
  843.3 0.4 copy.75
  843.6 1.7 add_convert_fusion
  845.3 0.3 copy.69
  845.7 0.6 gather_fusion.2
  846.2 0.2 fusion.55
  846.5 1.1 copy.68
  847.6 3.5 all-to-all-start.2
  851.2 49.2 %all-gather = bf16[32,4,2880]{2,1,0:T(4,128)(2,1)} all-gather(bf16[1,4,2880]{2,1,0:T(4,128)(2,1)S(1)} %fusion.60), channel_id=1, replica_groups=mesh['dp'=4,'expert'=8] {'dp','expert'}, dimensions={0}, use_global_device_ids=true | all-gather | bytes 760320 | tf_op jit(solution)/shard_map/all_gather | solution.py:208
  900.4 2.3 reshape.444
  902.7 2.0 reduce_sum.91
  904.6 4.5 fusion.79
  909.1 1.0 copy.70
  (62 shorter events, 1.6 us)
Async XLA Ops:
  7.2 76.5 %copy-start = (bf16[512,2880]{0,1:T(8,128)(2,1)S(1)}, bf16[512,2880]{0,1:T(8,128)(2,1)}, u32[]{:S(2)}) copy-start(bf16[512,2880]{0,1:T(8,128)(2,1)} %param.27) | copy-start | bytes 8847364
  7.2 53.2 %all-gather.4.cloned.1.call-start = ((), (), s32[]{:S(2)}) async-start(), calls=%async_computation.4 | async-start | bytes 2764800 | tf_op jit(solution)/shard_map/all_gather | solution.py:103
  7.9 108.9 %all-reduce.3.cloned.1.call-start = ((), (), s32[]{:S(2)}) async-start(), calls=%async_computation.6 | async-start | bytes 196608 | tf_op jit(solution)/shard_map/psum | solution.py:138
  62.6 6.0 copy-start.9
  62.6 6.0 copy-start.10
  79.6 3.0 copy-start.4
  81.9 0.8 copy-start.3
  83.6 81.3 %copy-start.2 = (bf16[384,720]{0,1:T(8,128)(2,1)S(1)}, bf16[384,720]{0,1:T(8,128)(2,1)}, u32[]{:S(2)}) copy-start(bf16[384,720]{0,1:T(8,128)(2,1)} %param.19) | copy-start | bytes 1658884
  83.6 81.3 %reduce-scatter.2.cloned.1.call-start = ((), (), s32[]{:S(2)}) async-start(), calls=%async_computation.5 | async-start | bytes 2764800 | tf_op jit(solution)/shard_map/reduce_scatter | solution.py:135
  87.8 79.6 %copy-start.5 = (s32[1,96,4]{1,2,0:T(4,128)S(1)}, s32[1,96,4]{1,2,0:T(4,128)}, u32[]{:S(2)}) copy-start(s32[1,96,4]{1,2,0:T(4,128)} %param.22) | copy-start | bytes 4612
  87.8 129.3 %copy-start.6 = (f32[2880]{0:T(1024)S(1)}, f32[2880]{0:T(1024)}, u32[]{:S(2)}) copy-start(f32[2880]{0:T(1024)} %param.32) | copy-start | bytes 34564
  87.8 127.2 %all-gather.6.cloned.1.call-start = ((), (), s32[]{:S(2)}) async-start(), calls=%async_computation.7 | async-start | bytes 2764800 | tf_op jit(solution)/shard_map/all_gather | solution.py:150
  554.4 4.4 copy-start.8
  554.4 271.3 %all-to-all-start.1 = ((bf16[32,64,2880]{2,1,0:T(8,128)(2,1)}), bf16[32,64,2880]{2,1,0:T(8,128)(2,1)}, u32[]{:S(2)}, u32[]{:S(2)}) async-start(bf16[32,64,2880]{2,1,0:T(8,128)(2,1)} %bitcast.114), calls=%async_computation.2 | async-start | bytes 24117248 | tf_op jit(solution)/shard_map/all_to_all | solution.py:185
  843.2 7.8 copy-start.7
  847.6 61.5 %all-to-all-start.2 = ((bf16[96,4,720]{2,0,1:T(8,128)(2,1)}), bf16[96,4,720]{2,0,1:T(8,128)(2,1)S(1)}, u32[]{:S(2)}, u32[]{:S(2)}) async-start(bf16[96,4,720]{2,0,1:T(8,128)(2,1)} %copy.68), calls=%async_computation.3 | async-start | bytes 1179648 | tf_op jit(solution)/shard_map/all_to_all | solution.py:197
  851.2 59.0 %copy-start.1 = (bf16[512,2880]{0,1:T(8,128)(2,1)S(1)}, bf16[512,2880]{0,1:T(8,128)(2,1)}, u32[]{:S(2)}) copy-start(bf16[512,2880]{0,1:T(8,128)(2,1)} %param.27) | copy-start | bytes 8847364
Sparse Core Ops, SparseCore 0:
  9.6 50.7 all-gather.3
  83.7 33.0 all-reduce.2
  119.3 45.5 reduce-scatter.1
  167.5 47.4 all-gather.5
where the time goes:
time: 918 us; the launch traced here: 917 us
  waiting for transfers between devices  435 us (47%)
  blocking collectives  316 us (34%)
  matrix products  68 us (7%)
  local copies, waits for them, and re-layouts  50.3 us (5%)
  other arithmetic  25.7 us (3%)
  between operations  14.1 us (2%)
    all_to_all x1, waiting for transfers between devices, shards(): lax.all_to_all(shares_out, ('dp', 'expert'), split_axis=0, concat_axis=0,...  267 us
    all_to_all x1, blocking collectives, shards(): lax.all_to_all(copies, ('dp', 'expert'), split_axis=0, concat_axis=0, til...  266 us
    all_gather x1, blocking collectives, shards(): spread_rows = lax.all_gather(ends, ('dp', 'expert'), axis=0, tiled=True)  49.2 us
    all_gather x1, waiting for transfers between devices, shards(): gathered_rows = lax.all_gather(hidden, 'dp', axis=1, tiled=True)  48.3 us
    reduce_scatter x1, waiting for transfers between devices, shards(): lax.psum_scatter(partial_out.astype(jnp.bfloat16), 'dp', scatter_dimensio...  48 us
    all_gather x1, waiting for transfers between devices, shards(): column_full = lax.all_gather(resid, 'dp', axis=1, tiled=True)  42.6 us
    psum x1, waiting for transfers between devices, shards(): lax.psum(jnp.dot(blended_hidden, output_down_maps, preferred_element_type...  29 us
    dot_general x1, matrix products, shards(): jnp.dot(activated, down_weight, preferred_element_type=jnp.float32)  26.6 us
  transfers between devices with their start and end apart: 6, of which 5 were waited for; matrix products, arithmetic and copies ran while one was open for 2% of the time, Pallas kernels for 0%

commit v1 on v0

--- a/solution.py
+++ b/solution.py
@@ -146,31 +146,28 @@
         selected_output, output_up_maps, preferred_element_type=jnp.float32
     )
     resid = (hidden.astype(jnp.float32) + mine_out + adapter_delta).astype(jnp.bfloat16)
+    column_full = lax.all_gather(resid, "dp", axis=1, tiled=True)
+    moe_in = rms_scale(column_full.astype(jnp.float32), expert_norm_gain).astype(jnp.bfloat16)
     share = col_tokens // groups
-    column_full = lax.all_gather(resid, "dp", axis=1, tiled=True)
-    own_rows = lax.dynamic_slice_in_dim(column_full, position_dp * share, share, 0)
-    moe_in = rms_scale(
-        lax.optimization_barrier(own_rows).astype(jnp.float32), expert_norm_gain
-    ).astype(jnp.bfloat16)
     experts = expert_gate_weight.shape[0] * columns
     capacity = 4 * share * TOP // (3 * experts)
-    route_flat = routes[0].reshape(-1)
+    col_capacity = groups * capacity
+    route_col = lax.all_gather(routes[0], "dp", axis=0, tiled=True)
+    gates_col = lax.all_gather(expert_gates[0], "dp", axis=0, tiled=True)
+    route_flat = route_col.reshape(-1)
     one_hot = (route_flat[:, None] == jnp.arange(experts, dtype=jnp.int32)[None, :]).astype(
         jnp.int32
     )
     slot_rows = jnp.sum((jnp.cumsum(one_hot, axis=0) - one_hot) * one_hot, axis=1)
-    target = route_flat * capacity + slot_rows
+    target = route_flat * col_capacity + slot_rows
     source_rows = jnp.arange(route_flat.shape[0], dtype=jnp.int32) // TOP
-    table = jnp.full((experts * capacity,), share, jnp.int32).at[target].set(source_rows)
+    table = jnp.full((experts * col_capacity,), col_tokens, jnp.int32).at[target].set(source_rows)
     padded = jnp.concatenate([moe_in, jnp.zeros((1, width), jnp.bfloat16)], axis=0)
-    outgoing = jnp.take(padded, table, axis=0).reshape(experts, capacity, width)
+    outgoing = jnp.take(padded, table, axis=0).reshape(experts, col_capacity, width)
     gate_weight = expert_gate_weight[0]
     up_weight = expert_up_weight[0]
     down_weight = expert_down_weight[0]
-    copies = jnp.tile(outgoing, (groups, 1, 1))
-    arrived = lax.all_to_all(copies, ("dp", "expert"), split_axis=0, concat_axis=0, tiled=True)
-    senders = arrived.shape[0]
-    slots_now = arrived.shape[1]
+    arrived = lax.all_to_all(outgoing, "expert", split_axis=0, concat_axis=0, tiled=True)
     rows_in = arrived.reshape(-1, width)
     gate_part = jnp.dot(rows_in, gate_weight, preferred_element_type=jnp.float32)
     up_part = jnp.dot(rows_in, up_weight, preferred_element_type=jnp.float32)
@@ -180,35 +177,34 @@
     shares_out = (
         jnp.dot(activated, down_weight, preferred_element_type=jnp.float32)
         .astype(jnp.bfloat16)
-        .reshape(senders, slots_now, width)
-    )
-    answers = lax.all_to_all(shares_out, ("dp", "expert"), split_axis=0, concat_axis=0, tiled=True)
-    merged = jnp.sum(
-        answers.reshape(groups, columns, capacity, width).astype(jnp.float32), axis=0
-    ).astype(jnp.bfloat16)
-    picked_out = jnp.take(merged.reshape(experts * capacity, width), target, axis=0).reshape(
-        share, TOP, width
+        .reshape(experts, col_capacity, width)
+    )
+    answers = lax.all_to_all(shares_out, "expert", split_axis=0, concat_axis=0, tiled=True)
+    picked_out = jnp.take(answers.reshape(experts * col_capacity, width), target, axis=0).reshape(
+        col_tokens, TOP, width
     )
     mixture = jnp.einsum(
-        "tk,tkd->td", expert_gates[0], picked_out, preferred_element_type=jnp.float32
-    )
-    moe_rounded = lax.optimization_barrier(mixture.astype(jnp.bfloat16))
-    finished = (own_rows.astype(jnp.float32) + moe_rounded.astype(jnp.float32)).astype(jnp.bfloat16)
-    hidden_out = lax.all_to_all(finished, "dp", split_axis=1, concat_axis=0, tiled=True)
+        "tk,tkd->td", gates_col, picked_out, preferred_element_type=jnp.float32
+    )
+    moe_part = lax.psum_scatter(
+        mixture.astype(jnp.bfloat16), "dp", scatter_dimension=1, tiled=True
+    )
+    moe_rounded = moe_part.astype(jnp.float32).astype(jnp.bfloat16)
+    hidden_out = (resid.astype(jnp.float32) + moe_rounded.astype(jnp.float32)).astype(jnp.bfloat16)
     counter = jnp.arange(col_tokens, dtype=jnp.int32)
     request_ids = jnp.arange(REQS, dtype=jnp.int32)
     last_index = jnp.max(
         jnp.where(segment_row[None, :] == request_ids[:, None], counter[None, :], -1), axis=1
     )
-    local_index = last_index - position_dp * share
-    inside = (local_index >= 0) & (local_index < share)
-    chosen = jnp.take(finished, jnp.clip(local_index, 0, share - 1), axis=0)
-    chosen = jnp.where(inside[:, None], chosen, jnp.zeros_like(chosen))
-    ends = rms_scale(chosen.astype(jnp.float32), closing_gain).astype(jnp.bfloat16)
-    spread_rows = lax.all_gather(ends, ("dp", "expert"), axis=0, tiled=True)
-    tail_rows = jnp.sum(
-        spread_rows.reshape(groups, columns * REQS, width).astype(jnp.float32), axis=0
-    ).astype(jnp.bfloat16)
+    chosen = jnp.take(hidden_out, jnp.clip(last_index, 0, col_tokens - 1), axis=0)
+    spread_rows = lax.all_gather(chosen, ("dp", "expert"), axis=0, tiled=True)
+    quarter = chosen.shape[1]
+    tail_full = (
+        spread_rows.reshape(groups, columns * REQS, quarter)
+        .transpose(1, 0, 2)
+        .reshape(columns * REQS, groups * quarter)
+    )
+    tail_rows = rms_scale(tail_full.astype(jnp.float32), closing_gain).astype(jnp.bfloat16)
     logits = jnp.dot(tail_rows, vocabulary_weight, preferred_element_type=jnp.float32)
     return (hidden_out, logits)
 

time: 918 us -> 775 us (0.84)
  waiting for transfers between devices: 435 us -> 309 us
  blocking collectives: 316 us -> 203 us
  local copies, waits for them, and re-layouts: 50.3 us -> 131 us
  other arithmetic: 25.7 us -> 43.1 us
    all_to_all x2 -> x1, waiting for transfers between devices: 267 us -> 116 us  [shards(): lax.all_to_all(shares_out, 'expert', split_axis=0, concat_axis=0, tiled=T...]
    all_to_all x1, blocking collectives: 266 us -> 134 us  [shards(): lax.all_to_all(outgoing, 'expert', split_axis=0, concat_axis=0, tiled=True)]
    gather x4 -> x5, local copies, waits for them, and re-layouts: 10.3 us -> 63.6 us  [the longest x2 35.8 us: shards(): jnp.take(answers.reshape(experts * col_capacity, width), target, axis=0)]
    reduce_scatter x0 -> x1, waiting for transfers between devices: none -> 43 us  [shards(): lax.psum_scatter(mixture.astype(jnp.bfloat16), 'dp', scatter_dimension=1,...]
    all_to_all x1 -> x2, local copies, waits for them, and re-layouts: 1.12 us -> 32.5 us  [the longest x1 16.3 us: shards(): lax.all_to_all(outgoing, 'expert', split_axis=0, concat_axis=0, tiled=True)]
    all_gather x1 -> x3, blocking collectives: 49.2 us -> 68.7 us  [the longest x1 40.3 us: shards(): spread_rows = lax.all_gather(chosen, ('dp', 'expert'), axis=0, tiled=True)]
    all_gather x1, waiting for transfers between devices: 42.6 us -> 23.9 us  [shards(): column_full = lax.all_gather(resid, 'dp', axis=1, tiled=True)]
    unnamed x4 -> x5, other arithmetic: 5.54 us -> 21.9 us
  transfers between devices with their start and end apart: 6 -> 6, of which waited for: 5 -> 6; matrix products, arithmetic and copies ran while one was open for 2% -> 2% of each run, Pallas kernels for 0% -> 0%
where the time goes in v1:
time: 775 us; the launch traced here: 773 us
  waiting for transfers between devices  309 us (40%)
  blocking collectives  203 us (26%)
  local copies, waits for them, and re-layouts  131 us (17%)
  matrix products  67.9 us (9%)
  other arithmetic  43.1 us (6%)
  between operations  14.1 us (2%)
    all_to_all x1, blocking collectives, shards(): lax.all_to_all(outgoing, 'expert', split_axis=0, concat_axis=0, tiled=True)  134 us
    all_to_all x1, waiting for transfers between devices, shards(): lax.all_to_all(shares_out, 'expert', split_axis=0, concat_axis=0, tiled=T...  116 us
    all_gather x1, waiting for transfers between devices, shards(): gathered_rows = lax.all_gather(hidden, 'dp', axis=1, tiled=True)  48.1 us
    reduce_scatter x1, waiting for transfers between devices, shards(): lax.psum_scatter(partial_out.astype(jnp.bfloat16), 'dp', scatter_dimensio...  48 us
    reduce_scatter x1, waiting for transfers between devices, shards(): lax.psum_scatter(mixture.astype(jnp.bfloat16), 'dp', scatter_dimension=1,...  43 us
    all_gather x1, blocking collectives, shards(): spread_rows = lax.all_gather(chosen, ('dp', 'expert'), axis=0, tiled=True)  40.3 us
    gather x2, local copies, waits for them, and re-layouts, shards(): jnp.take(answers.reshape(experts * col_capacity, width), target, axis=0)  35.8 us
    psum x1, waiting for transfers between devices, shards(): lax.psum(jnp.dot(blended_hidden, output_down_maps, preferred_element_type...  29 us
  transfers between devices with their start and end apart: 6, of which 6 were waited for; matrix products, arithmetic and copies ran while one was open for 2% of the time, Pallas kernels for 0%

profile of v1, /device:TPU:0, one launch (start us, length us, event | category | flops | bytes accessed | tf_op | source)
XLA Modules:
  0.0 773.1 jit_solution(7064949755682146424)
XLA Ops:
  7.2 0.7 all-gather.6.cloned.1.call-update
  8.0 0.8 reduce.7
  8.8 0.8 compare_reduce_fusion
  9.7 0.3 reduce-window.15
  10.1 0.7 exp.18
  10.9 0.9 select_reduce_fusion
  11.9 0.3 multiply_cosine_fusion
  12.3 48.1 %all-gather.6.cloned.1.call-done = bf16[384,2880]{0,1:T(8,128)(2,1)} async-done(((bf16[384,720]{0,1:T(8,128)(2,1)}), bf16[384,2880]{0,1:T(8,128)(2,1)}) %all-gather.6.cloned.1.call-update) | async-done | bytes 2211856 | tf_op jit(solution)/shard_map/all_gather | solution.py:103
  60.4 2.2 fusion
  62.6 5.9 fusion.14
  68.5 4.8 fusion.21
  73.3 2.5 copy.58
  75.8 1.2 slice_bitcast_fusion
  77.0 0.9 slice_bitcast_fusion.1
  77.9 0.3 fusion.63
  78.3 1.3 fusion.13
  79.6 2.3 fusion.23
  81.9 0.7 copy-done.4
  82.6 1.0 convolution_convert_fusion.2
  83.7 4.1 convolution_convert_fusion.1
  87.9 29.0 %all-reduce.3.cloned.1.call-done = bf16[384,128]{1,0:T(8,128)(2,1)} async-done(((bf16[384,128]{1,0:T(8,128)(2,1)}), bf16[384,128]{1,0:T(8,128)(2,1)}) %all-reduce.3.cloned.1.call-update) | async-done | bytes 98320 | tf_op jit(solution)/shard_map/psum | solution.py:138
  116.8 48.0 %reduce-scatter.3.cloned.1.call-done = bf16[384,720]{0,1:T(8,128)(2,1)} async-done(((bf16[384,2880]{0,1:T(8,128)(2,1)}), bf16[384,720]{0,1:T(8,128)(2,1)}) %reduce-scatter.3.cloned.1.call-update) | async-done | bytes 552976 | tf_op jit(solution)/shard_map/reduce_scatter | solution.py:135
  164.9 2.4 fusion.22
  167.5 14.5 %all-gather = s32[1,384,4]{2,1,0:T(8,128)S(1)} all-gather(s32[1,96,4]{2,1,0:T(8,128)S(1)} %copy.60), channel_id=2, replica_groups=mesh['dp'=4,'expert'=8] {'dp'}, dimensions={1}, use_global_device_ids=true | all-gather | bytes 7680 | tf_op jit(solution)/shard_map/all_gather | solution.py:155
  182.0 0.1 eq.94
  182.2 0.1 reshape.421
  182.3 2.3 reduce-window.19
  184.6 0.3 slice_reduce_fusion
  184.9 0.2 reduce-window.24
  185.1 0.2 mul.226
  185.4 6.2 scatter_custom_fusion
  191.7 23.9 %all-gather.8.cloned.1.call-done = bf16[384,2880]{0,1:T(8,128)(2,1)} async-done(((bf16[384,720]{0,1:T(8,128)(2,1)}), bf16[384,2880]{0,1:T(8,128)(2,1)}) %all-gather.8.cloned.1.call-update) | async-done | bytes 2211856 | tf_op jit(solution)/shard_map/all_gather | solution.py:149
  215.5 2.2 fusion.3
  217.7 2.2 fusion.5
  219.9 2.6 copy.76
  222.5 1.8 concatenate.31.clone
  224.3 12.0 %gather_fusion = bf16[2048,2880]{1,0:T(8,128)(2,1)} fusion(bf16[385,2880]{1,0:T(8,128)(2,1)S(1)} %concatenate.31.clone, s32[2048]{0:T(1024)S(1)} %fusion.67), kind=kCustom, calls=%fused_computation | custom fusion | bytes 23601152 | tf_op jit(solution)/shard_map/jit(_take)/gather | solution.py:166
  236.3 15.2 %copy.62 = bf16[8,256,2880]{1,2,0:T(8,128)(2,1)} copy(bf16[8,256,2880]{2,1,0:T(8,128)(2,1)} %bitcast.123) | data formatting | bytes 23592960 | tf_op jit(solution)/shard_map/jit(_take)/gather | solution.py:166
  251.5 6.5 broadcast_select_fusion
  258.0 134.2 %all_to_all.10 = bf16[8,256,2880]{1,2,0:T(8,128)(2,1)} all-to-all(bf16[8,256,2880]{1,2,0:T(8,128)(2,1)S(1)} %broadcast_select_fusion), channel_id=1, replica_groups=mesh['dp'=4,'expert'=8] {'expert'}, dimensions={0} | all-to-all | bytes 23592960 | tf_op jit(solution)/shard_map/all_to_all | solution.py:170
  392.2 16.3 %copy.63 = bf16[8,256,2880]{2,1,0:T(8,128)(2,1)} copy(bf16[8,256,2880]{1,2,0:T(8,128)(2,1)} %all_to_all.10) | data formatting | bytes 23592960 | tf_op jit(solution)/shard_map/all_to_all | solution.py:170
  408.4 15.1 %fusion.7 = f32[2048,720]{0,1:T(8,128)} fusion(bf16[2048,2880]{1,0:T(8,128)(2,1)} %bitcast.125, bf16[1,2880,720]{1,2,0:T(8,128)(2,1)} %param.34), kind=kOutput, calls=%fused_computation.22 | convolution fusion | flops 8493465600 | bytes 21841920 | tf_op jit(solution)/shard_map/dot_general | solution.py:173
  423.6 26.6 %convolution_convert_fusion = bf16[2048,2880]{0,1:T(8,128)(2,1)} fusion(bf16[1,720,2880]{2,1,0:T(8,128)(2,1)} %param.35, f32[2048,720]{0,1:T(8,128)} %fusion.7, bf16[2048,2880]{1,0:T(8,128)(2,1)} %bitcast.126, bf16[1,2880,720]{1,2,0:T(8,128)(2,1)} %param.33), kind=kOutput, calls=%fused_computation.7 | convolution fusion | flops 17004625920 | bytes 37785600 | tf_op jit(solution)/shard_map/dot_general | solution.py:178
  450.2 10.1 %copy.82 = bf16[360,8,8,256]{3,2,0,1:T(8,128)(2,1)} copy(bf16[360,8,8,256]{3,2,1,0:T(8,128)(2,1)} %bitcast.127) | data formatting | bytes 23592960 | tf_op jit(solution)/shard_map/reshape | solution.py:180
  460.3 5.5 all-to-all-start.1
  465.9 0.2 reduce_sum.69
  466.1 0.1 copy.66
  466.2 13.8 %all-gather.1 = bf16[1,384,4]{2,0,1:T(2,128)(2,1)S(1)} all-gather(bf16[1,96,4]{2,0,1:T(2,128)(2,1)S(1)} %copy.66), channel_id=3, replica_groups=mesh['dp'=4,'expert'=8] {'dp'}, dimensions={1}, use_global_device_ids=true | all-gather | bytes 3840 | tf_op jit(solution)/shard_map/all_gather | solution.py:156
  480.2 0.1 copy.75
  480.4 116.0 %all-to-all-done.1 = bf16[8,256,2880]{1,2,0:T(8,128)(2,1)} async-done(((bf16[8,256,2880]{1,2,0:T(8,128)(2,1)}), bf16[8,256,2880]{1,2,0:T(8,128)(2,1)}, u32[]{:S(2)}, u32[]{:S(2)}) %all-to-all-start.1) | async-done | bytes 11796512 | tf_op jit(solution)/shard_map/all_to_all | solution.py:182
  596.4 16.3 %copy.65 = bf16[8,256,2880]{2,1,0:T(8,128)(2,1)} copy(bf16[8,256,2880]{1,2,0:T(8,128)(2,1)} %all-to-all-done.1) | data formatting | bytes 23592960 | tf_op jit(solution)/shard_map/all_to_all | solution.py:182
  612.6 22.9 %gather_fusion.1 = bf16[1536,2880]{1,0:T(8,128)(2,1)} fusion(bf16[2048,2880]{1,0:T(8,128)(2,1)} %bitcast.122, s32[2048]{0:T(1024)S(1)} %pad_clamp_fusion), kind=kCustom, calls=%fused_computation.1 | custom fusion | bytes 17700864 | tf_op jit(solution)/shard_map/jit(_take)/gather | solution.py:183
  635.5 12.9 %gather.19 = bf16[384,4,2880]{2,1,0:T(4,128)(2,1)} reshape(bf16[1536,2880]{1,0:T(8,128)(2,1)} %gather_fusion.1) | data formatting | bytes 17694720 | tf_op jit(solution)/shard_map/jit(_take)/gather | solution.py:183
  648.4 20.9 %multiply_reduce_fusion = bf16[384,2880]{1,0:T(8,128)(2,1)S(1)} fusion(f32[384,4]{1,0:T(8,128)S(1)} %copy.75, bf16[384,4,2880]{2,1,0:T(4,128)(2,1)} %gather.19, pred[384,4]{1,0:T(8,128)(4,1)S(1)} %compare_and_fusion), kind=kLoop, calls=%fused_computation.4 | loop fusion | flops 16588800 | bytes 11066880
  669.4 2.5 copy.74
  672.1 43.0 %reduce-scatter.5.cloned.1.call-done = bf16[384,720]{0,1:T(8,128)(2,1)} async-done(((bf16[384,2880]{0,1:T(8,128)(2,1)}), bf16[384,720]{0,1:T(8,128)(2,1)}) %reduce-scatter.5.cloned.1.call-update) | async-done | bytes 552976 | tf_op jit(solution)/shard_map/reduce_scatter | solution.py:189
  715.1 2.1 add_convert_fusion
  717.3 1.3 copy.68
  718.6 0.6 gather_fusion.2
  719.2 40.3 %all-gather.2 = bf16[32,4,720]{2,1,0:T(4,128)(2,1)S(1)} all-gather(bf16[1,4,720]{2,1,0:T(4,128)(2,1)S(1)} %select_bitcast_fusion), channel_id=1, replica_groups=mesh['dp'=4,'expert'=8] {'dp','expert'}, dimensions={0}, use_global_device_ids=true | all-gather | bytes 190080 | tf_op jit(solution)/shard_map/all_gather | solution.py:200
  759.6 0.2 multiply_reduce_fusion.1
  759.8 1.0 copy.83
  760.8 1.2 reshape.426
  762.1 4.4 fusion.36
  (69 shorter events, 1.9 us)
Async XLA Ops:
  7.2 76.5 %copy-start = (bf16[512,2880]{0,1:T(8,128)(2,1)S(1)}, bf16[512,2880]{0,1:T(8,128)(2,1)}, u32[]{:S(2)}) copy-start(bf16[512,2880]{0,1:T(8,128)(2,1)} %param.27) | copy-start | bytes 8847364
  7.2 53.2 %all-gather.6.cloned.1.call-start = ((), (), s32[]{:S(2)}) async-start(), calls=%async_computation.4 | async-start | bytes 2764800 | tf_op jit(solution)/shard_map/all_gather | solution.py:103
  7.9 108.9 %all-reduce.3.cloned.1.call-start = ((), (), s32[]{:S(2)}) async-start(), calls=%async_computation.6 | async-start | bytes 196608 | tf_op jit(solution)/shard_map/psum | solution.py:138
  8.8 59.8 %copy-start.6 = (s32[384]{0:T(512)}, s32[384]{0:T(512)S(1)}, u32[]{:S(2)}) copy-start(s32[384]{0:T(512)S(1)} %reduce.7) | copy-start | bytes 4612
  62.6 6.0 copy-start.11
  62.6 6.0 copy-start.12
  79.6 3.0 copy-start.5
  81.9 0.8 copy-start.4
  83.6 81.3 %copy-start.3 = (bf16[384,720]{0,1:T(8,128)(2,1)S(1)}, bf16[384,720]{0,1:T(8,128)(2,1)}, u32[]{:S(2)}) copy-start(bf16[384,720]{0,1:T(8,128)(2,1)} %param.19) | copy-start | bytes 1658884
  83.6 81.3 %reduce-scatter.3.cloned.1.call-start = ((), (), s32[]{:S(2)}) async-start(), calls=%async_computation.5 | async-start | bytes 2764800 | tf_op jit(solution)/shard_map/reduce_scatter | solution.py:135
  87.8 79.6 %copy-start.9 = (s32[1,96,4]{1,2,0:T(4,128)S(1)}, s32[1,96,4]{1,2,0:T(4,128)}, u32[]{:S(2)}) copy-start(s32[1,96,4]{1,2,0:T(4,128)} %param.22) | copy-start | bytes 4612
  87.8 129.9 %copy-start.8 = (f32[2880]{0:T(1024)S(1)}, f32[2880]{0:T(1024)}, u32[]{:S(2)}) copy-start(f32[2880]{0:T(1024)} %param.32) | copy-start | bytes 34564
  87.8 127.7 %all-gather.8.cloned.1.call-start = ((), (), s32[]{:S(2)}) async-start(), calls=%async_computation.7 | async-start | bytes 2764800 | tf_op jit(solution)/shard_map/all_gather | solution.py:149
  460.3 5.7 copy-start.10
  460.3 136.1 %all-to-all-start.1 = ((bf16[8,256,2880]{1,2,0:T(8,128)(2,1)}), bf16[8,256,2880]{1,2,0:T(8,128)(2,1)}, u32[]{:S(2)}, u32[]{:S(2)}) async-start(bf16[8,256,2880]{1,2,0:T(8,128)(2,1)} %bitcast.124), calls=%async_computation.2 | async-start | bytes 23592960 | tf_op jit(solution)/shard_map/all_to_all | solution.py:182
  465.8 249.3 %reduce-scatter.5.cloned.1.call-start = ((), (), s32[]{:S(2)}) async-start(), calls=%async_computation.8 | async-start | bytes 2764800 | tf_op jit(solution)/shard_map/reduce_scatter | solution.py:189
  669.3 2.6 copy-start.7
  669.3 45.8 %copy-start.2 = (bf16[384,720]{0,1:T(8,128)(2,1)S(1)}, bf16[384,720]{0,1:T(8,128)(2,1)}, u32[]{:S(2)}) copy-start(bf16[384,720]{0,1:T(8,128)(2,1)} %fusion.22) | copy-start | bytes 1658884
  715.1 51.4 %copy-start.1 = (bf16[512,2880]{0,1:T(8,128)(2,1)S(1)}, bf16[512,2880]{0,1:T(8,128)(2,1)}, u32[]{:S(2)}) copy-start(bf16[512,2880]{0,1:T(8,128)(2,1)} %param.27) | copy-start | bytes 8847364
Sparse Core Ops, SparseCore 0:
  9.6 50.7 all-gather.5
  83.7 33.0 all-reduce.2
  119.3 45.5 reduce-scatter.2
  167.5 47.9 all-gather.7
  672.0 43.0 reduce-scatter.4

commit v2 on v1

--- a/solution.py
+++ b/solution.py
@@ -152,8 +152,12 @@
     experts = expert_gate_weight.shape[0] * columns
     capacity = 4 * share * TOP // (3 * experts)
     col_capacity = groups * capacity
-    route_col = lax.all_gather(routes[0], "dp", axis=0, tiled=True)
-    gates_col = lax.all_gather(expert_gates[0], "dp", axis=0, tiled=True)
+    route_pack = jnp.concatenate(
+        [routes[0].astype(jnp.bfloat16), expert_gates[0].astype(jnp.bfloat16)], axis=1
+    )
+    pack_col = lax.all_gather(route_pack, "dp", axis=0, tiled=True)
+    route_col = pack_col[:, :TOP].astype(jnp.int32)
+    gates_col = pack_col[:, TOP:]
     route_flat = route_col.reshape(-1)
     one_hot = (route_flat[:, None] == jnp.arange(experts, dtype=jnp.int32)[None, :]).astype(
         jnp.int32
@@ -162,8 +166,14 @@
     target = route_flat * col_capacity + slot_rows
     source_rows = jnp.arange(route_flat.shape[0], dtype=jnp.int32) // TOP
     table = jnp.full((experts * col_capacity,), col_tokens, jnp.int32).at[target].set(source_rows)
-    padded = jnp.concatenate([moe_in, jnp.zeros((1, width), jnp.bfloat16)], axis=0)
-    outgoing = jnp.take(padded, table, axis=0).reshape(experts, col_capacity, width)
+    dispatch = (table[:, None] == jnp.arange(col_tokens, dtype=jnp.int32)[None, :]).astype(
+        jnp.bfloat16
+    )
+    outgoing = (
+        jnp.dot(dispatch, moe_in, preferred_element_type=jnp.float32)
+        .astype(jnp.bfloat16)
+        .reshape(experts, col_capacity, width)
+    )
     gate_weight = expert_gate_weight[0]
     up_weight = expert_up_weight[0]
     down_weight = expert_down_weight[0]
@@ -180,11 +190,17 @@
         .reshape(experts, col_capacity, width)
     )
     answers = lax.all_to_all(shares_out, "expert", split_axis=0, concat_axis=0, tiled=True)
-    picked_out = jnp.take(answers.reshape(experts * col_capacity, width), target, axis=0).reshape(
-        col_tokens, TOP, width
-    )
-    mixture = jnp.einsum(
-        "tk,tkd->td", gates_col, picked_out, preferred_element_type=jnp.float32
+    slot_ids = jnp.arange(experts * col_capacity, dtype=jnp.int32)
+    combine = jnp.sum(
+        jnp.where(
+            target.reshape(col_tokens, TOP)[:, :, None] == slot_ids[None, None, :],
+            gates_col[:, :, None],
+            jnp.zeros((), jnp.bfloat16),
+        ),
+        axis=1,
+    ).astype(jnp.bfloat16)
+    mixture = jnp.dot(
+        combine, answers.reshape(experts * col_capacity, width), preferred_element_type=jnp.float32
     )
     moe_part = lax.psum_scatter(
         mixture.astype(jnp.bfloat16), "dp", scatter_dimension=1, tiled=True
@@ -197,13 +213,8 @@
         jnp.where(segment_row[None, :] == request_ids[:, None], counter[None, :], -1), axis=1
     )
     chosen = jnp.take(hidden_out, jnp.clip(last_index, 0, col_tokens - 1), axis=0)
-    spread_rows = lax.all_gather(chosen, ("dp", "expert"), axis=0, tiled=True)
-    quarter = chosen.shape[1]
-    tail_full = (
-        spread_rows.reshape(groups, columns * REQS, quarter)
-        .transpose(1, 0, 2)
-        .reshape(columns * REQS, groups * quarter)
-    )
+    row_full = lax.all_gather(chosen, "dp", axis=1, tiled=True)
+    tail_full = lax.all_gather(row_full, "expert", axis=0, tiled=True)
     tail_rows = rms_scale(tail_full.astype(jnp.float32), closing_gain).astype(jnp.bfloat16)
     logits = jnp.dot(tail_rows, vocabulary_weight, preferred_element_type=jnp.float32)
     return (hidden_out, logits)

time: 775 us -> 675 us (0.87)
  local copies, waits for them, and re-layouts: 131 us -> 59.9 us
  blocking collectives: 203 us -> 169 us
  other arithmetic: 43.1 us -> 15.3 us
  matrix products: 67.9 us -> 87.3 us
  waiting for transfers between devices: 309 us -> 322 us
    gather x4 -> x0, local copies, waits for them, and re-layouts: 63 us -> none  [the longest x2 35.8 us: shards(): jnp.take(answers.reshape(experts * col_capacity, width), target, axis=0)]
    all_gather x3, blocking collectives: 68.7 us -> 34.5 us  [the longest x1 13.1 us: shards(): row_full = lax.all_gather(chosen, 'dp', axis=1, tiled=True)]
    unnamed x5 -> x4, other arithmetic: 21.9 us -> 0.97 us
    dot_general x0 -> x2, matrix products: none -> 19.4 us  [the longest x1 11 us: shards(): jnp.dot(combine, answers.reshape(experts * col_capacity, width), preferre...]
    all_to_all x1, waiting for transfers between devices: 116 us -> 128 us  [shards(): lax.all_to_all(shares_out, 'expert', split_axis=0, concat_axis=0, tiled=T...]
  transfers between devices with their start and end apart: 6 -> 6, of which waited for: 6 -> 6; matrix products, arithmetic and copies ran while one was open for 2% -> 3% of each run, Pallas kernels for 0% -> 0%
where the time goes in v2:
time: 675 us; the launch traced here: 673 us
  waiting for transfers between devices  322 us (48%)
  blocking collectives  169 us (25%)
  matrix products  87.3 us (13%)
  local copies, waits for them, and re-layouts  59.9 us (9%)
  other arithmetic  15.3 us (2%)
  between operations  14.1 us (2%)
    all_to_all x1, blocking collectives, shards(): lax.all_to_all(outgoing, 'expert', split_axis=0, concat_axis=0, tiled=True)  134 us
    all_to_all x1, waiting for transfers between devices, shards(): lax.all_to_all(shares_out, 'expert', split_axis=0, concat_axis=0, tiled=T...  128 us
    all_gather x1, waiting for transfers between devices, shards(): gathered_rows = lax.all_gather(hidden, 'dp', axis=1, tiled=True)  48.3 us
    reduce_scatter x1, waiting for transfers between devices, shards(): lax.psum_scatter(partial_out.astype(jnp.bfloat16), 'dp', scatter_dimensio...  48 us
    reduce_scatter x1, waiting for transfers between devices, shards(): lax.psum_scatter(mixture.astype(jnp.bfloat16), 'dp', scatter_dimension=1,...  42.9 us
    psum x1, waiting for transfers between devices, shards(): lax.psum(jnp.dot(blended_hidden, output_down_maps, preferred_element_type...  29 us
    dot_general x1, matrix products, shards(): jnp.dot(activated, down_weight, preferred_element_type=jnp.float32)  26.6 us
    all_gather x1, waiting for transfers between devices, shards(): column_full = lax.all_gather(resid, 'dp', axis=1, tiled=True)  25.2 us
  transfers between devices with their start and end apart: 6, of which 6 were waited for; matrix products, arithmetic and copies ran while one was open for 3% of the time, Pallas kernels for 0%

profile of v2, /device:TPU:0, one launch (start us, length us, event | category | flops | bytes accessed | tf_op | source)
XLA Modules:
  0.0 673.3 jit_solution(4813058274132309141)
XLA Ops:
  7.2 0.7 all-gather.6.cloned.1.call-update
  8.0 0.8 reduce.2
  8.8 0.8 compare_reduce_fusion
  9.7 0.3 reduce-window.15
  10.1 0.7 exp.18
  10.8 0.1 slice_reduce_fusion.1
  10.9 0.7 select_reduce_fusion.1
  11.7 0.3 multiply_cosine_fusion
  12.0 0.1 fusion.36
  12.1 48.3 %all-gather.6.cloned.1.call-done = bf16[384,2880]{0,1:T(8,128)(2,1)} async-done(((bf16[384,720]{0,1:T(8,128)(2,1)}), bf16[384,2880]{0,1:T(8,128)(2,1)}) %all-gather.6.cloned.1.call-update) | async-done | bytes 2211856 | tf_op jit(solution)/shard_map/all_gather | solution.py:103
  60.4 2.2 fusion.2
  62.6 5.9 fusion.16
  68.5 4.8 fusion.27
  73.3 2.5 copy.65
  75.8 1.2 slice_bitcast_fusion
  77.0 0.9 slice_bitcast_fusion.1
  77.9 0.3 fusion.69
  78.1 0.1 subtract_convert_fusion
  78.3 1.3 fusion.15
  79.6 2.2 fusion.29
  81.9 0.7 copy-done.4
  82.6 1.0 convolution_convert_fusion.4
  83.7 4.1 convolution_convert_fusion.2
  87.9 29.0 %all-reduce.2.cloned.1.call-done = bf16[384,128]{1,0:T(8,128)(2,1)} async-done(((bf16[384,128]{1,0:T(8,128)(2,1)}), bf16[384,128]{1,0:T(8,128)(2,1)}) %all-reduce.2.cloned.1.call-update) | async-done | bytes 98320 | tf_op jit(solution)/shard_map/psum | solution.py:138
  116.8 48.0 %reduce-scatter.3.cloned.1.call-done = bf16[384,720]{0,1:T(8,128)(2,1)} async-done(((bf16[384,2880]{0,1:T(8,128)(2,1)}), bf16[384,720]{0,1:T(8,128)(2,1)}) %reduce-scatter.3.cloned.1.call-update) | async-done | bytes 552976 | tf_op jit(solution)/shard_map/reduce_scatter | solution.py:135
  164.9 2.4 fusion.28
  167.4 12.2 %all-gather = bf16[4,96,8]{1,2,0:T(8,128)(2,1)S(1)} all-gather(bf16[1,96,8]{1,2,0:T(8,128)(2,1)S(1)} %maximum_bitcast_fusion.2), channel_id=1, replica_groups=mesh['dp'=4,'expert'=8] {'dp'}, dimensions={0}, use_global_device_ids=true | all-gather | bytes 7680 | tf_op jit(solution)/shard_map/all_gather | solution.py:158
  179.6 0.1 reshape.418
  179.7 0.1 copy.68
  179.8 0.1 eq.123
  180.0 0.1 eq.119
  180.1 2.3 reduce-window.19
  182.4 0.3 slice_reduce_fusion
  182.7 0.2 reduce-window.24
  182.9 0.1 add_bitcast_fusion
  183.0 0.2 reduce_sum.74
  183.3 0.2 copy.71
  183.5 0.2 mul.222
  183.7 6.2 scatter_custom_fusion
  189.9 25.2 %all-gather.8.cloned.1.call-done = bf16[384,2880]{0,1:T(8,128)(2,1)} async-done(((bf16[384,720]{0,1:T(8,128)(2,1)}), bf16[384,2880]{0,1:T(8,128)(2,1)}) %all-gather.8.cloned.1.call-update) | async-done | bytes 2211856 | tf_op jit(solution)/shard_map/all_gather | solution.py:149
  215.1 2.2 fusion.5
  217.3 8.5 %convolution_convert_fusion.1 = bf16[2048,2880]{0,1:T(8,128)(2,1)S(1)} fusion(bf16[384,2880]{0,1:T(8,128)(2,1)} %all-gather.8.cloned.1.call-done, f32[2880]{0:T(1024)S(1)} %copy-done.10, f32[384]{0:T(512)S(1)} %add_rsqrt_fusion, s32[2048]{0:T(1024)S(1)} %scatter_custom_fusion), kind=kOutput, calls=%fused_computation.7 | convolution fusion | flops 4540956672 | bytes 14029568 | tf_op jit(solution)/shard_map/dot_general | solution.py:173
  225.7 1.4 copy.86
  227.2 134.2 %all_to_all.10 = bf16[8,256,2880]{1,2,0:T(8,128)(2,1)} all-to-all(bf16[8,256,2880]{1,2,0:T(8,128)(2,1)S(1)} %bitcast.131), channel_id=1, replica_groups=mesh['dp'=4,'expert'=8] {'expert'}, dimensions={0} | all-to-all | bytes 23592960 | tf_op jit(solution)/shard_map/all_to_all | solution.py:180
  361.4 16.3 %copy.73 = bf16[8,256,2880]{2,1,0:T(8,128)(2,1)} copy(bf16[8,256,2880]{1,2,0:T(8,128)(2,1)} %all_to_all.10) | data formatting | bytes 23592960 | tf_op jit(solution)/shard_map/all_to_all | solution.py:180
  377.6 15.1 %fusion.9 = f32[2048,720]{0,1:T(8,128)} fusion(bf16[2048,2880]{1,0:T(8,128)(2,1)} %bitcast.132, bf16[1,2880,720]{1,2,0:T(8,128)(2,1)} %param.34), kind=kOutput, calls=%fused_computation.23 | convolution fusion | flops 8493465600 | bytes 21841920 | tf_op jit(solution)/shard_map/dot_general | solution.py:183
  392.7 26.6 %convolution_convert_fusion = bf16[2048,2880]{0,1:T(8,128)(2,1)} fusion(bf16[1,720,2880]{2,1,0:T(8,128)(2,1)} %param.35, f32[2048,720]{0,1:T(8,128)} %fusion.9, bf16[2048,2880]{1,0:T(8,128)(2,1)} %bitcast.133, bf16[1,2880,720]{1,2,0:T(8,128)(2,1)} %param.33), kind=kOutput, calls=%fused_computation.6 | convolution fusion | flops 17004625920 | bytes 37785600 | tf_op jit(solution)/shard_map/dot_general | solution.py:188
  419.4 10.1 %copy.85 = bf16[360,8,8,256]{3,2,0,1:T(8,128)(2,1)} copy(bf16[360,8,8,256]{3,2,1,0:T(8,128)(2,1)} %bitcast.136) | data formatting | bytes 23592960 | tf_op jit(solution)/shard_map/reshape | solution.py:190
  429.5 5.3 all-to-all-start.1
  434.8 0.3 reduce-scatter.5.cloned.1.call-start
  435.1 2.2 fusion.1
  437.4 128.0 %all-to-all-done.1 = bf16[8,256,2880]{1,2,0:T(8,128)(2,1)} async-done(((bf16[8,256,2880]{1,2,0:T(8,128)(2,1)}), bf16[8,256,2880]{1,2,0:T(8,128)(2,1)}, u32[]{:S(2)}, u32[]{:S(2)}) %all-to-all-start.1) | async-done | bytes 11796512 | tf_op jit(solution)/shard_map/all_to_all | solution.py:192
  565.4 16.3 %copy.75 = bf16[8,256,2880]{2,1,0:T(8,128)(2,1)} copy(bf16[8,256,2880]{1,2,0:T(8,128)(2,1)} %all-to-all-done.1) | data formatting | bytes 23592960 | tf_op jit(solution)/shard_map/all_to_all | solution.py:192
  581.7 11.0 %convolution_convert_fusion.3 = bf16[384,2880]{0,1:T(8,128)(2,1)} fusion(bf16[384,2048]{1,0:T(8,128)(2,1)S(1)} %fusion.1, bf16[2048,2880]{1,0:T(8,128)(2,1)} %bitcast.134), kind=kOutput, calls=%fused_computation.28 | convolution fusion | flops 4530954240 | bytes 15581184 | tf_op jit(solution)/shard_map/dot_general | solution.py:202
  592.7 0.1 select_reduce_fusion
  592.8 42.9 %reduce-scatter.5.cloned.1.call-done = bf16[384,720]{0,1:T(8,128)(2,1)} async-done(((bf16[384,2880]{0,1:T(8,128)(2,1)}), bf16[384,720]{0,1:T(8,128)(2,1)}) %reduce-scatter.5.cloned.1.call-update) | async-done | bytes 552976 | tf_op jit(solution)/shard_map/reduce_scatter | solution.py:205
  635.7 2.0 add_convert_fusion
  637.7 1.3 copy.76
  639.0 0.6 gather_fusion
  639.6 13.1 %all-gather.1 = bf16[4,720,4]{1,2,0:T(4,128)(2,1)S(1)} all-gather(bf16[1,720,4]{1,2,0:T(4,128)(2,1)S(1)} %select_bitcast_fusion), channel_id=1, replica_groups=mesh['dp'=4,'expert'=8] {'dp'}, dimensions={0}, use_global_device_ids=true | all-gather | bytes 28800 | tf_op jit(solution)/shard_map/all_gather | solution.py:216
  652.8 0.1 reshape.420
  652.9 9.2 %all-gather.2 = bf16[8,4,2880]{2,1,0:T(4,128)(2,1)S(1)} all-gather(bf16[1,4,2880]{2,1,0:T(4,128)(2,1)S(1)} %bitcast.142), channel_id=1, replica_groups=mesh['dp'=4,'expert'=8] {'expert'}, dimensions={0}, use_global_device_ids=true | all-gather | bytes 207360 | tf_op jit(solution)/shard_map/all_gather | solution.py:217
  662.2 0.1 multiply_reduce_fusion
  662.3 4.4 fusion.42
  (55 shorter events, 1.0 us)
Async XLA Ops:
  7.2 76.5 %copy-start = (bf16[512,2880]{0,1:T(8,128)(2,1)S(1)}, bf16[512,2880]{0,1:T(8,128)(2,1)}, u32[]{:S(2)}) copy-start(bf16[512,2880]{0,1:T(8,128)(2,1)} %param.27) | copy-start | bytes 8847364
  7.2 53.2 %all-gather.6.cloned.1.call-start = ((), (), s32[]{:S(2)}) async-start(), calls=%async_computation.4 | async-start | bytes 2764800 | tf_op jit(solution)/shard_map/all_gather | solution.py:103
  7.9 108.9 %all-reduce.2.cloned.1.call-start = ((), (), s32[]{:S(2)}) async-start(), calls=%async_computation.6 | async-start | bytes 196608 | tf_op jit(solution)/shard_map/psum | solution.py:138
  62.6 6.0 copy-start.8
  62.6 6.0 copy-start.9
  79.6 3.0 copy-start.5
  81.9 0.8 copy-start.4
  83.6 81.3 %copy-start.3 = (bf16[384,720]{0,1:T(8,128)(2,1)S(1)}, bf16[384,720]{0,1:T(8,128)(2,1)}, u32[]{:S(2)}) copy-start(bf16[384,720]{0,1:T(8,128)(2,1)} %param.19) | copy-start | bytes 1658884
  83.6 81.3 %reduce-scatter.3.cloned.1.call-start = ((), (), s32[]{:S(2)}) async-start(), calls=%async_computation.5 | async-start | bytes 2764800 | tf_op jit(solution)/shard_map/reduce_scatter | solution.py:135
  87.8 79.6 %copy-start.6 = (s32[1,96,4]{1,2,0:T(4,128)S(1)}, s32[1,96,4]{1,2,0:T(4,128)}, u32[]{:S(2)}) copy-start(s32[1,96,4]{1,2,0:T(4,128)} %param.22) | copy-start | bytes 4612
  87.8 79.6 %copy-start.7 = (bf16[1,96,4]{1,2,0:T(4,128)(2,1)S(1)}, bf16[1,96,4]{1,2,0:T(4,128)(2,1)}, u32[]{:S(2)}) copy-start(bf16[1,96,4]{1,2,0:T(4,128)(2,1)} %param.23) | copy-start | bytes 2308
  87.8 129.5 %copy-start.10 = (f32[2880]{0:T(1024)S(1)}, f32[2880]{0:T(1024)}, u32[]{:S(2)}) copy-start(f32[2880]{0:T(1024)} %param.32) | copy-start | bytes 34564
  87.8 127.2 %all-gather.8.cloned.1.call-start = ((), (), s32[]{:S(2)}) async-start(), calls=%async_computation.7 | async-start | bytes 2764800 | tf_op jit(solution)/shard_map/all_gather | solution.py:149
  429.5 135.9 %all-to-all-start.1 = ((bf16[8,256,2880]{1,2,0:T(8,128)(2,1)}), bf16[8,256,2880]{1,2,0:T(8,128)(2,1)}, u32[]{:S(2)}, u32[]{:S(2)}) async-start(bf16[8,256,2880]{1,2,0:T(8,128)(2,1)} %bitcast.130), calls=%async_computation.2 | async-start | bytes 23592960 | tf_op jit(solution)/shard_map/all_to_all | solution.py:192
  434.8 200.9 %reduce-scatter.5.cloned.1.call-start = ((), (), s32[]{:S(2)}) async-start(), calls=%async_computation.8 | async-start | bytes 2764800 | tf_op jit(solution)/shard_map/reduce_scatter | solution.py:205
  581.7 54.0 %copy-start.2 = (bf16[384,720]{0,1:T(8,128)(2,1)S(1)}, bf16[384,720]{0,1:T(8,128)(2,1)}, u32[]{:S(2)}) copy-start(bf16[384,720]{0,1:T(8,128)(2,1)} %fusion.28) | copy-start | bytes 1658884
  592.8 73.9 %copy-start.1 = (bf16[512,2880]{0,1:T(8,128)(2,1)S(1)}, bf16[512,2880]{0,1:T(8,128)(2,1)}, u32[]{:S(2)}) copy-start(bf16[512,2880]{0,1:T(8,128)(2,1)} %param.27) | copy-start | bytes 8847364
Sparse Core Ops, SparseCore 0:
  9.6 50.7 all-gather.5
  83.7 33.0 all-reduce.1
  119.3 45.5 reduce-scatter.2
  167.5 47.5 all-gather.7
  592.8 42.8 reduce-scatter.4

commit v3 on v2

--- a/solution.py
+++ b/solution.py
@@ -131,23 +131,23 @@
     key_heads = rotate_heads(joined_projection[:, :, QUERY_GROUP], positions).astype(jnp.bfloat16)
     value_heads = joined_projection[:, :, QUERY_GROUP + 1].astype(jnp.bfloat16)
     blended_hidden = attend_heads(queries, key_heads, value_heads, segment_row, sinks)
-    partial_out = jnp.dot(blended_hidden, attention_out_weight, preferred_element_type=jnp.float32)
+    up_full = lax.all_gather(output_up_maps, "dp", axis=1, tiled=True)
+    low_local = jnp.dot(blended_hidden, output_down_maps, preferred_element_type=jnp.float32)
+    selected_output = jnp.where(adapter_mask, low_local, jnp.zeros_like(low_local))
+    partial_out = jnp.dot(
+        blended_hidden, attention_out_weight, preferred_element_type=jnp.float32
+    ) + adapter_scale * jnp.dot(
+        selected_output.astype(jnp.bfloat16), up_full, preferred_element_type=jnp.float32
+    )
     mine_out = lax.psum_scatter(
         partial_out.astype(jnp.bfloat16), "dp", scatter_dimension=1, tiled=True
     ).astype(jnp.float32)
-    output_reduced = lax.psum(
-        jnp.dot(blended_hidden, output_down_maps, preferred_element_type=jnp.float32).astype(
-            jnp.bfloat16
-        ),
-        "dp",
-    )
-    selected_output = jnp.where(adapter_mask, output_reduced, jnp.zeros_like(output_reduced))
-    adapter_delta = adapter_scale * jnp.dot(
-        selected_output, output_up_maps, preferred_element_type=jnp.float32
-    )
-    resid = (hidden.astype(jnp.float32) + mine_out + adapter_delta).astype(jnp.bfloat16)
+    resid = (hidden.astype(jnp.float32) + mine_out).astype(jnp.bfloat16)
     column_full = lax.all_gather(resid, "dp", axis=1, tiled=True)
     moe_in = rms_scale(column_full.astype(jnp.float32), expert_norm_gain).astype(jnp.bfloat16)
+    lane_pad = -width % 128
+    moe_in = jnp.pad(moe_in, ((0, 0), (0, lane_pad)))
+    wide = width + lane_pad
     share = col_tokens // groups
     experts = expert_gate_weight.shape[0] * columns
     capacity = 4 * share * TOP // (3 * experts)
@@ -172,13 +172,13 @@
     outgoing = (
         jnp.dot(dispatch, moe_in, preferred_element_type=jnp.float32)
         .astype(jnp.bfloat16)
-        .reshape(experts, col_capacity, width)
+        .reshape(experts, col_capacity, wide)
     )
     gate_weight = expert_gate_weight[0]
     up_weight = expert_up_weight[0]
-    down_weight = expert_down_weight[0]
+    down_weight = jnp.pad(expert_down_weight[0], ((0, 0), (0, lane_pad)))
     arrived = lax.all_to_all(outgoing, "expert", split_axis=0, concat_axis=0, tiled=True)
-    rows_in = arrived.reshape(-1, width)
+    rows_in = arrived.reshape(-1, wide)[:, :width]
     gate_part = jnp.dot(rows_in, gate_weight, preferred_element_type=jnp.float32)
     up_part = jnp.dot(rows_in, up_weight, preferred_element_type=jnp.float32)
     activated = (gate_part * jax.nn.sigmoid(glu_alpha * gate_part) * (up_part + 1.0)).astype(
@@ -187,7 +187,7 @@
     shares_out = (
         jnp.dot(activated, down_weight, preferred_element_type=jnp.float32)
         .astype(jnp.bfloat16)
-        .reshape(experts, col_capacity, width)
+        .reshape(experts, col_capacity, wide)
     )
     answers = lax.all_to_all(shares_out, "expert", split_axis=0, concat_axis=0, tiled=True)
     slot_ids = jnp.arange(experts * col_capacity, dtype=jnp.int32)
@@ -200,8 +200,8 @@
         axis=1,
     ).astype(jnp.bfloat16)
     mixture = jnp.dot(
-        combine, answers.reshape(experts * col_capacity, width), preferred_element_type=jnp.float32
-    )
+        combine, answers.reshape(experts * col_capacity, wide), preferred_element_type=jnp.float32
+    )[:, :width]
     moe_part = lax.psum_scatter(
         mixture.astype(jnp.bfloat16), "dp", scatter_dimension=1, tiled=True
     )

time: 675 us -> 617 us (0.914)
  waiting for transfers between devices: 322 us -> 271 us
  local copies, waits for them, and re-layouts: 59.9 us -> 17.5 us
  blocking collectives: 169 us -> 200 us
    all_to_all x2 -> x0, local copies, waits for them, and re-layouts: 32.5 us -> none  [the longest x1 16.3 us: shards(): lax.all_to_all(shares_out, 'expert', split_axis=0, concat_axis=0, tiled=T...]
    psum x1 -> x0, waiting for transfers between devices: 29 us -> none  [shards(): lax.psum(jnp.dot(blended_hidden, output_down_maps, preferred_element_type...]
    all_gather x0 -> x1, blocking collectives: none -> 28.3 us  [shards(): up_full = lax.all_gather(output_up_maps, 'dp', axis=1, tiled=True)]
    all_gather x1, waiting for transfers between devices: 48.3 us -> 27.3 us  [shards(): gathered_rows = lax.all_gather(hidden, 'dp', axis=1, tiled=True)]
    reshape x2 -> x0, local copies, waits for them, and re-layouts: 11.6 us -> none  [the longest x1 10.1 us: shards(): shares_out = jnp.dot(activated, down_weight, preferred_element_type=jnp.f...]
    dot_general x3 -> x2, matrix products: 14.4 us -> 14.5 us  [the longest x1 10.2 us: shards(): jnp.dot(combine, answers.reshape(experts * col_capacity, wide), preferred...]
  transfers between devices with their start and end apart: 6 -> 5, of which waited for: 6 -> 5; matrix products, arithmetic and copies ran while one was open for 3% -> 3% of each run, Pallas kernels for 0% -> 0%
where the time goes in v3:
time: 617 us; the launch traced here: 616 us
  waiting for transfers between devices  271 us (44%)
  blocking collectives  200 us (32%)
  matrix products  86.6 us (14%)
  other arithmetic  20.9 us (3%)
  local copies, waits for them, and re-layouts  17.5 us (3%)
  between operations  14.1 us (2%)
    all_to_all x1, blocking collectives, shards(): lax.all_to_all(outgoing, 'expert', split_axis=0, concat_axis=0, tiled=True)  137 us
    all_to_all x1, waiting for transfers between devices, shards(): lax.all_to_all(shares_out, 'expert', split_axis=0, concat_axis=0, tiled=T...  130 us
    reduce_scatter x1, waiting for transfers between devices, shards(): lax.psum_scatter(partial_out.astype(jnp.bfloat16), 'dp', scatter_dimensio...  45.5 us
    reduce_scatter x1, waiting for transfers between devices, shards(): lax.psum_scatter(mixture.astype(jnp.bfloat16), 'dp', scatter_dimension=1,...  42.9 us
    all_gather x1, blocking collectives, shards(): up_full = lax.all_gather(output_up_maps, 'dp', axis=1, tiled=True)  28.3 us
    all_gather x1, waiting for transfers between devices, shards(): gathered_rows = lax.all_gather(hidden, 'dp', axis=1, tiled=True)  27.3 us
    dot_general x1, matrix products, shards(): jnp.dot(activated, down_weight, preferred_element_type=jnp.float32)  27.2 us
    all_gather x1, waiting for transfers between devices, shards(): column_full = lax.all_gather(resid, 'dp', axis=1, tiled=True)  25.2 us
  transfers between devices with their start and end apart: 5, of which 5 were waited for; matrix products, arithmetic and copies ran while one was open for 3% of the time, Pallas kernels for 0%

profile of v3, /device:TPU:0, one launch (start us, length us, event | category | flops | bytes accessed | tf_op | source)
XLA Modules:
  0.0 615.8 jit_solution(3175171448357153518)
XLA Ops:
  7.2 0.7 all-gather.6.cloned.1.call-update
  8.0 0.8 reduce.2
  8.8 0.8 compare_reduce_fusion
  9.6 0.1 add_select_fusion.1
  9.7 0.3 reduce-window.15
  10.1 0.7 exp.18
  10.8 0.1 slice_reduce_fusion.1
  10.9 0.7 select_reduce_fusion.1
  11.7 0.3 multiply_cosine_fusion
  12.0 0.1 fusion.42
  12.1 28.3 %all_gather.19 = bf16[128,2880]{0,1:T(8,128)(2,1)} all-gather(bf16[128,720]{0,1:T(8,128)(2,1)} %param.31), channel_id=1, replica_groups=mesh['dp'=4,'expert'=8] {'dp'}, dimensions={1}, use_global_device_ids=true | all-gather | bytes 921600 | tf_op jit(solution)/shard_map/all_gather | solution.py:134
  40.4 27.3 %all-gather.6.cloned.1.call-done = bf16[384,2880]{0,1:T(8,128)(2,1)} async-done(((bf16[384,720]{0,1:T(8,128)(2,1)}), bf16[384,2880]{0,1:T(8,128)(2,1)}) %all-gather.6.cloned.1.call-update) | async-done | bytes 2211856 | tf_op jit(solution)/shard_map/all_gather | solution.py:103
  67.7 2.2 fusion.6
  69.9 5.9 fusion.21
  75.9 4.8 fusion.33
  80.6 2.5 copy.48
  83.1 1.2 slice_bitcast_fusion
  84.3 0.9 slice_bitcast_fusion.1
  85.2 0.3 fusion.76
  85.5 0.1 subtract_convert_fusion
  85.6 1.3 fusion.16
  87.0 2.2 fusion.34
  89.2 0.7 copy-done.4
  89.9 4.3 convolution_multiply_fusion
  94.3 5.5 fusion.15
  99.9 45.5 %reduce-scatter.3.cloned.1.call-done = bf16[384,720]{0,1:T(8,128)(2,1)} async-done(((bf16[384,2880]{0,1:T(8,128)(2,1)}), bf16[384,720]{0,1:T(8,128)(2,1)}) %reduce-scatter.3.cloned.1.call-update) | async-done | bytes 552976 | tf_op jit(solution)/shard_map/reduce_scatter | solution.py:142
  145.4 2.0 add_convert_fusion.1
  147.5 12.2 %all-gather = bf16[4,96,8]{1,2,0:T(8,128)(2,1)S(1)} all-gather(bf16[1,96,8]{1,2,0:T(8,128)(2,1)S(1)} %maximum_bitcast_fusion.2), channel_id=1, replica_groups=mesh['dp'=4,'expert'=8] {'dp'}, dimensions={0}, use_global_device_ids=true | all-gather | bytes 7680 | tf_op jit(solution)/shard_map/all_gather | solution.py:158
  159.6 0.1 reshape.418
  159.7 0.1 copy.51
  159.9 0.1 eq.123
  160.0 0.1 eq.119
  160.2 2.3 reduce-window.19
  162.5 0.3 slice_reduce_fusion
  162.8 0.2 reduce-window.24
  162.9 0.1 add_bitcast_fusion
  163.1 0.2 reduce_sum.74
  163.3 0.1 copy.53
  163.4 0.2 copy.54
  163.6 0.2 mul.222
  163.8 6.2 %scatter_custom_fusion = s32[2048]{0:T(1024)S(1)} fusion(s32[1536]{0:T(1024)S(1)} %fusion.80, s32[1536]{0:T(1024)S(1)} %add_select_fusion, s32[]{:T(128)} %constant.94.clone.1), kind=kCustom, calls=%fused_computation.119 | custom fusion | bytes 8196 | tf_op jit(solution)/shard_map/scatter | solution.py:168
  169.9 25.2 %all-gather.8.cloned.1.call-done = bf16[384,2880]{0,1:T(8,128)(2,1)} async-done(((bf16[384,720]{0,1:T(8,128)(2,1)}), bf16[384,2880]{0,1:T(8,128)(2,1)}) %all-gather.8.cloned.1.call-update) | async-done | bytes 2211856 | tf_op jit(solution)/shard_map/all_gather | solution.py:146
  195.1 2.2 fusion.9
  197.3 2.3 fusion.11
  199.7 6.8 %convolution_convert_fusion.1 = bf16[2048,2944]{1,0:T(8,128)(2,1)S(1)} fusion(bf16[384,2880]{0,1:T(8,128)(2,1)S(1)} %fusion.11, s32[2048]{0:T(1024)S(1)} %scatter_custom_fusion), kind=kOutput, calls=%fused_computation.5 | convolution fusion | flops 4637327360 | bytes 14278656 | tf_op jit(solution)/shard_map/dot_general | solution.py:173
  206.5 137.0 %all_to_all.10 = bf16[8,256,2944]{2,1,0:T(8,128)(2,1)} all-to-all(bf16[8,256,2944]{2,1,0:T(8,128)(2,1)S(1)} %bitcast.121), channel_id=1, replica_groups=mesh['dp'=4,'expert'=8] {'expert'}, dimensions={0} | all-to-all | bytes 24117248 | tf_op jit(solution)/shard_map/all_to_all | solution.py:180
  343.5 13.8 %fusion.1 = f32[2048,720]{0,1:T(8,128)} fusion(bf16[2048,2944]{1,0:T(8,128)(2,1)} %bitcast.122, bf16[1,2880,720]{1,2,0:T(8,128)(2,1)S(1)} %bitcast.134), kind=kOutput, calls=%fused_computation.6 | convolution fusion | flops 8493465600 | bytes 22104064 | tf_op jit(solution)/shard_map/dot_general | solution.py:183
  357.4 27.2 %convolution_convert_fusion = bf16[2048,2944]{1,0:T(8,128)(2,1)} fusion(bf16[720,2880]{1,0:T(8,128)(2,1)} %bitcast.135, f32[2048,720]{0,1:T(8,128)} %fusion.1, bf16[1,2880,720]{1,2,0:T(8,128)(2,1)} %param.33, bf16[2048,2944]{1,0:T(8,128)(2,1)} %bitcast.123), kind=kOutput, calls=%fused_computation.4 | convolution fusion | flops 17193500672 | bytes 38309888 | tf_op jit(solution)/shard_map/dot_general | solution.py:188
  384.6 5.4 all-to-all-start.1
  389.9 0.3 reduce-scatter.5.cloned.1.call-start
  390.2 3.5 fusion.5
  393.7 129.6 %all-to-all-done.1 = bf16[8,256,2944]{2,1,0:T(8,128)(2,1)} async-done(((bf16[8,256,2944]{2,1,0:T(8,128)(2,1)}), bf16[8,256,2944]{2,1,0:T(8,128)(2,1)}, u32[]{:S(2)}, u32[]{:S(2)}) %all-to-all-start.1) | async-done | bytes 12058656 | tf_op jit(solution)/shard_map/all_to_all | solution.py:192
  523.3 10.2 %fusion.96 = bf16[384,2944]{0,1:T(8,128)(2,1)S(1)} fusion(bf16[384,2048]{1,0:T(8,128)(2,1)} %fusion.5, bf16[2048,2944]{1,0:T(8,128)(2,1)} %bitcast.31), kind=kOutput, calls=%fused_computation.153 | convolution fusion | flops 4630511616 | bytes 15892480 | tf_op jit(solution)/shard_map/dot_general | solution.py:202
  533.5 1.6 slice.127
  535.2 0.1 select_reduce_fusion
  535.3 42.9 %reduce-scatter.5.cloned.1.call-done = bf16[384,720]{0,1:T(8,128)(2,1)} async-done(((bf16[384,2880]{0,1:T(8,128)(2,1)}), bf16[384,720]{0,1:T(8,128)(2,1)}) %reduce-scatter.5.cloned.1.call-update) | async-done | bytes 552976 | tf_op jit(solution)/shard_map/reduce_scatter | solution.py:205
  578.2 2.0 add_convert_fusion
  580.2 1.3 copy.55
  581.5 0.6 gather_fusion
  582.1 13.1 %all-gather.1 = bf16[4,720,4]{1,2,0:T(4,128)(2,1)S(1)} all-gather(bf16[1,720,4]{1,2,0:T(4,128)(2,1)S(1)} %select_bitcast_fusion), channel_id=1, replica_groups=mesh['dp'=4,'expert'=8] {'dp'}, dimensions={0}, use_global_device_ids=true | all-gather | bytes 28800 | tf_op jit(solution)/shard_map/all_gather | solution.py:216
  595.3 0.1 reshape.420
  595.4 9.2 %all-gather.2 = bf16[8,4,2880]{2,1,0:T(4,128)(2,1)S(1)} all-gather(bf16[1,4,2880]{2,1,0:T(4,128)(2,1)S(1)} %bitcast.129), channel_id=1, replica_groups=mesh['dp'=4,'expert'=8] {'expert'}, dimensions={0}, use_global_device_ids=true | all-gather | bytes 207360 | tf_op jit(solution)/shard_map/all_gather | solution.py:217
  604.7 0.1 multiply_reduce_fusion
  604.8 4.4 fusion.49
  (54 shorter events, 0.8 us)
Async XLA Ops:
  7.2 87.1 %copy-start = (bf16[512,2880]{0,1:T(8,128)(2,1)S(1)}, bf16[512,2880]{0,1:T(8,128)(2,1)}, u32[]{:S(2)}) copy-start(bf16[512,2880]{0,1:T(8,128)(2,1)} %param.27) | copy-start | bytes 8847364
  7.2 60.5 %all-gather.6.cloned.1.call-start = ((), (), s32[]{:S(2)}) async-start(), calls=%async_computation.4 | async-start | bytes 2764800 | tf_op jit(solution)/shard_map/all_gather | solution.py:103
  7.9 137.5 %reduce-scatter.3.cloned.1.call-start = ((), (), s32[]{:S(2)}) async-start(), calls=%async_computation.5 | async-start | bytes 2764800 | tf_op jit(solution)/shard_map/reduce_scatter | solution.py:142
  69.9 6.0 copy-start.8
  69.9 6.0 copy-start.9
  89.2 0.8 copy-start.4
  94.3 51.1 %copy-start.3 = (bf16[384,720]{0,1:T(8,128)(2,1)S(1)}, bf16[384,720]{0,1:T(8,128)(2,1)}, u32[]{:S(2)}) copy-start(bf16[384,720]{0,1:T(8,128)(2,1)} %param.19) | copy-start | bytes 1658884
  99.8 47.6 %copy-start.6 = (s32[1,96,4]{1,2,0:T(4,128)S(1)}, s32[1,96,4]{1,2,0:T(4,128)}, u32[]{:S(2)}) copy-start(s32[1,96,4]{1,2,0:T(4,128)} %param.22) | copy-start | bytes 4612
  99.8 47.6 %copy-start.7 = (bf16[1,96,4]{1,2,0:T(4,128)(2,1)S(1)}, bf16[1,96,4]{1,2,0:T(4,128)(2,1)}, u32[]{:S(2)}) copy-start(bf16[1,96,4]{1,2,0:T(4,128)(2,1)} %param.23) | copy-start | bytes 2308
  99.8 97.5 %copy-start.5 = (f32[2880]{0:T(1024)S(1)}, f32[2880]{0:T(1024)}, u32[]{:S(2)}) copy-start(f32[2880]{0:T(1024)} %param.32) | copy-start | bytes 34564
  99.8 95.3 %all-gather.8.cloned.1.call-start = ((), (), s32[]{:S(2)}) async-start(), calls=%async_computation.6 | async-start | bytes 2764800 | tf_op jit(solution)/shard_map/all_gather | solution.py:146
  197.3 146.2 %slice-start = ((s8[4239360]{0:T(1024)(128)(4,1)}), s8[4194304]{0:T(1024)(128)(4,1)S(1)}, s32[]{:S(2)}) async-start(s8[4239360]{0:T(1024)(128)(4,1)} %bitcast.133), calls=%async_computation.8 | async-start | bytes 8388608
  199.7 143.9 %slice-start.1 = ((s8[4239360]{0:T(1024)(128)(4,1)}), s8[45056]{0:T(1024)(128)(4,1)S(1)}, s32[]{:S(2)}) async-start(s8[4239360]{0:T(1024)(128)(4,1)} %bitcast.133), calls=%async_computation.9 | async-start | bytes 90112
  384.6 138.8 %all-to-all-start.1 = ((bf16[8,256,2944]{2,1,0:T(8,128)(2,1)}), bf16[8,256,2944]{2,1,0:T(8,128)(2,1)}, u32[]{:S(2)}, u32[]{:S(2)}) async-start(bf16[8,256,2944]{2,1,0:T(8,128)(2,1)} %bitcast.120), calls=%async_computation.2 | async-start | bytes 24117248 | tf_op jit(solution)/shard_map/all_to_all | solution.py:192
  389.9 188.3 %reduce-scatter.5.cloned.1.call-start = ((), (), s32[]{:S(2)}) async-start(), calls=%async_computation.7 | async-start | bytes 2764800 | tf_op jit(solution)/shard_map/reduce_scatter | solution.py:205
  533.5 44.7 %copy-start.2 = (bf16[384,720]{0,1:T(8,128)(2,1)S(1)}, bf16[384,720]{0,1:T(8,128)(2,1)}, u32[]{:S(2)}) copy-start(bf16[384,720]{0,1:T(8,128)(2,1)} %add_convert_fusion.1) | copy-start | bytes 1658884
  535.3 73.9 %copy-start.1 = (bf16[512,2880]{0,1:T(8,128)(2,1)S(1)}, bf16[512,2880]{0,1:T(8,128)(2,1)}, u32[]{:S(2)}) copy-start(bf16[512,2880]{0,1:T(8,128)(2,1)} %param.27) | copy-start | bytes 8847364
Sparse Core Ops, SparseCore 0:
  9.6 58.0 all-gather.5
  100.0 45.3 reduce-scatter.2
  147.6 47.5 all-gather.7
  535.3 42.8 reduce-scatter.4

commit v4 on v1

--- a/solution.py
+++ b/solution.py
@@ -131,16 +131,33 @@
     key_heads = rotate_heads(joined_projection[:, :, QUERY_GROUP], positions).astype(jnp.bfloat16)
     value_heads = joined_projection[:, :, QUERY_GROUP + 1].astype(jnp.bfloat16)
     blended_hidden = attend_heads(queries, key_heads, value_heads, segment_row, sinks)
+    share = col_tokens // groups
+    quarter = hidden.shape[1]
+    rank_total = output_down_maps.shape[1]
+    route_pack = jnp.concatenate(
+        [routes[0].astype(jnp.bfloat16), expert_gates[0].astype(jnp.bfloat16)], axis=1
+    )
+    pack_width = -(quarter + rank_total) % 128 or 128
+    route_pack = jnp.pad(route_pack, ((0, 0), (0, pack_width - 2 * TOP)))
+    pack_rows = lax.dynamic_update_slice_in_dim(
+        jnp.zeros((col_tokens, pack_width), jnp.bfloat16), route_pack, position_dp * share, 0
+    )
     partial_out = jnp.dot(blended_hidden, attention_out_weight, preferred_element_type=jnp.float32)
-    mine_out = lax.psum_scatter(
-        partial_out.astype(jnp.bfloat16), "dp", scatter_dimension=1, tiled=True
-    ).astype(jnp.float32)
-    output_reduced = lax.psum(
-        jnp.dot(blended_hidden, output_down_maps, preferred_element_type=jnp.float32).astype(
-            jnp.bfloat16
-        ),
-        "dp",
-    )
+    low_local = jnp.dot(blended_hidden, output_down_maps, preferred_element_type=jnp.float32)
+    joined_send = jnp.concatenate(
+        [
+            partial_out.astype(jnp.bfloat16).reshape(col_tokens, groups, quarter),
+            jnp.broadcast_to(
+                low_local.astype(jnp.bfloat16)[:, None, :], (col_tokens, groups, rank_total)
+            ),
+            jnp.broadcast_to(pack_rows[:, None, :], (col_tokens, groups, pack_width)),
+        ],
+        axis=2,
+    ).reshape(col_tokens, -1)
+    joined_back = lax.psum_scatter(joined_send, "dp", scatter_dimension=1, tiled=True)
+    mine_out = joined_back[:, :quarter].astype(jnp.float32)
+    output_reduced = joined_back[:, quarter : quarter + rank_total]
+    pack_col = joined_back[:, quarter + rank_total :]
     selected_output = jnp.where(adapter_mask, output_reduced, jnp.zeros_like(output_reduced))
     adapter_delta = adapter_scale * jnp.dot(
         selected_output, output_up_maps, preferred_element_type=jnp.float32
@@ -148,12 +165,14 @@
     resid = (hidden.astype(jnp.float32) + mine_out + adapter_delta).astype(jnp.bfloat16)
     column_full = lax.all_gather(resid, "dp", axis=1, tiled=True)
     moe_in = rms_scale(column_full.astype(jnp.float32), expert_norm_gain).astype(jnp.bfloat16)
-    share = col_tokens // groups
+    lane_pad = -width % 128
+    moe_in = jnp.pad(moe_in, ((0, 0), (0, lane_pad)))
+    wide = width + lane_pad
     experts = expert_gate_weight.shape[0] * columns
     capacity = 4 * share * TOP // (3 * experts)
     col_capacity = groups * capacity
-    route_col = lax.all_gather(routes[0], "dp", axis=0, tiled=True)
-    gates_col = lax.all_gather(expert_gates[0], "dp", axis=0, tiled=True)
+    route_col = pack_col[:, :TOP].astype(jnp.int32)
+    gates_col = pack_col[:, TOP : 2 * TOP]
     route_flat = route_col.reshape(-1)
     one_hot = (route_flat[:, None] == jnp.arange(experts, dtype=jnp.int32)[None, :]).astype(
         jnp.int32
@@ -162,49 +181,72 @@
     target = route_flat * col_capacity + slot_rows
     source_rows = jnp.arange(route_flat.shape[0], dtype=jnp.int32) // TOP
     table = jnp.full((experts * col_capacity,), col_tokens, jnp.int32).at[target].set(source_rows)
-    padded = jnp.concatenate([moe_in, jnp.zeros((1, width), jnp.bfloat16)], axis=0)
-    outgoing = jnp.take(padded, table, axis=0).reshape(experts, col_capacity, width)
+    table = table.reshape(experts, col_capacity)
+    slot_ids = jnp.arange(experts * col_capacity, dtype=jnp.int32).reshape(experts, col_capacity)
+    target_tk = target.reshape(col_tokens, TOP)
     gate_weight = expert_gate_weight[0]
     up_weight = expert_up_weight[0]
-    down_weight = expert_down_weight[0]
-    arrived = lax.all_to_all(outgoing, "expert", split_axis=0, concat_axis=0, tiled=True)
-    rows_in = arrived.reshape(-1, width)
-    gate_part = jnp.dot(rows_in, gate_weight, preferred_element_type=jnp.float32)
-    up_part = jnp.dot(rows_in, up_weight, preferred_element_type=jnp.float32)
-    activated = (gate_part * jax.nn.sigmoid(glu_alpha * gate_part) * (up_part + 1.0)).astype(
-        jnp.bfloat16
-    )
-    shares_out = (
-        jnp.dot(activated, down_weight, preferred_element_type=jnp.float32)
-        .astype(jnp.bfloat16)
-        .reshape(experts, col_capacity, width)
-    )
-    answers = lax.all_to_all(shares_out, "expert", split_axis=0, concat_axis=0, tiled=True)
-    picked_out = jnp.take(answers.reshape(experts * col_capacity, width), target, axis=0).reshape(
-        col_tokens, TOP, width
-    )
-    mixture = jnp.einsum(
-        "tk,tkd->td", gates_col, picked_out, preferred_element_type=jnp.float32
-    )
-    moe_part = lax.psum_scatter(
-        mixture.astype(jnp.bfloat16), "dp", scatter_dimension=1, tiled=True
-    )
-    moe_rounded = moe_part.astype(jnp.float32).astype(jnp.bfloat16)
-    hidden_out = (resid.astype(jnp.float32) + moe_rounded.astype(jnp.float32)).astype(jnp.bfloat16)
+    down_weight = jnp.pad(expert_down_weight[0], ((0, 0), (0, lane_pad)))
+    halves = 2 if col_capacity % 16 == 0 else 1
+    piece = col_capacity // halves
+    mixture = None
+    for h in range(halves):
+        table_h = table[:, h * piece : (h + 1) * piece].reshape(-1)
+        dispatch = (table_h[:, None] == jnp.arange(col_tokens, dtype=jnp.int32)[None, :]).astype(
+            jnp.bfloat16
+        )
+        outgoing = (
+            jnp.dot(dispatch, moe_in, preferred_element_type=jnp.float32)
+            .astype(jnp.bfloat16)
+            .reshape(experts, piece, wide)
+        )
+        arrived = lax.all_to_all(outgoing, "expert", split_axis=0, concat_axis=0, tiled=True)
+        rows_in = arrived.reshape(-1, wide)[:, :width]
+        gate_part = jnp.dot(rows_in, gate_weight, preferred_element_type=jnp.float32)
+        up_part = jnp.dot(rows_in, up_weight, preferred_element_type=jnp.float32)
+        activated = (gate_part * jax.nn.sigmoid(glu_alpha * gate_part) * (up_part + 1.0)).astype(
+            jnp.bfloat16
+        )
+        shares_out = (
+            jnp.dot(activated, down_weight, preferred_element_type=jnp.float32)
+            .astype(jnp.bfloat16)
+            .reshape(experts, piece, wide)
+        )
+        answers = lax.all_to_all(shares_out, "expert", split_axis=0, concat_axis=0, tiled=True)
+        slots_h = slot_ids[:, h * piece : (h + 1) * piece].reshape(-1)
+        combine = jnp.sum(
+            jnp.where(
+                target_tk[:, :, None] == slots_h[None, None, :],
+                gates_col[:, :, None],
+                jnp.zeros((), jnp.bfloat16),
+            ),
+            axis=1,
+        ).astype(jnp.bfloat16)
+        part = jnp.dot(
+            combine, answers.reshape(experts * piece, wide), preferred_element_type=jnp.float32
+        )
+        mixture = part if mixture is None else mixture + part
+    mixture = mixture[:, :width]
     counter = jnp.arange(col_tokens, dtype=jnp.int32)
     request_ids = jnp.arange(REQS, dtype=jnp.int32)
     last_index = jnp.max(
         jnp.where(segment_row[None, :] == request_ids[:, None], counter[None, :], -1), axis=1
     )
-    chosen = jnp.take(hidden_out, jnp.clip(last_index, 0, col_tokens - 1), axis=0)
-    spread_rows = lax.all_gather(chosen, ("dp", "expert"), axis=0, tiled=True)
-    quarter = chosen.shape[1]
-    tail_full = (
-        spread_rows.reshape(groups, columns * REQS, quarter)
-        .transpose(1, 0, 2)
-        .reshape(columns * REQS, groups * quarter)
-    )
-    tail_rows = rms_scale(tail_full.astype(jnp.float32), closing_gain).astype(jnp.bfloat16)
+    last_index = jnp.clip(last_index, 0, col_tokens - 1)
+    last_mix = jnp.take(mixture, last_index, axis=0).reshape(REQS * groups, quarter)
+    moe_send = jnp.concatenate(
+        [mixture, jnp.tile(last_mix, (1, groups))], axis=0
+    ).astype(jnp.bfloat16)
+    moe_back = lax.psum_scatter(moe_send, "dp", scatter_dimension=1, tiled=True)
+    moe_rounded = moe_back[:col_tokens].astype(jnp.float32).astype(jnp.bfloat16)
+    hidden_out = (resid.astype(jnp.float32) + moe_rounded.astype(jnp.float32)).astype(jnp.bfloat16)
+    last_moe = moe_back[col_tokens:].reshape(REQS, width)
+    last_resid = jnp.take(column_full, last_index, axis=0)
+    last_hidden = (last_resid.astype(jnp.float32) + last_moe.astype(jnp.float32)).astype(
+        jnp.bfloat16
+    )
+    ends = rms_scale(last_hidden.astype(jnp.float32), closing_gain).astype(jnp.bfloat16)
+    tail_rows = lax.all_gather(ends, "expert", axis=0, tiled=True)
     logits = jnp.dot(tail_rows, vocabulary_weight, preferred_element_type=jnp.float32)
     return (hidden_out, logits)
 

time: 775 us -> 597 us (0.77)
  blocking collectives: 203 us -> 9.22 us
  local copies, waits for them, and re-layouts: 131 us -> 29.4 us
  waiting for transfers between devices: 309 us -> 388 us
  matrix products: 67.9 us -> 102 us
  other arithmetic: 43.1 us -> 24.8 us
  starting transfers between devices: 5.67 us -> 20 us
    all_to_all x1 -> x0, blocking collectives: 134 us -> none  [shards(): lax.all_to_all(outgoing, 'expert', split_axis=0, concat_axis=0, tiled=True)]
    all_to_all x0 -> x2, waiting for transfers between devices: none -> 105 us  [shards(): lax.all_to_all(outgoing, 'expert', split_axis=0, concat_axis=0, tiled=True)]
    unnamed x5 -> x6, waiting for transfers between devices: 0.75 us -> 101 us
    reduce_scatter x2 -> x0, waiting for transfers between devices: 91.1 us -> none  [the longest x1 48 us: shards(): lax.psum_scatter(partial_out.astype(jnp.bfloat16), 'dp', scatter_dimensio...]
    all_gather x3 -> x1, blocking collectives: 68.7 us -> 9.22 us  [shards(): tail_rows = lax.all_gather(ends, 'expert', axis=0, tiled=True)]
    gather x5 -> x4, local copies, waits for them, and re-layouts: 63.6 us -> 5.24 us  [the longest x2 2.62 us: shards(): last_resid = jnp.take(column_full, last_index, axis=0)]
    all_to_all x2 -> x0, local copies, waits for them, and re-layouts: 32.5 us -> none  [the longest x1 16.3 us: shards(): lax.all_to_all(outgoing, 'expert', split_axis=0, concat_axis=0, tiled=True)]
    psum x1 -> x0, waiting for transfers between devices: 29 us -> none  [shards(): lax.psum(jnp.dot(blended_hidden, output_down_maps, preferred_element_type...]
  transfers between devices with their start and end apart: 6 -> 8, of which waited for: 6 -> 8; matrix products, arithmetic and copies ran while one was open for 2% -> 16% of each run, Pallas kernels for 0% -> 0%
where the time goes in v4:
time: 597 us; the launch traced here: 589 us
  waiting for transfers between devices  388 us (65%)
  matrix products  102 us (17%)
  local copies, waits for them, and re-layouts  29.4 us (5%)
  other arithmetic  24.8 us (4%)
  starting transfers between devices  20 us (3%)
  between operations  14.7 us (2%)
  blocking collectives  9.22 us (2%)
    all_to_all x2, waiting for transfers between devices, shards(): lax.all_to_all(outgoing, 'expert', split_axis=0, concat_axis=0, tiled=True)  105 us
    unnamed x6, waiting for transfers between devices  101 us
    all_to_all x2, waiting for transfers between devices, shards(): lax.all_to_all(shares_out, 'expert', split_axis=0, concat_axis=0, tiled=T...  98.4 us
    all_gather x1, waiting for transfers between devices, shards(): gathered_rows = lax.all_gather(hidden, 'dp', axis=1, tiled=True)  46.7 us
    all_gather x1, waiting for transfers between devices, shards(): column_full = lax.all_gather(resid, 'dp', axis=1, tiled=True)  37.2 us
    dot_general x2, matrix products, shards(): jnp.dot(activated, down_weight, preferred_element_type=jnp.float32)  33.6 us
    dot_general x2, matrix products, shards(): up_part = jnp.dot(rows_in, up_weight, preferred_element_type=jnp.float32)  20.7 us
    dot_general x2, matrix products, shards(): jnp.dot(combine, answers.reshape(experts * piece, wide), preferred_elemen...  14 us
  transfers between devices with their start and end apart: 8, of which 8 were waited for; matrix products, arithmetic and copies ran while one was open for 16% of the time, Pallas kernels for 0%

profile of v4, /device:TPU:0, one launch (start us, length us, event | category | flops | bytes accessed | tf_op | source)
XLA Modules:
  0.0 588.6 jit_solution(11044853060282309407)
XLA Ops:
  7.2 0.7 all-gather.4.cloned.1.call-update
  8.0 0.7 exp.21
  8.7 0.7 reduce.5
  9.4 0.8 compare_reduce_fusion
  10.3 0.3 reduce-window.15
  10.8 0.7 convert_bitcast_fusion
  11.5 0.7 fusion.96
  12.5 0.7 select_reduce_fusion.1
  13.3 0.3 multiply_cosine_fusion
  13.7 46.7 %all-gather.4.cloned.1.call-done = bf16[384,2880]{0,1:T(8,128)(2,1)} async-done(((bf16[384,720]{0,1:T(8,128)(2,1)}), bf16[384,2880]{0,1:T(8,128)(2,1)}) %all-gather.4.cloned.1.call-update) | async-done | bytes 2211856 | tf_op jit(solution)/shard_map/all_gather | solution.py:103
  60.4 2.2 fusion.8
  62.6 5.9 %fusion.21 = f32[384,640]{1,0:T(8,128)} fusion(bf16[2880,1,640]{2,0,1:T(8,128)(2,1)} %param.25, bf16[384,2880]{0,1:T(8,128)(2,1)} %all-gather.4.cloned.1.call-done, f32[2880]{0:T(1024)} %param.24, f32[384]{0:T(512)S(1)} %add_rsqrt_fusion.1), kind=kOutput, calls=%fused_computation.38 | convolution fusion | flops 1420001280 | bytes 6894336 | tf_op jit(solution)/shard_map/dot_general | solution.py:108
  68.5 4.8 fusion.50
  73.3 2.5 copy.63
  75.8 0.9 slice_bitcast_fusion.1
  76.7 1.2 slice_bitcast_fusion
  77.9 0.3 fusion.94
  78.3 1.3 fusion.18
  79.6 2.2 fusion.52
  81.9 0.3 convolution_convert_fusion.5
  82.4 1.7 convolution_convert_fusion.4
  84.2 1.8 pad_maximum_fusion
  86.0 0.2 all-gather.6.cloned.1.call-start
  86.3 52.9 %reduce-scatter.7.cloned.1.call-done = bf16[896,384]{1,0:T(8,128)(2,1)} async-done(((bf16[3584,384]{1,0:T(8,128)(2,1)}), bf16[896,384]{1,0:T(8,128)(2,1)}) %reduce-scatter.7.cloned.1.call-update) | async-done | bytes 688144
  139.1 0.9 slice.123
  140.2 2.3 fusion.51
  142.5 0.8 fusion.118
  143.8 2.3 reduce-window.19
  146.1 0.3 slice_reduce_fusion
  147.1 6.2 %scatter_custom_fusion = s32[2048]{0:T(1024)S(1)} fusion(s32[1536]{0:T(1024)S(1)} %fusion.100, s32[1536]{0:T(1024)S(1)} %add_select_fusion, s32[]{:T(128)} %constant.117.clone.1), kind=kCustom, calls=%fused_computation.148 | custom fusion | bytes 8196 | tf_op jit(solution)/shard_map/scatter | solution.py:183
  153.3 37.2 %all-gather.6.cloned.1.call-done = bf16[384,2880]{0,1:T(8,128)(2,1)} async-done(((bf16[384,720]{0,1:T(8,128)(2,1)}), bf16[384,2880]{0,1:T(8,128)(2,1)}) %all-gather.6.cloned.1.call-update) | async-done | bytes 2211856 | tf_op jit(solution)/shard_map/all_gather | solution.py:166
  190.5 2.2 fusion.11
  192.7 2.2 fusion.13
  194.9 5.5 convolution_convert_fusion
  200.4 4.8 all-to-all-start.2
  205.2 5.4 convolution_convert_fusion.1
  210.6 63.4 %all-to-all-done.2 = bf16[8,128,2944]{2,1,0:T(8,128)(2,1)} async-done(((bf16[8,128,2944]{2,1,0:T(8,128)(2,1)}), bf16[8,128,2944]{2,1,0:T(8,128)(2,1)}, u32[]{:S(2)}, u32[]{:S(2)}) %all-to-all-start.2) | async-done | bytes 6029344 | tf_op jit(solution)/shard_map/all_to_all | solution.py:203
  274.0 4.9 all-to-all-start
  278.9 10.4 %fusion = f32[1024,720]{0,1:T(8,128)} fusion(bf16[1024,2944]{1,0:T(8,128)(2,1)} %bitcast.38, bf16[1,2880,720]{1,2,0:T(8,128)(2,1)} %param.34), kind=kOutput, calls=%fused_computation.13 | convolution fusion | flops 4246732800 | bytes 13125632 | tf_op jit(solution)/shard_map/dot_general | solution.py:206
  289.3 16.8 %convolution_convert_fusion.2 = bf16[1024,2944]{1,0:T(8,128)(2,1)} fusion(bf16[720,2880]{1,0:T(8,128)(2,1)} %bitcast.162, f32[1024,720]{0,1:T(8,128)} %fusion, bf16[1,2880,720]{1,2,0:T(8,128)(2,1)} %param.33, bf16[1024,2944]{1,0:T(8,128)(2,1)} %bitcast.38), kind=kOutput, calls=%fused_computation.7 | convolution fusion | flops 8596750336 | bytes 23302144 | tf_op jit(solution)/shard_map/dot_general | solution.py:211
  306.1 41.6 %all-to-all-done = bf16[8,128,2944]{2,1,0:T(8,128)(2,1)} async-done(((bf16[8,128,2944]{2,1,0:T(8,128)(2,1)}), bf16[8,128,2944]{2,1,0:T(8,128)(2,1)}, u32[]{:S(2)}, u32[]{:S(2)}) %all-to-all-start) | async-done | bytes 6029344 | tf_op jit(solution)/shard_map/all_to_all | solution.py:203
  347.7 5.0 all-to-all-start.3
  352.7 10.4 %fusion.4 = f32[1024,720]{0,1:T(8,128)} fusion(bf16[1024,2944]{1,0:T(8,128)(2,1)} %bitcast.29, bf16[1,2880,720]{1,2,0:T(8,128)(2,1)} %param.34), kind=kOutput, calls=%fused_computation.17 | convolution fusion | flops 4246732800 | bytes 13125632 | tf_op jit(solution)/shard_map/dot_general | solution.py:206
  363.1 16.8 %convolution_convert_fusion.3 = bf16[1024,2944]{1,0:T(8,128)(2,1)} fusion(bf16[720,2880]{1,0:T(8,128)(2,1)} %bitcast.163, f32[1024,720]{0,1:T(8,128)} %fusion.4, bf16[1,2880,720]{1,2,0:T(8,128)(2,1)} %param.33, bf16[1024,2944]{1,0:T(8,128)(2,1)} %bitcast.29), kind=kOutput, calls=%fused_computation.8 | convolution fusion | flops 8596750336 | bytes 23302144 | tf_op jit(solution)/shard_map/dot_general | solution.py:211
  379.9 41.6 %all-to-all-done.3 = bf16[8,128,2944]{2,1,0:T(8,128)(2,1)} async-done(((bf16[8,128,2944]{2,1,0:T(8,128)(2,1)}), bf16[8,128,2944]{2,1,0:T(8,128)(2,1)}, u32[]{:S(2)}, u32[]{:S(2)}) %all-to-all-start.3) | async-done | bytes 6029344 | tf_op jit(solution)/shard_map/all_to_all | solution.py:215
  421.5 4.7 all-to-all-start.1
  426.2 0.3 reduce-scatter.9.cloned.1.call-start
  426.9 0.3 copy-done.9
  427.3 2.8 fusion.23
  430.1 8.1 %fusion.120 = f32[384,2944]{0,1:T(8,128)} fusion(bf16[384,1024]{1,0:T(8,128)(2,1)S(1)} %get-tuple-element.5, bf16[1024,2944]{1,0:T(8,128)(2,1)} %bitcast.40), kind=kOutput, calls=%fused_computation.183 | convolution fusion | flops 2315255808 | bytes 11337728 | tf_op jit(solution)/shard_map/dot_general | solution.py:225
  438.2 56.8 %all-to-all-done.1 = bf16[8,128,2944]{2,1,0:T(8,128)(2,1)} async-done(((bf16[8,128,2944]{2,1,0:T(8,128)(2,1)}), bf16[8,128,2944]{2,1,0:T(8,128)(2,1)}, u32[]{:S(2)}, u32[]{:S(2)}) %all-to-all-start.1) | async-done | bytes 6029344 | tf_op jit(solution)/shard_map/all_to_all | solution.py:215
  495.0 5.8 fusion.119
  500.8 0.7 slice_add_fusion
  501.5 2.6 copy.70
  504.1 2.5 gather_fusion
  507.1 2.0 maximum_bitcast_fusion
  509.1 4.4 copy.74
  513.5 2.5 gather_fusion.1
  516.1 47.4 %reduce-scatter.9.cloned.1.call-done = bf16[720,400]{1,0:T(8,128)(2,1)} async-done(((bf16[2880,400]{1,0:T(8,128)(2,1)}), bf16[720,400]{1,0:T(8,128)(2,1)}) %reduce-scatter.9.cloned.1.call-update) | async-done | bytes 576016
  563.5 2.0 add_convert_fusion
  565.5 0.9 slice.136
  567.1 0.8 fusion.95
  567.9 9.2 %all-gather = bf16[8,4,2880]{2,1,0:T(4,128)(2,1)S(1)} all-gather(bf16[1,4,2880]{2,1,0:T(4,128)(2,1)S(1)} %fusion.95), channel_id=1, replica_groups=mesh['dp'=4,'expert'=8] {'expert'}, dimensions={0}, use_global_device_ids=true | all-gather | bytes 207360 | tf_op jit(solution)/shard_map/all_gather | solution.py:249
  577.2 4.4 fusion.121
  (84 shorter events, 4.3 us)
Async XLA Ops:
  7.2 75.2 %copy-start = (bf16[512,2880]{0,1:T(8,128)(2,1)S(1)}, bf16[512,2880]{0,1:T(8,128)(2,1)}, u32[]{:S(2)}) copy-start(bf16[512,2880]{0,1:T(8,128)(2,1)} %param.27) | copy-start | bytes 8847364
  7.2 53.2 %all-gather.4.cloned.1.call-start = ((), (), s32[]{:S(2)}) async-start(), calls=%async_computation.6 | async-start | bytes 2764800 | tf_op jit(solution)/shard_map/all_gather | solution.py:103
  7.9 131.2 %reduce-scatter.7.cloned.1.call-start = ((), (), s32[]{:S(2)}) async-start(), calls=%async_computation.8 | async-start | bytes 3440640
  12.4 0.9 copy-start.5
  62.6 6.0 %copy-start.11 = (bf16[128,1,640]{2,0,1:T(8,128)(2,1)S(1)}, bf16[128,1,640]{2,0,1:T(8,128)(2,1)}, u32[]{:S(2)}) copy-start(bf16[128,1,640]{2,0,1:T(8,128)(2,1)} %param.29) | copy-start | bytes 491524
  62.6 6.0 %copy-start.12 = (f32[2880]{0:T(1024)S(1)}, f32[2880]{0:T(1024)}, u32[]{:S(2)}) copy-start(f32[2880]{0:T(1024)} %param.24) | copy-start | bytes 34564
  79.6 2.3 copy-start.7
  82.3 1.7 copy-start.6
  84.1 56.0 %copy-start.4 = (bf16[384,720]{0,1:T(8,128)(2,1)S(1)}, bf16[384,720]{0,1:T(8,128)(2,1)}, u32[]{:S(2)}) copy-start(bf16[384,720]{0,1:T(8,128)(2,1)} %param.19) | copy-start | bytes 1658884
  84.1 56.0 %copy-start.10 = (bf16[128,720]{0,1:T(8,128)(2,1)S(1)}, bf16[128,720]{0,1:T(8,128)(2,1)}, u32[]{:S(2)}) copy-start(bf16[128,720]{0,1:T(8,128)(2,1)} %param.31) | copy-start | bytes 552964
  86.0 106.7 %copy-start.8 = (f32[2880]{0:T(1024)S(1)}, f32[2880]{0:T(1024)}, u32[]{:S(2)}) copy-start(f32[2880]{0:T(1024)} %param.32) | copy-start | bytes 34564
  86.0 104.5 %all-gather.6.cloned.1.call-start = ((), (), s32[]{:S(2)}) async-start(), calls=%async_computation.7 | async-start | bytes 2764800 | tf_op jit(solution)/shard_map/all_gather | solution.py:166
  200.4 73.6 %all-to-all-start.2 = ((bf16[8,128,2944]{2,1,0:T(8,128)(2,1)}), bf16[8,128,2944]{2,1,0:T(8,128)(2,1)}, u32[]{:S(2)}, u32[]{:S(2)}) async-start(bf16[8,128,2944]{2,1,0:T(8,128)(2,1)} %bitcast.146), calls=%async_computation.2 | async-start | bytes 12058624 | tf_op jit(solution)/shard_map/all_to_all | solution.py:203
  274.0 73.7 %all-to-all-start = ((bf16[8,128,2944]{2,1,0:T(8,128)(2,1)}), bf16[8,128,2944]{2,1,0:T(8,128)(2,1)}, u32[]{:S(2)}, u32[]{:S(2)}) async-start(bf16[8,128,2944]{2,1,0:T(8,128)(2,1)} %bitcast.144), calls=%async_computation | async-start | bytes 12058624 | tf_op jit(solution)/shard_map/all_to_all | solution.py:203
  347.7 73.8 %all-to-all-start.3 = ((bf16[8,128,2944]{2,1,0:T(8,128)(2,1)}), bf16[8,128,2944]{2,1,0:T(8,128)(2,1)}, u32[]{:S(2)}, u32[]{:S(2)}) async-start(bf16[8,128,2944]{2,1,0:T(8,128)(2,1)} %bitcast.145), calls=%async_computation.3 | async-start | bytes 12058624 | tf_op jit(solution)/shard_map/all_to_all | solution.py:215
  421.5 73.5 %all-to-all-start.1 = ((bf16[8,128,2944]{2,1,0:T(8,128)(2,1)}), bf16[8,128,2944]{2,1,0:T(8,128)(2,1)}, u32[]{:S(2)}, u32[]{:S(2)}) async-start(bf16[8,128,2944]{2,1,0:T(8,128)(2,1)} %bitcast.143), calls=%async_computation.1 | async-start | bytes 12058624 | tf_op jit(solution)/shard_map/all_to_all | solution.py:215
  426.2 137.3 %reduce-scatter.9.cloned.1.call-start = ((), (), s32[]{:S(2)}) async-start(), calls=%async_computation.9 | async-start | bytes 3686400
  426.7 0.5 copy-start.9
  495.0 5.8 copy-start.2
  509.1 54.4 %copy-start.3 = (bf16[384,720]{0,1:T(8,128)(2,1)S(1)}, bf16[384,720]{0,1:T(8,128)(2,1)}, u32[]{:S(2)}) copy-start(bf16[384,720]{0,1:T(8,128)(2,1)} %fusion.51) | copy-start | bytes 1658884
  509.1 72.5 %copy-start.1 = (bf16[512,2880]{0,1:T(8,128)(2,1)S(1)}, bf16[512,2880]{0,1:T(8,128)(2,1)}, u32[]{:S(2)}) copy-start(bf16[512,2880]{0,1:T(8,128)(2,1)} %param.27) | copy-start | bytes 8847364
Sparse Core Ops, SparseCore 0:
  9.6 50.7 all-gather.3
  86.1 52.9 reduce-scatter.6
  142.6 47.8 all-gather.5
  509.2 54.2 reduce-scatter.8

commit v5 on v4

--- a/solution.py
+++ b/solution.py
@@ -163,44 +163,61 @@
         selected_output, output_up_maps, preferred_element_type=jnp.float32
     )
     resid = (hidden.astype(jnp.float32) + mine_out + adapter_delta).astype(jnp.bfloat16)
-    column_full = lax.all_gather(resid, "dp", axis=1, tiled=True)
-    moe_in = rms_scale(column_full.astype(jnp.float32), expert_norm_gain).astype(jnp.bfloat16)
     lane_pad = -width % 128
-    moe_in = jnp.pad(moe_in, ((0, 0), (0, lane_pad)))
     wide = width + lane_pad
     experts = expert_gate_weight.shape[0] * columns
     capacity = 4 * share * TOP // (3 * experts)
-    col_capacity = groups * capacity
-    route_col = pack_col[:, :TOP].astype(jnp.int32)
-    gates_col = pack_col[:, TOP : 2 * TOP]
-    route_flat = route_col.reshape(-1)
-    one_hot = (route_flat[:, None] == jnp.arange(experts, dtype=jnp.int32)[None, :]).astype(
-        jnp.int32
-    )
-    slot_rows = jnp.sum((jnp.cumsum(one_hot, axis=0) - one_hot) * one_hot, axis=1)
-    target = route_flat * col_capacity + slot_rows
-    source_rows = jnp.arange(route_flat.shape[0], dtype=jnp.int32) // TOP
-    table = jnp.full((experts * col_capacity,), col_tokens, jnp.int32).at[target].set(source_rows)
-    table = table.reshape(experts, col_capacity)
-    slot_ids = jnp.arange(experts * col_capacity, dtype=jnp.int32).reshape(experts, col_capacity)
-    target_tk = target.reshape(col_tokens, TOP)
     gate_weight = expert_gate_weight[0]
     up_weight = expert_up_weight[0]
     down_weight = jnp.pad(expert_down_weight[0], ((0, 0), (0, lane_pad)))
-    halves = 2 if col_capacity % 16 == 0 else 1
-    piece = col_capacity // halves
-    mixture = None
+    halves = 2 if groups % 2 == 0 else 1
+    half_tokens = col_tokens // halves
+    half_capacity = (groups // halves) * capacity
+    counter = jnp.arange(col_tokens, dtype=jnp.int32)
+    request_ids = jnp.arange(REQS, dtype=jnp.int32)
+    last_index = jnp.max(
+        jnp.where(segment_row[None, :] == request_ids[:, None], counter[None, :], -1), axis=1
+    )
+    last_index = jnp.clip(last_index, 0, col_tokens - 1)
+    moe_rows = []
+    last_parts = []
+    last_resid_parts = []
+    held = None
     for h in range(halves):
-        table_h = table[:, h * piece : (h + 1) * piece].reshape(-1)
-        dispatch = (table_h[:, None] == jnp.arange(col_tokens, dtype=jnp.int32)[None, :]).astype(
+        lo = h * half_tokens
+        resid_h = resid[lo : lo + half_tokens]
+        column_h = lax.all_gather(resid_h, "dp", axis=1, tiled=True)
+        if held is not None:
+            column_h, held = lax.optimization_barrier((column_h, held))
+        moe_in = rms_scale(column_h.astype(jnp.float32), expert_norm_gain).astype(jnp.bfloat16)
+        moe_in = jnp.pad(moe_in, ((0, 0), (0, lane_pad)))
+        pack_h = pack_col[lo : lo + half_tokens]
+        route_flat = pack_h[:, :TOP].astype(jnp.int32).reshape(-1)
+        gates_h = pack_h[:, TOP : 2 * TOP]
+        one_hot = (route_flat[:, None] == jnp.arange(experts, dtype=jnp.int32)[None, :]).astype(
+            jnp.int32
+        )
+        slot_rows = jnp.sum((jnp.cumsum(one_hot, axis=0) - one_hot) * one_hot, axis=1)
+        target = route_flat * half_capacity + slot_rows
+        source_rows = jnp.arange(route_flat.shape[0], dtype=jnp.int32) // TOP
+        table = (
+            jnp.full((experts * half_capacity,), half_tokens, jnp.int32)
+            .at[target]
+            .set(source_rows)
+        )
+        dispatch = (table[:, None] == jnp.arange(half_tokens, dtype=jnp.int32)[None, :]).astype(
             jnp.bfloat16
         )
         outgoing = (
             jnp.dot(dispatch, moe_in, preferred_element_type=jnp.float32)
             .astype(jnp.bfloat16)
-            .reshape(experts, piece, wide)
+            .reshape(experts, half_capacity, wide)
         )
         arrived = lax.all_to_all(outgoing, "expert", split_axis=0, concat_axis=0, tiled=True)
+        if h == 0:
+            held = arrived
+        else:
+            arrived = lax.optimization_barrier((arrived, held))[0]
         rows_in = arrived.reshape(-1, wide)[:, :width]
         gate_part = jnp.dot(rows_in, gate_weight, preferred_element_type=jnp.float32)
         up_part = jnp.dot(rows_in, up_weight, preferred_element_type=jnp.float32)
@@ -210,41 +227,45 @@
         shares_out = (
             jnp.dot(activated, down_weight, preferred_element_type=jnp.float32)
             .astype(jnp.bfloat16)
-            .reshape(experts, piece, wide)
+            .reshape(experts, half_capacity, wide)
         )
         answers = lax.all_to_all(shares_out, "expert", split_axis=0, concat_axis=0, tiled=True)
-        slots_h = slot_ids[:, h * piece : (h + 1) * piece].reshape(-1)
+        slot_ids = jnp.arange(experts * half_capacity, dtype=jnp.int32)
         combine = jnp.sum(
             jnp.where(
-                target_tk[:, :, None] == slots_h[None, None, :],
-                gates_col[:, :, None],
+                target.reshape(half_tokens, TOP)[:, :, None] == slot_ids[None, None, :],
+                gates_h[:, :, None],
                 jnp.zeros((), jnp.bfloat16),
             ),
             axis=1,
         ).astype(jnp.bfloat16)
-        part = jnp.dot(
-            combine, answers.reshape(experts * piece, wide), preferred_element_type=jnp.float32
-        )
-        mixture = part if mixture is None else mixture + part
-    mixture = mixture[:, :width]
-    counter = jnp.arange(col_tokens, dtype=jnp.int32)
-    request_ids = jnp.arange(REQS, dtype=jnp.int32)
-    last_index = jnp.max(
-        jnp.where(segment_row[None, :] == request_ids[:, None], counter[None, :], -1), axis=1
-    )
-    last_index = jnp.clip(last_index, 0, col_tokens - 1)
-    last_mix = jnp.take(mixture, last_index, axis=0).reshape(REQS * groups, quarter)
-    moe_send = jnp.concatenate(
-        [mixture, jnp.tile(last_mix, (1, groups))], axis=0
-    ).astype(jnp.bfloat16)
-    moe_back = lax.psum_scatter(moe_send, "dp", scatter_dimension=1, tiled=True)
+        mixture = jnp.dot(
+            combine,
+            answers.reshape(experts * half_capacity, wide),
+            preferred_element_type=jnp.float32,
+        )[:, :width]
+        local_last = jnp.clip(last_index - lo, 0, half_tokens - 1)
+        inside = ((last_index >= lo) & (last_index < lo + half_tokens))[:, None]
+        last_parts.append(
+            jnp.where(inside, jnp.take(mixture, local_last, axis=0), jnp.zeros((), jnp.float32))
+        )
+        last_resid_parts.append(
+            jnp.where(inside, jnp.take(column_h, local_last, axis=0), jnp.zeros((), jnp.bfloat16))
+        )
+        if h < halves - 1:
+            moe_send = mixture.astype(jnp.bfloat16)
+        else:
+            last_mix = sum(last_parts).reshape(REQS * groups, quarter)
+            moe_send = jnp.concatenate(
+                [mixture, jnp.tile(last_mix, (1, groups))], axis=0
+            ).astype(jnp.bfloat16)
+        moe_rows.append(lax.psum_scatter(moe_send, "dp", scatter_dimension=1, tiled=True))
+    moe_back = jnp.concatenate(moe_rows, axis=0)
     moe_rounded = moe_back[:col_tokens].astype(jnp.float32).astype(jnp.bfloat16)
     hidden_out = (resid.astype(jnp.float32) + moe_rounded.astype(jnp.float32)).astype(jnp.bfloat16)
     last_moe = moe_back[col_tokens:].reshape(REQS, width)
-    last_resid = jnp.take(column_full, last_index, axis=0)
-    last_hidden = (last_resid.astype(jnp.float32) + last_moe.astype(jnp.float32)).astype(
-        jnp.bfloat16
-    )
+    last_resid = sum(part.astype(jnp.float32) for part in last_resid_parts)
+    last_hidden = (last_resid + last_moe.astype(jnp.float32)).astype(jnp.bfloat16)
     ends = rms_scale(last_hidden.astype(jnp.float32), closing_gain).astype(jnp.bfloat16)
     tail_rows = lax.all_gather(ends, "expert", axis=0, tiled=True)
     logits = jnp.dot(tail_rows, vocabulary_weight, preferred_element_type=jnp.float32)

time: 597 us -> 593 us (level)
  local copies, waits for them, and re-layouts: 29.4 us -> 40 us
    all_to_all x2, waiting for transfers between devices: 105 us -> 71.8 us  [shards(): lax.all_to_all(outgoing, 'expert', split_axis=0, concat_axis=0, tiled=True)]
    unnamed x6 -> x9, waiting for transfers between devices: 101 us -> 115 us
    all_gather x1 -> x2, waiting for transfers between devices: 37.2 us -> 48.3 us  [shards(): column_h = lax.all_gather(resid_h, 'dp', axis=1, tiled=True)]
    unnamed x30 -> x34, local copies, waits for them, and re-layouts: 0.89 us -> 11.3 us
  transfers between devices with their start and end apart: 8 -> 10, of which waited for: 8 -> 10; matrix products, arithmetic and copies ran while one was open for 16% -> 16% of each run, Pallas kernels for 0% -> 0%
where the time goes in v5:
time: 593 us; the launch traced here: 584 us
  waiting for transfers between devices  383 us (65%)
  matrix products  96.9 us (16%)
  local copies, waits for them, and re-layouts  40 us (7%)
  other arithmetic  20.3 us (3%)
  starting transfers between devices  19.6 us (3%)
  between operations  15.1 us (3%)
  blocking collectives  9.37 us (2%)
    unnamed x9, waiting for transfers between devices  115 us
    all_to_all x2, waiting for transfers between devices, shards(): lax.all_to_all(shares_out, 'expert', split_axis=0, concat_axis=0, tiled=T...  101 us
    all_to_all x2, waiting for transfers between devices, shards(): lax.all_to_all(outgoing, 'expert', split_axis=0, concat_axis=0, tiled=True)  71.8 us
    all_gather x2, waiting for transfers between devices, shards(): column_h = lax.all_gather(resid_h, 'dp', axis=1, tiled=True)  48.3 us
    all_gather x1, waiting for transfers between devices, shards(): gathered_rows = lax.all_gather(hidden, 'dp', axis=1, tiled=True)  46.6 us
    dot_general x2, matrix products, shards(): jnp.dot(activated, down_weight, preferred_element_type=jnp.float32)  33.6 us
    dot_general x2, matrix products, shards(): up_part = jnp.dot(rows_in, up_weight, preferred_element_type=jnp.float32)  20.7 us
  transfers between devices with their start and end apart: 10, of which 10 were waited for; matrix products, arithmetic and copies ran while one was open for 16% of the time, Pallas kernels for 0%

profile of v5, /device:TPU:0, one launch (start us, length us, event | category | flops | bytes accessed | tf_op | source)
XLA Modules:
  0.0 584.2 jit_solution(11289110133759135964)
XLA Ops:
  7.2 0.7 all-gather.7.cloned.1.call-update
  8.0 0.8 exp.21
  8.7 0.7 reduce.3
  9.4 0.8 compare_reduce_fusion
  10.8 0.7 convert_bitcast_fusion
  11.5 0.7 fusion.113
  12.5 0.7 select_reduce_fusion.1
  13.7 46.6 %all-gather.7.cloned.1.call-done = bf16[384,2880]{0,1:T(8,128)(2,1)} async-done(((bf16[384,720]{0,1:T(8,128)(2,1)}), bf16[384,2880]{0,1:T(8,128)(2,1)}) %all-gather.7.cloned.1.call-update) | async-done | bytes 2211856 | tf_op jit(solution)/shard_map/all_gather | solution.py:103
  60.4 2.2 fusion.12
  62.6 5.9 %fusion.22 = f32[384,640]{1,0:T(8,128)} fusion(bf16[2880,1,640]{2,0,1:T(8,128)(2,1)} %param.29, bf16[384,2880]{0,1:T(8,128)(2,1)} %all-gather.7.cloned.1.call-done, f32[2880]{0:T(1024)S(1)} %copy-done.10, f32[384]{0:T(512)S(1)} %add_rsqrt_fusion), kind=kOutput, calls=%fused_computation.37 | convolution fusion | flops 1420001280 | bytes 6894336 | tf_op jit(solution)/shard_map/dot_general | solution.py:108
  68.5 4.8 fusion.57
  73.3 2.5 copy.96
  75.8 0.9 slice_bitcast_fusion.3
  76.7 1.2 slice_bitcast_fusion
  78.3 1.3 fusion.19
  79.6 2.2 fusion.59
  82.4 1.7 convolution_convert_fusion.4
  84.1 1.8 pad_maximum_fusion
  86.2 52.9 %reduce-scatter.10.cloned.1.call-done = bf16[896,384]{1,0:T(8,128)(2,1)} async-done(((bf16[3584,384]{1,0:T(8,128)(2,1)}), bf16[896,384]{1,0:T(8,128)(2,1)}) %reduce-scatter.10.cloned.1.call-update) | async-done | bytes 688144
  139.1 0.9 slice.147
  140.2 1.5 fusion.58
  141.9 0.9 copy.105
  142.8 0.9 fusion.137
  144.1 1.7 reduce-window.25
  146.6 3.4 scatter_custom_fusion
  150.0 23.1 %all-gather.9.cloned.1.call-done = bf16[4,720,192]{1,2,0:T(8,128)(2,1)} async-done(((bf16[1,720,192]{1,2,0:T(8,128)(2,1)}), bf16[4,720,192]{1,2,0:T(8,128)(2,1)}) %all-gather.9.cloned.1.call-update) | async-done | bytes 1105936 | tf_op jit(solution)/shard_map/all_gather | solution.py:189
  173.2 2.2 copy.106
  175.3 1.0 reshape.553
  177.0 4.5 convolution_convert_fusion.1
  181.4 4.7 all-to-all-start
  186.2 0.9 copy.111
  187.5 1.7 reduce-window.29
  190.1 3.6 scatter_custom_fusion.1
  193.7 25.2 %all-gather.11.cloned.1.call-done = bf16[4,720,192]{1,2,0:T(8,128)(2,1)} async-done(((bf16[1,720,192]{1,2,0:T(8,128)(2,1)}), bf16[4,720,192]{1,2,0:T(8,128)(2,1)}) %all-gather.11.cloned.1.call-update) | async-done | bytes 1105936 | tf_op jit(solution)/shard_map/all_gather | solution.py:189
  218.9 3.2 copy.112
  222.1 2.7 reshape.555
  224.8 30.2 %all-to-all-done = bf16[8,128,2944]{2,1,0:T(8,128)(2,1)} async-done(((bf16[8,128,2944]{2,1,0:T(8,128)(2,1)}), bf16[8,128,2944]{2,1,0:T(8,128)(2,1)}, u32[]{:S(2)}, u32[]{:S(2)}) %all-to-all-start) | async-done | bytes 6029344 | tf_op jit(solution)/shard_map/all_to_all | solution.py:216
  255.6 4.4 convolution_convert_fusion
  260.0 4.7 all-to-all-start.2
  264.8 10.4 %fusion.8 = f32[1024,720]{0,1:T(8,128)} fusion(bf16[1024,2944]{1,0:T(8,128)(2,1)} %bitcast.32, bf16[1,2880,720]{1,2,0:T(8,128)(2,1)} %param.38), kind=kOutput, calls=%fused_computation.20 | convolution fusion | flops 4246732800 | bytes 13125632 | tf_op jit(solution)/shard_map/dot_general | solution.py:223
  275.1 16.8 %convolution_convert_fusion.3 = bf16[1024,2944]{1,0:T(8,128)(2,1)} fusion(bf16[720,2880]{1,0:T(8,128)(2,1)} %bitcast.175, f32[1024,720]{0,1:T(8,128)} %fusion.8, bf16[1,2880,720]{1,2,0:T(8,128)(2,1)} %param.37, bf16[1024,2944]{1,0:T(8,128)(2,1)} %bitcast.32), kind=kOutput, calls=%fused_computation.13 | convolution fusion | flops 8596750336 | bytes 23302144 | tf_op jit(solution)/shard_map/dot_general | solution.py:228
  291.9 41.6 %all-to-all-done.2 = bf16[8,128,2944]{2,1,0:T(8,128)(2,1)} async-done(((bf16[8,128,2944]{2,1,0:T(8,128)(2,1)}), bf16[8,128,2944]{2,1,0:T(8,128)(2,1)}, u32[]{:S(2)}, u32[]{:S(2)}) %all-to-all-start.2) | async-done | bytes 6029344 | tf_op jit(solution)/shard_map/all_to_all | solution.py:216
  333.5 5.0 all-to-all-start.1
  338.5 10.4 %fusion.4 = f32[1024,720]{0,1:T(8,128)} fusion(bf16[1024,2944]{1,0:T(8,128)(2,1)} %bitcast.45, bf16[1,2880,720]{1,2,0:T(8,128)(2,1)} %param.38), kind=kOutput, calls=%fused_computation.16 | convolution fusion | flops 4246732800 | bytes 13125632 | tf_op jit(solution)/shard_map/dot_general | solution.py:223
  348.9 16.8 %convolution_convert_fusion.2 = bf16[1024,2944]{1,0:T(8,128)(2,1)} fusion(bf16[720,2880]{1,0:T(8,128)(2,1)} %bitcast.176, f32[1024,720]{0,1:T(8,128)} %fusion.4, bf16[1,2880,720]{1,2,0:T(8,128)(2,1)} %param.37, bf16[1024,2944]{1,0:T(8,128)(2,1)} %bitcast.45), kind=kOutput, calls=%fused_computation.12 | convolution fusion | flops 8596750336 | bytes 23302144 | tf_op jit(solution)/shard_map/dot_general | solution.py:228
  365.7 41.6 %all-to-all-done.1 = bf16[8,128,2944]{2,1,0:T(8,128)(2,1)} async-done(((bf16[8,128,2944]{2,1,0:T(8,128)(2,1)}), bf16[8,128,2944]{2,1,0:T(8,128)(2,1)}, u32[]{:S(2)}, u32[]{:S(2)}) %all-to-all-start.1) | async-done | bytes 6029344 | tf_op jit(solution)/shard_map/all_to_all | solution.py:232
  407.3 4.7 all-to-all-start.3
  412.4 0.4 fusion.51
  413.3 5.8 fusion.139
  419.1 2.2 gather_fusion
  421.3 59.5 %all-to-all-done.3 = bf16[8,128,2944]{2,1,0:T(8,128)(2,1)} async-done(((bf16[8,128,2944]{2,1,0:T(8,128)(2,1)}), bf16[8,128,2944]{2,1,0:T(8,128)(2,1)}, u32[]{:S(2)}, u32[]{:S(2)}) %all-to-all-start.3) | async-done | bytes 6029344 | tf_op jit(solution)/shard_map/all_to_all | solution.py:232
  480.8 5.8 %fusion.138 = (bf16[192,2880]{1,0:T(8,128)(2,1)}, f32[192,2880]{1,0:T(8,128)}) fusion(bf16[192,1024]{1,0:T(8,128)(2,1)S(1)} %fusion.50, bf16[1024,2944]{1,0:T(8,128)(2,1)} %bitcast.47), kind=kOutput, calls=%fused_computation.214 | convolution fusion | flops 1133015040 | bytes 9740288 | tf_op jit(solution)/shard_map/dot_general | solution.py:242
  486.7 2.2 gather_fusion.1
  489.3 2.4 pad_maximum_fusion.1
  491.6 2.5 copy.121
  494.2 2.5 copy.119
  496.8 0.6 gather_fusion.2
  497.3 0.6 gather_fusion.3
  497.9 27.5 %reduce-scatter.14.cloned.1.call-done = bf16[720,208]{1,0:T(8,128)(2,1)} async-done(((bf16[2880,208]{1,0:T(8,128)(2,1)}), bf16[720,208]{1,0:T(8,128)(2,1)}) %reduce-scatter.14.cloned.1.call-update) | async-done | bytes 299536
  525.4 1.0 slice.160
  526.5 34.0 %reduce-scatter.12.cloned.1.call-done = bf16[720,192]{1,0:T(8,128)(2,1)} async-done(((bf16[2880,192]{1,0:T(8,128)(2,1)}), bf16[720,192]{1,0:T(8,128)(2,1)}) %reduce-scatter.12.cloned.1.call-update) | async-done | bytes 276496
  560.4 2.1 add_convert_fusion
  563.1 9.4 %all-gather.2 = bf16[8,4,2880]{2,1,0:T(4,128)(2,1)S(1)} all-gather(bf16[1,4,2880]{2,1,0:T(4,128)(2,1)S(1)} %fusion.110), channel_id=1, replica_groups=mesh['dp'=4,'expert'=8] {'expert'}, dimensions={0}, use_global_device_ids=true | all-gather | bytes 207360 | tf_op jit(solution)/shard_map/all_gather | solution.py:270
  572.6 4.4 fusion.140
  (106 shorter events, 8.5 us)
Async XLA Ops:
  7.2 75.2 %copy-start = (bf16[512,2880]{0,1:T(8,128)(2,1)S(1)}, bf16[512,2880]{0,1:T(8,128)(2,1)}, u32[]{:S(2)}) copy-start(bf16[512,2880]{0,1:T(8,128)(2,1)} %param.31) | copy-start | bytes 8847364
  7.2 55.4 %copy-start.10 = (f32[2880]{0:T(1024)S(1)}, f32[2880]{0:T(1024)}, u32[]{:S(2)}) copy-start(f32[2880]{0:T(1024)} %param.28) | copy-start | bytes 34564
  7.2 53.2 %all-gather.7.cloned.1.call-start = ((), (), s32[]{:S(2)}) async-start(), calls=%async_computation.7 | async-start | bytes 2764800 | tf_op jit(solution)/shard_map/all_gather | solution.py:103
  7.9 131.2 %reduce-scatter.10.cloned.1.call-start = ((), (), s32[]{:S(2)}) async-start(), calls=%async_computation.10 | async-start | bytes 3440640
  12.4 0.9 copy-start.3
  62.6 5.9 %copy-start.9 = (bf16[128,1,640]{2,0,1:T(8,128)(2,1)S(1)}, bf16[128,1,640]{2,0,1:T(8,128)(2,1)}, u32[]{:S(2)}) copy-start(bf16[128,1,640]{2,0,1:T(8,128)(2,1)} %param.33) | copy-start | bytes 491524
  79.6 2.3 copy-start.5
  82.3 1.7 copy-start.4
  86.0 54.2 %copy-start.2 = (bf16[384,720]{0,1:T(8,128)(2,1)S(1)}, bf16[384,720]{0,1:T(8,128)(2,1)}, u32[]{:S(2)}) copy-start(bf16[384,720]{0,1:T(8,128)(2,1)} %param.23) | copy-start | bytes 1658884
  86.0 54.2 %copy-start.8 = (bf16[128,720]{0,1:T(8,128)(2,1)S(1)}, bf16[128,720]{0,1:T(8,128)(2,1)}, u32[]{:S(2)}) copy-start(bf16[128,720]{0,1:T(8,128)(2,1)} %param.35) | copy-start | bytes 552964
  86.0 87.2 %all-gather.9.cloned.1.call-start = ((), (), s32[]{:S(2)}) async-start(), calls=%async_computation.8 | async-start | bytes 1474560 | tf_op jit(solution)/shard_map/all_gather | solution.py:189
  146.5 30.1 %copy-start.6 = (f32[2880]{0:T(1024)S(1)}, f32[2880]{0:T(1024)}, u32[]{:S(2)}) copy-start(f32[2880]{0:T(1024)} %param.36) | copy-start | bytes 34564
  181.4 73.5 %all-to-all-start = ((bf16[8,128,2944]{2,1,0:T(8,128)(2,1)}), bf16[8,128,2944]{2,1,0:T(8,128)(2,1)}, u32[]{:S(2)}, u32[]{:S(2)}) async-start(bf16[8,128,2944]{2,1,0:T(8,128)(2,1)} %bitcast.146), calls=%async_computation | async-start | bytes 12058624 | tf_op jit(solution)/shard_map/all_to_all | solution.py:216
  186.2 32.7 %all-gather.11.cloned.1.call-start = ((), (), s32[]{:S(2)}) async-start(), calls=%async_computation.9 | async-start | bytes 1474560 | tf_op jit(solution)/shard_map/all_gather | solution.py:189
  260.0 73.5 %all-to-all-start.2 = ((bf16[8,128,2944]{2,1,0:T(8,128)(2,1)}), bf16[8,128,2944]{2,1,0:T(8,128)(2,1)}, u32[]{:S(2)}, u32[]{:S(2)}) async-start(bf16[8,128,2944]{2,1,0:T(8,128)(2,1)} %bitcast.147), calls=%async_computation.2 | async-start | bytes 12058624 | tf_op jit(solution)/shard_map/all_to_all | solution.py:216
  333.5 73.8 %all-to-all-start.1 = ((bf16[8,128,2944]{2,1,0:T(8,128)(2,1)}), bf16[8,128,2944]{2,1,0:T(8,128)(2,1)}, u32[]{:S(2)}, u32[]{:S(2)}) async-start(bf16[8,128,2944]{2,1,0:T(8,128)(2,1)} %bitcast.154), calls=%async_computation.1 | async-start | bytes 12058624 | tf_op jit(solution)/shard_map/all_to_all | solution.py:232
  407.3 73.5 %all-to-all-start.3 = ((bf16[8,128,2944]{2,1,0:T(8,128)(2,1)}), bf16[8,128,2944]{2,1,0:T(8,128)(2,1)}, u32[]{:S(2)}, u32[]{:S(2)}) async-start(bf16[8,128,2944]{2,1,0:T(8,128)(2,1)} %bitcast.153), calls=%async_computation.3 | async-start | bytes 12058624 | tf_op jit(solution)/shard_map/all_to_all | solution.py:232
  412.1 113.4 %reduce-scatter.14.cloned.1.call-start = ((), (), s32[]{:S(2)}) async-start(), calls=%async_computation.12 | async-start | bytes 1843200
  494.2 66.2 %reduce-scatter.12.cloned.1.call-start = ((), (), s32[]{:S(2)}) async-start(), calls=%async_computation.11 | async-start | bytes 1843200
  494.2 68.8 %copy-start.7 = (f32[2880]{0:T(1024)S(1)}, f32[2880]{0:T(1024)}, u32[]{:S(2)}) copy-start(f32[2880]{0:T(1024)} %param.40) | copy-start | bytes 34564
  562.6 14.4 %copy-start.1 = (bf16[512,2880]{0,1:T(8,128)(2,1)S(1)}, bf16[512,2880]{0,1:T(8,128)(2,1)}, u32[]{:S(2)}) copy-start(bf16[512,2880]{0,1:T(8,128)(2,1)} %param.31) | copy-start | bytes 8847364
Sparse Core Ops, SparseCore 0:
  9.6 50.7 all-gather.6
  86.1 52.9 reduce-scatter.9
  142.9 30.2 all-gather.8
  188.8 29.9 all-gather.10
  494.3 31.0 reduce-scatter.13
  527.7 32.6 reduce-scatter.11

commit v6 on v5

--- a/solution.py
+++ b/solution.py
@@ -154,15 +154,28 @@
         ],
         axis=2,
     ).reshape(col_tokens, -1)
-    joined_back = lax.psum_scatter(joined_send, "dp", scatter_dimension=1, tiled=True)
-    mine_out = joined_back[:, :quarter].astype(jnp.float32)
-    output_reduced = joined_back[:, quarter : quarter + rank_total]
-    pack_col = joined_back[:, quarter + rank_total :]
-    selected_output = jnp.where(adapter_mask, output_reduced, jnp.zeros_like(output_reduced))
-    adapter_delta = adapter_scale * jnp.dot(
-        selected_output, output_up_maps, preferred_element_type=jnp.float32
-    )
-    resid = (hidden.astype(jnp.float32) + mine_out + adapter_delta).astype(jnp.bfloat16)
+    reduced_parts = []
+
+    def reduce_rows(lo, rows):
+        joined_back = lax.psum_scatter(
+            joined_send[lo : lo + rows], "dp", scatter_dimension=1, tiled=True
+        )
+        return joined_back
+
+    def resid_rows(joined_back, lo, rows):
+        mine_out = joined_back[:, :quarter].astype(jnp.float32)
+        output_reduced = joined_back[:, quarter : quarter + rank_total]
+        selected_output = jnp.where(
+            adapter_mask[lo : lo + rows], output_reduced, jnp.zeros_like(output_reduced)
+        )
+        adapter_delta = adapter_scale * jnp.dot(
+            selected_output, output_up_maps, preferred_element_type=jnp.float32
+        )
+        resid_part = (
+            hidden[lo : lo + rows].astype(jnp.float32) + mine_out + adapter_delta
+        ).astype(jnp.bfloat16)
+        return resid_part, joined_back[:, quarter + rank_total :]
+
     lane_pad = -width % 128
     wide = width + lane_pad
     experts = expert_gate_weight.shape[0] * columns
@@ -183,15 +196,19 @@
     last_parts = []
     last_resid_parts = []
     held = None
+    pending = None
     for h in range(halves):
         lo = h * half_tokens
-        resid_h = resid[lo : lo + half_tokens]
+        joined_h = reduce_rows(lo, half_tokens)
+        if held is not None:
+            joined_h, held = lax.optimization_barrier((joined_h, held))
+        resid_h, pack_h = resid_rows(joined_h, lo, half_tokens)
+        reduced_parts.append(resid_h)
         column_h = lax.all_gather(resid_h, "dp", axis=1, tiled=True)
         if held is not None:
             column_h, held = lax.optimization_barrier((column_h, held))
         moe_in = rms_scale(column_h.astype(jnp.float32), expert_norm_gain).astype(jnp.bfloat16)
         moe_in = jnp.pad(moe_in, ((0, 0), (0, lane_pad)))
-        pack_h = pack_col[lo : lo + half_tokens]
         route_flat = pack_h[:, :TOP].astype(jnp.int32).reshape(-1)
         gates_h = pack_h[:, TOP : 2 * TOP]
         one_hot = (route_flat[:, None] == jnp.arange(experts, dtype=jnp.int32)[None, :]).astype(
@@ -229,6 +246,10 @@
             .astype(jnp.bfloat16)
             .reshape(experts, half_capacity, wide)
         )
+        if pending is not None:
+            shares_out, pending = lax.optimization_barrier((shares_out, pending))
+            moe_rows.append(lax.psum_scatter(pending, "dp", scatter_dimension=1, tiled=True))
+            pending = None
         answers = lax.all_to_all(shares_out, "expert", split_axis=0, concat_axis=0, tiled=True)
         slot_ids = jnp.arange(experts * half_capacity, dtype=jnp.int32)
         combine = jnp.sum(
@@ -253,15 +274,16 @@
             jnp.where(inside, jnp.take(column_h, local_last, axis=0), jnp.zeros((), jnp.bfloat16))
         )
         if h < halves - 1:
-            moe_send = mixture.astype(jnp.bfloat16)
+            pending = mixture.astype(jnp.bfloat16)
         else:
             last_mix = sum(last_parts).reshape(REQS * groups, quarter)
             moe_send = jnp.concatenate(
                 [mixture, jnp.tile(last_mix, (1, groups))], axis=0
             ).astype(jnp.bfloat16)
-        moe_rows.append(lax.psum_scatter(moe_send, "dp", scatter_dimension=1, tiled=True))
+            moe_rows.append(lax.psum_scatter(moe_send, "dp", scatter_dimension=1, tiled=True))
     moe_back = jnp.concatenate(moe_rows, axis=0)
     moe_rounded = moe_back[:col_tokens].astype(jnp.float32).astype(jnp.bfloat16)
+    resid = jnp.concatenate(reduced_parts, axis=0)
     hidden_out = (resid.astype(jnp.float32) + moe_rounded.astype(jnp.float32)).astype(jnp.bfloat16)
     last_moe = moe_back[col_tokens:].reshape(REQS, width)
     last_resid = sum(part.astype(jnp.float32) for part in last_resid_parts)

time: 593 us -> 602 us (1.015)
  starting transfers between devices: 19.6 us -> 29.3 us
  local copies, waits for them, and re-layouts: 40 us -> 48.7 us
    all_to_all x2, waiting for transfers between devices: 71.8 us -> 130 us  [shards(): lax.all_to_all(outgoing, 'expert', split_axis=0, concat_axis=0, tiled=True)]
    unnamed x9 -> x11, waiting for transfers between devices: 115 us -> 67.1 us
    all_to_all x2, waiting for transfers between devices: 101 us -> 88.3 us  [shards(): lax.all_to_all(shares_out, 'expert', split_axis=0, concat_axis=0, tiled=T...]
    all_to_all x2, starting transfers between devices: 9.45 us -> 19.1 us  [shards(): lax.all_to_all(outgoing, 'expert', split_axis=0, concat_axis=0, tiled=True)]
    unnamed x34 -> x43, local copies, waits for them, and re-layouts: 11.3 us -> 16.1 us
  transfers between devices with their start and end apart: 10 -> 11, of which waited for: 10 -> 9; matrix products, arithmetic and copies ran while one was open for 16% -> 15% of each run, Pallas kernels for 0% -> 0%
where the time goes in v6:
time: 602 us; the launch traced here: 597 us
  waiting for transfers between devices  379 us (63%)
  matrix products  97.6 us (16%)
  local copies, waits for them, and re-layouts  48.7 us (8%)
  starting transfers between devices  29.3 us (5%)
  other arithmetic  19.1 us (3%)
  between operations  14.9 us (2%)
  blocking collectives  9.25 us (2%)
    all_to_all x2, waiting for transfers between devices, shards(): lax.all_to_all(outgoing, 'expert', split_axis=0, concat_axis=0, tiled=True)  130 us
    all_to_all x2, waiting for transfers between devices, shards(): lax.all_to_all(shares_out, 'expert', split_axis=0, concat_axis=0, tiled=T...  88.3 us
    unnamed x11, waiting for transfers between devices  67.1 us
    all_gather x1, waiting for transfers between devices, shards(): gathered_rows = lax.all_gather(hidden, 'dp', axis=1, tiled=True)  46.6 us
    all_gather x2, waiting for transfers between devices, shards(): column_h = lax.all_gather(resid_h, 'dp', axis=1, tiled=True)  46.4 us
    dot_general x2, matrix products, shards(): jnp.dot(activated, down_weight, preferred_element_type=jnp.float32)  33.7 us
    dot_general x2, matrix products, shards(): up_part = jnp.dot(rows_in, up_weight, preferred_element_type=jnp.float32)  20.6 us
    all_to_all x2, starting transfers between devices, shards(): lax.all_to_all(outgoing, 'expert', split_axis=0, concat_axis=0, tiled=True)  19.1 us
  transfers between devices with their start and end apart: 11, of which 9 were waited for; matrix products, arithmetic and copies ran while one was open for 15% of the time, Pallas kernels for 0%

profile of v6, /device:TPU:0, one launch (start us, length us, event | category | flops | bytes accessed | tf_op | source)
XLA Modules:
  0.0 597.5 jit_solution(2650004049317802738)
XLA Ops:
  8.0 0.8 exp.21
  8.7 0.7 reduce.3
  9.4 0.8 compare_reduce_fusion
  10.8 0.7 convert_bitcast_fusion
  11.5 0.7 fusion.112
  12.5 0.7 select_reduce_fusion.1
  13.7 46.6 %all-gather.7.cloned.1.call-done = bf16[384,2880]{0,1:T(8,128)(2,1)} async-done(((bf16[384,720]{0,1:T(8,128)(2,1)}), bf16[384,2880]{0,1:T(8,128)(2,1)}) %all-gather.7.cloned.1.call-update) | async-done | bytes 2211856 | tf_op jit(solution)/shard_map/all_gather | solution.py:103
  60.4 2.2 fusion.12
  62.6 5.9 fusion.22
  68.5 4.7 fusion.56
  73.2 2.5 copy.64
  75.7 0.9 slice_bitcast_fusion.1
  76.6 1.2 slice_bitcast_fusion
  78.2 1.3 fusion.19
  79.6 2.2 fusion.59
  82.3 1.7 convolution_convert_fusion.4
  84.4 2.7 fusion.137
  87.9 37.6 %reduce-scatter.13.cloned.1.call-done = bf16[896,192]{1,0:T(8,128)(2,1)} async-done(((bf16[3584,192]{1,0:T(8,128)(2,1)}), bf16[896,192]{1,0:T(8,128)(2,1)}) %reduce-scatter.13.cloned.1.call-update) | async-done | bytes 344080
  125.5 0.8 slice.178
  126.4 1.0 slice.176
  127.7 1.0 fusion.63
  128.7 0.8 fusion.139
  129.8 1.7 reduce-window.25
  132.4 3.4 scatter_custom_fusion
  135.8 22.6 %all-gather.9.cloned.1.call-done = bf16[4,720,192]{1,2,0:T(8,128)(2,1)} async-done(((bf16[1,720,192]{1,2,0:T(8,128)(2,1)}), bf16[4,720,192]{1,2,0:T(8,128)(2,1)}) %all-gather.9.cloned.1.call-update) | async-done | bytes 1105936 | tf_op jit(solution)/shard_map/all_gather | solution.py:207
  158.4 2.2 copy.72
  160.6 1.0 reshape.552
  162.2 4.5 convolution_convert_fusion.1
  166.7 4.7 all-to-all-start
  172.0 68.2 %all-to-all-done = bf16[8,128,2944]{2,1,0:T(8,128)(2,1)} async-done(((bf16[8,128,2944]{2,1,0:T(8,128)(2,1)}), bf16[8,128,2944]{2,1,0:T(8,128)(2,1)}, u32[]{:S(2)}, u32[]{:S(2)}) %all-to-all-start) | async-done | bytes 6029344 | tf_op jit(solution)/shard_map/all_to_all | solution.py:233
  240.2 10.3 %fusion.4 = f32[1024,720]{0,1:T(8,128)} fusion(bf16[1024,2944]{1,0:T(8,128)(2,1)} %bitcast.45, bf16[1,2880,720]{1,2,0:T(8,128)(2,1)} %param.38), kind=kOutput, calls=%fused_computation.16 | convolution fusion | flops 4246732800 | bytes 13125632 | tf_op jit(solution)/shard_map/dot_general | solution.py:240
  250.5 16.9 %convolution_convert_fusion.2 = bf16[1024,2944]{1,0:T(8,128)(2,1)} fusion(bf16[720,2880]{1,0:T(8,128)(2,1)} %bitcast.181, f32[1024,720]{0,1:T(8,128)} %fusion.4, bf16[1,2880,720]{1,2,0:T(8,128)(2,1)} %param.37, bf16[1024,2944]{1,0:T(8,128)(2,1)} %bitcast.45), kind=kOutput, calls=%fused_computation.12 | convolution fusion | flops 8596750336 | bytes 23302144 | tf_op jit(solution)/shard_map/dot_general | solution.py:245
  267.4 4.9 all-to-all-start.2
  272.5 1.2 copy.87
  273.8 1.0 fusion.62
  275.1 1.7 reduce-window.29
  277.7 3.4 scatter_custom_fusion.1
  281.1 23.8 %all-gather.11.cloned.1.call-done = bf16[4,720,192]{1,2,0:T(8,128)(2,1)} async-done(((bf16[1,720,192]{1,2,0:T(8,128)(2,1)}), bf16[4,720,192]{1,2,0:T(8,128)(2,1)}) %all-gather.11.cloned.1.call-update) | async-done | bytes 1105936 | tf_op jit(solution)/shard_map/all_gather | solution.py:207
  304.9 3.2 copy.75
  308.1 2.7 reshape.554
  311.5 4.4 convolution_convert_fusion
  315.9 25.2 %all-to-all-done.2 = bf16[8,128,2944]{2,1,0:T(8,128)(2,1)} async-done(((bf16[8,128,2944]{2,1,0:T(8,128)(2,1)}), bf16[8,128,2944]{2,1,0:T(8,128)(2,1)}, u32[]{:S(2)}, u32[]{:S(2)}) %all-to-all-start.2) | async-done | bytes 6029344 | tf_op jit(solution)/shard_map/all_to_all | solution.py:253
  341.1 14.4 %all-to-all-start.1 = ((bf16[8,128,2944]{2,1,0:T(8,128)(2,1)}), bf16[8,128,2944]{2,1,0:T(8,128)(2,1)}, u32[]{:S(2)}, u32[]{:S(2)}) async-start(bf16[8,128,2944]{2,1,0:T(8,128)(2,1)} %bitcast.149), calls=%async_computation.1 | async-start | bytes 12058624 | tf_op jit(solution)/shard_map/all_to_all | solution.py:233
  356.0 6.0 fusion.141
  361.9 62.1 %all-to-all-done.1 = bf16[8,128,2944]{2,1,0:T(8,128)(2,1)} async-done(((bf16[8,128,2944]{2,1,0:T(8,128)(2,1)}), bf16[8,128,2944]{2,1,0:T(8,128)(2,1)}, u32[]{:S(2)}, u32[]{:S(2)}) %all-to-all-start.1) | async-done | bytes 6029344 | tf_op jit(solution)/shard_map/all_to_all | solution.py:233
  424.0 10.3 %fusion.8 = f32[1024,720]{0,1:T(8,128)} fusion(bf16[1024,2944]{1,0:T(8,128)(2,1)} %bitcast.40, bf16[1,2880,720]{1,2,0:T(8,128)(2,1)} %param.38), kind=kOutput, calls=%fused_computation.20 | convolution fusion | flops 4246732800 | bytes 13125632 | tf_op jit(solution)/shard_map/dot_general | solution.py:240
  434.3 16.8 %convolution_convert_fusion.3 = bf16[1024,2944]{1,0:T(8,128)(2,1)} fusion(bf16[720,2880]{1,0:T(8,128)(2,1)} %bitcast.182, f32[1024,720]{0,1:T(8,128)} %fusion.8, bf16[1,2880,720]{1,2,0:T(8,128)(2,1)} %param.37, bf16[1024,2944]{1,0:T(8,128)(2,1)} %bitcast.40), kind=kOutput, calls=%fused_computation.13 | convolution fusion | flops 8596750336 | bytes 23302144 | tf_op jit(solution)/shard_map/dot_general | solution.py:245
  451.1 4.7 all-to-all-start.3
  455.9 2.5 copy.88
  459.3 2.2 gather_fusion
  461.5 63.1 %all-to-all-done.3 = bf16[8,128,2944]{2,1,0:T(8,128)(2,1)} async-done(((bf16[8,128,2944]{2,1,0:T(8,128)(2,1)}), bf16[8,128,2944]{2,1,0:T(8,128)(2,1)}, u32[]{:S(2)}, u32[]{:S(2)}) %all-to-all-start.3) | async-done | bytes 6029344 | tf_op jit(solution)/shard_map/all_to_all | solution.py:253
  524.7 5.9 fusion.142
  530.6 2.2 gather_fusion.1
  533.2 2.4 pad_maximum_fusion.1
  535.6 2.6 copy.90
  539.3 1.9 copy.89
  541.2 28.2 %reduce-scatter.19.cloned.1.call-done = bf16[720,208]{1,0:T(8,128)(2,1)} async-done(((bf16[2880,208]{1,0:T(8,128)(2,1)}), bf16[720,208]{1,0:T(8,128)(2,1)}) %reduce-scatter.19.cloned.1.call-update) | async-done | bytes 299536
  569.4 1.1 copy.91
  570.5 0.7 copy-done.4
  571.7 9.2 %all-gather.2 = bf16[8,4,2880]{2,1,0:T(4,128)(2,1)S(1)} all-gather(bf16[1,4,2880]{2,1,0:T(4,128)(2,1)S(1)} %fusion.109), channel_id=1, replica_groups=mesh['dp'=4,'expert'=8] {'expert'}, dimensions={0}, use_global_device_ids=true | all-gather | bytes 207360 | tf_op jit(solution)/shard_map/all_gather | solution.py:292
  580.9 0.8 reshape.556
  581.7 2.2 add_convert_fusion
  583.9 2.1 copy.80
  586.0 4.5 fusion.143
  (125 shorter events, 12.2 us)
Async XLA Ops:
  7.2 75.1 %copy-start = (bf16[512,2880]{0,1:T(8,128)(2,1)S(1)}, bf16[512,2880]{0,1:T(8,128)(2,1)}, u32[]{:S(2)}) copy-start(bf16[512,2880]{0,1:T(8,128)(2,1)} %param.31) | copy-start | bytes 8847364
  7.2 55.4 %copy-start.14 = (f32[2880]{0:T(1024)S(1)}, f32[2880]{0:T(1024)}, u32[]{:S(2)}) copy-start(f32[2880]{0:T(1024)} %param.28) | copy-start | bytes 34564
  7.2 53.2 %all-gather.7.cloned.1.call-start = ((), (), s32[]{:S(2)}) async-start(), calls=%async_computation.8 | async-start | bytes 2764800 | tf_op jit(solution)/shard_map/all_gather | solution.py:103
  7.9 117.6 %reduce-scatter.13.cloned.1.call-start = ((), (), s32[]{:S(2)}) async-start(), calls=%async_computation.11 | async-start | bytes 2293760
  12.4 0.9 copy-start.8
  62.6 5.9 copy-start.13
  79.6 2.3 copy-start.10
  82.3 1.7 copy-start.9
  84.4 3.1 copy-start.2
  87.1 40.6 %copy-start.6 = (bf16[128,720]{0,1:T(8,128)(2,1)S(1)}, bf16[128,720]{0,1:T(8,128)(2,1)}, u32[]{:S(2)}) copy-start(bf16[128,720]{0,1:T(8,128)(2,1)} %param.35) | copy-start | bytes 552964
  87.1 71.3 %all-gather.9.cloned.1.call-start = ((), (), s32[]{:S(2)}) async-start(), calls=%async_computation.9 | async-start | bytes 1474560 | tf_op jit(solution)/shard_map/all_gather | solution.py:207
  132.2 29.6 %copy-start.11 = (f32[2880]{0:T(1024)S(1)}, f32[2880]{0:T(1024)}, u32[]{:S(2)}) copy-start(f32[2880]{0:T(1024)} %param.36) | copy-start | bytes 34564
  166.7 73.5 %all-to-all-start = ((bf16[8,128,2944]{2,1,0:T(8,128)(2,1)}), bf16[8,128,2944]{2,1,0:T(8,128)(2,1)}, u32[]{:S(2)}, u32[]{:S(2)}) async-start(bf16[8,128,2944]{2,1,0:T(8,128)(2,1)} %bitcast.150), calls=%async_computation | async-start | bytes 12058624 | tf_op jit(solution)/shard_map/all_to_all | solution.py:233
  171.5 101.1 %reduce-scatter.15.cloned.1.call-start = ((), (), s32[]{:S(2)}) async-start(), calls=%async_computation.12 | async-start | bytes 2293760
  267.4 6.4 %copy-start.7 = (bf16[128,720]{0,1:T(8,128)(2,1)S(1)}, bf16[128,720]{0,1:T(8,128)(2,1)}, u32[]{:S(2)}) copy-start(bf16[128,720]{0,1:T(8,128)(2,1)} %param.35) | copy-start | bytes 552964
  267.4 73.7 %all-to-all-start.2 = ((bf16[8,128,2944]{2,1,0:T(8,128)(2,1)}), bf16[8,128,2944]{2,1,0:T(8,128)(2,1)}, u32[]{:S(2)}, u32[]{:S(2)}) async-start(bf16[8,128,2944]{2,1,0:T(8,128)(2,1)} %bitcast.157), calls=%async_computation.2 | async-start | bytes 12058624 | tf_op jit(solution)/shard_map/all_to_all | solution.py:253
  272.3 32.6 %all-gather.11.cloned.1.call-start = ((), (), s32[]{:S(2)}) async-start(), calls=%async_computation.10 | async-start | bytes 1474560 | tf_op jit(solution)/shard_map/all_gather | solution.py:207
  341.1 83.0 %all-to-all-start.1 = ((bf16[8,128,2944]{2,1,0:T(8,128)(2,1)}), bf16[8,128,2944]{2,1,0:T(8,128)(2,1)}, u32[]{:S(2)}, u32[]{:S(2)}) async-start(bf16[8,128,2944]{2,1,0:T(8,128)(2,1)} %bitcast.149), calls=%async_computation.1 | async-start | bytes 12058624 | tf_op jit(solution)/shard_map/all_to_all | solution.py:233
  451.1 73.5 %all-to-all-start.3 = ((bf16[8,128,2944]{2,1,0:T(8,128)(2,1)}), bf16[8,128,2944]{2,1,0:T(8,128)(2,1)}, u32[]{:S(2)}, u32[]{:S(2)}) async-start(bf16[8,128,2944]{2,1,0:T(8,128)(2,1)} %bitcast.158), calls=%async_computation.3 | async-start | bytes 12058624 | tf_op jit(solution)/shard_map/all_to_all | solution.py:253
  455.9 83.5 %reduce-scatter.17.cloned.1.call-start = ((), (), s32[]{:S(2)}) async-start(), calls=%async_computation.13 | async-start | bytes 1843200
  458.5 110.9 %reduce-scatter.19.cloned.1.call-start = ((), (), s32[]{:S(2)}) async-start(), calls=%async_computation.14 | async-start | bytes 1843200
  535.5 36.1 %copy-start.12 = (f32[2880]{0:T(1024)S(1)}, f32[2880]{0:T(1024)}, u32[]{:S(2)}) copy-start(f32[2880]{0:T(1024)} %param.40) | copy-start | bytes 34564
  535.5 46.2 %copy-start.3 = (bf16[192,720]{1,0:T(8,128)(2,1)S(1)}, bf16[192,720]{1,0:T(8,128)(2,1)}, u32[]{:S(2)}) copy-start(bf16[192,720]{1,0:T(8,128)(2,1)} %fusion.63) | copy-start | bytes 829444
  535.6 46.2 %copy-start.5 = (bf16[192,720]{1,0:T(8,128)(2,1)S(1)}, bf16[192,720]{1,0:T(8,128)(2,1)}, u32[]{:S(2)}) copy-start(bf16[192,720]{1,0:T(8,128)(2,1)} %fusion.62) | copy-start | bytes 829444
  570.5 0.7 copy-start.4
  581.7 8.7 %copy-start.1 = (bf16[512,2880]{0,1:T(8,128)(2,1)S(1)}, bf16[512,2880]{0,1:T(8,128)(2,1)}, u32[]{:S(2)}) copy-start(bf16[512,2880]{0,1:T(8,128)(2,1)} %param.31) | copy-start | bytes 8847364
Sparse Core Ops, SparseCore 0:
  9.6 50.7 all-gather.6
  87.2 38.2 reduce-scatter.12
  128.8 29.5 all-gather.8
  174.3 38.9 reduce-scatter.14
  274.9 29.9 all-gather.10
  458.7 33.2 reduce-scatter.16
  538.3 31.0 reduce-scatter.18

commit v7 on v6

--- a/solution.py
+++ b/solution.py
@@ -200,8 +200,6 @@
     for h in range(halves):
         lo = h * half_tokens
         joined_h = reduce_rows(lo, half_tokens)
-        if held is not None:
-            joined_h, held = lax.optimization_barrier((joined_h, held))
         resid_h, pack_h = resid_rows(joined_h, lo, half_tokens)
         reduced_parts.append(resid_h)
         column_h = lax.all_gather(resid_h, "dp", axis=1, tiled=True)

time: 602 us -> 567 us (0.942)
  waiting for transfers between devices: 379 us -> 346 us
  starting transfers between devices: 29.3 us -> 19.7 us
    all_to_all x2, waiting for transfers between devices: 130 us -> 41.6 us  [shards(): lax.all_to_all(outgoing, 'expert', split_axis=0, concat_axis=0, tiled=True)]
    unnamed x11, waiting for transfers between devices: 67.1 us -> 108 us
    all_to_all x2, waiting for transfers between devices: 88.3 us -> 104 us  [shards(): lax.all_to_all(shares_out, 'expert', split_axis=0, concat_axis=0, tiled=T...]
    all_to_all x2, starting transfers between devices: 19.1 us -> 9.45 us  [shards(): lax.all_to_all(outgoing, 'expert', split_axis=0, concat_axis=0, tiled=True)]
    unnamed x43 -> x46, local copies, waits for them, and re-layouts: 16.1 us -> 16.6 us
  transfers between devices with their start and end apart: 11 -> 11, of which waited for: 9 -> 9; matrix products, arithmetic and copies ran while one was open for 15% -> 19% of each run, Pallas kernels for 0% -> 0%
where the time goes in v7:
time: 567 us; the launch traced here: 557 us
  waiting for transfers between devices  346 us (61%)
  matrix products  97.7 us (17%)
  local copies, waits for them, and re-layouts  50.8 us (9%)
  starting transfers between devices  19.7 us (3%)
  other arithmetic  18.9 us (3%)
  between operations  15.2 us (3%)
  blocking collectives  9.22 us (2%)
    unnamed x11, waiting for transfers between devices  108 us
    all_to_all x2, waiting for transfers between devices, shards(): lax.all_to_all(shares_out, 'expert', split_axis=0, concat_axis=0, tiled=T...  104 us
    all_gather x1, waiting for transfers between devices, shards(): gathered_rows = lax.all_gather(hidden, 'dp', axis=1, tiled=True)  46.6 us
    all_gather x2, waiting for transfers between devices, shards(): column_h = lax.all_gather(resid_h, 'dp', axis=1, tiled=True)  45 us
    all_to_all x2, waiting for transfers between devices, shards(): lax.all_to_all(outgoing, 'expert', split_axis=0, concat_axis=0, tiled=True)  41.6 us
    dot_general x2, matrix products, shards(): jnp.dot(activated, down_weight, preferred_element_type=jnp.float32)  33.6 us
    dot_general x2, matrix products, shards(): up_part = jnp.dot(rows_in, up_weight, preferred_element_type=jnp.float32)  20.7 us
    unnamed x46, local copies, waits for them, and re-layouts  16.6 us
  transfers between devices with their start and end apart: 11, of which 9 were waited for; matrix products, arithmetic and copies ran while one was open for 19% of the time, Pallas kernels for 0%

profile of v7, /device:TPU:0, one launch (start us, length us, event | category | flops | bytes accessed | tf_op | source)
XLA Modules:
  0.0 557.2 jit_solution(7392613321738211520)
XLA Ops:
  8.0 0.8 exp.21
  8.7 0.7 reduce.3
  9.4 0.8 compare_reduce_fusion
  12.5 0.7 select_reduce_fusion.1
  13.7 46.6 %all-gather.7.cloned.1.call-done = bf16[384,2880]{0,1:T(8,128)(2,1)} async-done(((bf16[384,720]{0,1:T(8,128)(2,1)}), bf16[384,2880]{0,1:T(8,128)(2,1)}) %all-gather.7.cloned.1.call-update) | async-done | bytes 2211856 | tf_op jit(solution)/shard_map/all_gather | solution.py:103
  60.4 2.2 fusion.12
  62.6 5.9 %fusion.22 = f32[384,640]{1,0:T(8,128)} fusion(bf16[2880,1,640]{2,0,1:T(8,128)(2,1)} %param.29, bf16[384,2880]{0,1:T(8,128)(2,1)} %all-gather.7.cloned.1.call-done, f32[2880]{0:T(1024)S(1)} %copy-done.14, f32[384]{0:T(512)S(1)} %add_rsqrt_fusion), kind=kOutput, calls=%fused_computation.37 | convolution fusion | flops 1420001280 | bytes 6894336 | tf_op jit(solution)/shard_map/dot_general | solution.py:108
  68.5 4.8 fusion.56
  73.3 2.5 copy.64
  75.8 0.9 slice_bitcast_fusion.1
  76.7 1.2 slice_bitcast_fusion
  78.3 1.3 fusion.19
  79.6 2.2 fusion.59
  82.4 1.7 convolution_convert_fusion.4
  84.4 2.9 fusion.136
  88.1 37.7 %reduce-scatter.13.cloned.1.call-done = bf16[896,192]{1,0:T(8,128)(2,1)} async-done(((bf16[3584,192]{1,0:T(8,128)(2,1)}), bf16[896,192]{1,0:T(8,128)(2,1)}) %reduce-scatter.13.cloned.1.call-update) | async-done | bytes 344080
  125.8 0.8 slice.178
  126.6 1.0 slice.176
  127.9 1.0 fusion.63
  128.9 0.8 fusion.138
  130.1 1.7 reduce-window.29
  132.7 3.4 scatter_custom_fusion.1
  136.1 22.6 %all-gather.11.cloned.1.call-done = bf16[4,720,192]{1,2,0:T(8,128)(2,1)} async-done(((bf16[1,720,192]{1,2,0:T(8,128)(2,1)}), bf16[4,720,192]{1,2,0:T(8,128)(2,1)}) %all-gather.11.cloned.1.call-update) | async-done | bytes 1105936 | tf_op jit(solution)/shard_map/all_gather | solution.py:205
  158.7 2.2 copy.75
  160.8 1.0 reshape.554
  162.5 4.5 convolution_convert_fusion.1
  166.9 4.7 all-to-all-start
  172.5 41.0 %reduce-scatter.15.cloned.1.call-done = bf16[896,192]{1,0:T(8,128)(2,1)} async-done(((bf16[3584,192]{1,0:T(8,128)(2,1)}), bf16[896,192]{1,0:T(8,128)(2,1)}) %reduce-scatter.15.cloned.1.call-update) | async-done | bytes 344080
  213.5 0.8 slice.182
  214.3 1.0 slice.180
  215.6 1.0 fusion.62
  216.6 0.8 fusion.139
  217.8 1.7 reduce-window.25
  220.3 3.6 scatter_custom_fusion
  223.9 22.4 %all-gather.9.cloned.1.call-done = bf16[4,720,192]{1,2,0:T(8,128)(2,1)} async-done(((bf16[1,720,192]{1,2,0:T(8,128)(2,1)}), bf16[4,720,192]{1,2,0:T(8,128)(2,1)}) %all-gather.9.cloned.1.call-update) | async-done | bytes 1105936 | tf_op jit(solution)/shard_map/all_gather | solution.py:205
  246.4 3.2 copy.72
  249.6 2.7 reshape.552
  253.0 4.4 convolution_convert_fusion
  257.4 4.7 all-to-all-start.1
  262.1 10.4 %fusion.4 = f32[1024,720]{0,1:T(8,128)} fusion(bf16[1024,2944]{1,0:T(8,128)(2,1)} %bitcast.45, bf16[1,2880,720]{1,2,0:T(8,128)(2,1)} %param.38), kind=kOutput, calls=%fused_computation.16 | convolution fusion | flops 4246732800 | bytes 13125632 | tf_op jit(solution)/shard_map/dot_general | solution.py:238
  272.5 16.8 %convolution_convert_fusion.2 = bf16[1024,2944]{1,0:T(8,128)(2,1)} fusion(bf16[720,2880]{1,0:T(8,128)(2,1)} %bitcast.183, f32[1024,720]{0,1:T(8,128)} %fusion.4, bf16[1,2880,720]{1,2,0:T(8,128)(2,1)} %param.37, bf16[1024,2944]{1,0:T(8,128)(2,1)} %bitcast.45), kind=kOutput, calls=%fused_computation.12 | convolution fusion | flops 8596750336 | bytes 23302144 | tf_op jit(solution)/shard_map/dot_general | solution.py:243
  289.3 41.6 %all-to-all-done.1 = bf16[8,128,2944]{2,1,0:T(8,128)(2,1)} async-done(((bf16[8,128,2944]{2,1,0:T(8,128)(2,1)}), bf16[8,128,2944]{2,1,0:T(8,128)(2,1)}, u32[]{:S(2)}, u32[]{:S(2)}) %all-to-all-start.1) | async-done | bytes 6029344 | tf_op jit(solution)/shard_map/all_to_all | solution.py:231
  330.9 5.0 all-to-all-start.2
  336.5 10.4 %fusion.8 = f32[1024,720]{0,1:T(8,128)} fusion(bf16[1024,2944]{1,0:T(8,128)(2,1)} %bitcast.40, bf16[1,2880,720]{1,2,0:T(8,128)(2,1)} %param.38), kind=kOutput, calls=%fused_computation.20 | convolution fusion | flops 4246732800 | bytes 13125632 | tf_op jit(solution)/shard_map/dot_general | solution.py:238
  346.8 16.8 %convolution_convert_fusion.3 = bf16[1024,2944]{1,0:T(8,128)(2,1)} fusion(bf16[720,2880]{1,0:T(8,128)(2,1)} %bitcast.184, f32[1024,720]{0,1:T(8,128)} %fusion.8, bf16[1,2880,720]{1,2,0:T(8,128)(2,1)} %param.37, bf16[1024,2944]{1,0:T(8,128)(2,1)} %bitcast.40), kind=kOutput, calls=%fused_computation.13 | convolution fusion | flops 8596750336 | bytes 23302144 | tf_op jit(solution)/shard_map/dot_general | solution.py:243
  363.7 41.1 %all-to-all-done.2 = bf16[8,128,2944]{2,1,0:T(8,128)(2,1)} async-done(((bf16[8,128,2944]{2,1,0:T(8,128)(2,1)}), bf16[8,128,2944]{2,1,0:T(8,128)(2,1)}, u32[]{:S(2)}, u32[]{:S(2)}) %all-to-all-start.2) | async-done | bytes 6029344 | tf_op jit(solution)/shard_map/all_to_all | solution.py:251
  404.8 5.8 %fusion.140 = (bf16[192,2880]{1,0:T(8,128)(2,1)}, f32[192,2880]{1,0:T(8,128)}) fusion(bf16[192,1024]{1,0:T(8,128)(2,1)S(1)} %fusion.51, bf16[1024,2944]{1,0:T(8,128)(2,1)} %bitcast.47), kind=kOutput, calls=%fused_computation.218 | convolution fusion | flops 1133015040 | bytes 9740288 | tf_op jit(solution)/shard_map/dot_general | solution.py:261
  410.6 4.7 all-to-all-start.3
  415.4 2.5 copy.88
  418.6 2.2 gather_fusion
  420.9 63.2 %all-to-all-done.3 = bf16[8,128,2944]{2,1,0:T(8,128)(2,1)} async-done(((bf16[8,128,2944]{2,1,0:T(8,128)(2,1)}), bf16[8,128,2944]{2,1,0:T(8,128)(2,1)}, u32[]{:S(2)}, u32[]{:S(2)}) %all-to-all-start.3) | async-done | bytes 6029344 | tf_op jit(solution)/shard_map/all_to_all | solution.py:251
  484.1 6.0 %fusion.141 = (bf16[192,2880]{1,0:T(8,128)(2,1)}, f32[192,2880]{1,0:T(8,128)}) fusion(bf16[192,1024]{1,0:T(8,128)(2,1)S(1)} %fusion.50, bf16[1024,2944]{1,0:T(8,128)(2,1)} %bitcast.48), kind=kOutput, calls=%fused_computation.219 | convolution fusion | flops 1133015040 | bytes 9740288 | tf_op jit(solution)/shard_map/dot_general | solution.py:261
  490.1 2.2 gather_fusion.1
  492.7 2.4 pad_maximum_fusion.1
  495.1 2.6 copy.90
  498.8 1.9 copy.89
  500.7 28.2 %reduce-scatter.19.cloned.1.call-done = bf16[720,208]{1,0:T(8,128)(2,1)} async-done(((bf16[2880,208]{1,0:T(8,128)(2,1)}), bf16[720,208]{1,0:T(8,128)(2,1)}) %reduce-scatter.19.cloned.1.call-update) | async-done | bytes 299536
  528.9 1.1 copy.91
  530.0 0.7 copy-done.5
  531.2 9.2 %all-gather.2 = bf16[8,4,2880]{2,1,0:T(4,128)(2,1)S(1)} all-gather(bf16[1,4,2880]{2,1,0:T(4,128)(2,1)S(1)} %fusion.108), channel_id=1, replica_groups=mesh['dp'=4,'expert'=8] {'expert'}, dimensions={0}, use_global_device_ids=true | all-gather | bytes 207360 | tf_op jit(solution)/shard_map/all_gather | solution.py:290
  540.4 0.8 reshape.556
  541.2 2.2 add_convert_fusion
  543.3 2.1 copy.80
  545.4 4.5 fusion.142
  (129 shorter events, 13.7 us)
Async XLA Ops:
  7.2 75.2 %copy-start = (bf16[512,2880]{0,1:T(8,128)(2,1)S(1)}, bf16[512,2880]{0,1:T(8,128)(2,1)}, u32[]{:S(2)}) copy-start(bf16[512,2880]{0,1:T(8,128)(2,1)} %param.31) | copy-start | bytes 8847364
  7.2 55.4 %copy-start.14 = (f32[2880]{0:T(1024)S(1)}, f32[2880]{0:T(1024)}, u32[]{:S(2)}) copy-start(f32[2880]{0:T(1024)} %param.28) | copy-start | bytes 34564
  7.2 53.2 %all-gather.7.cloned.1.call-start = ((), (), s32[]{:S(2)}) async-start(), calls=%async_computation.8 | async-start | bytes 2764800 | tf_op jit(solution)/shard_map/all_gather | solution.py:103
  7.9 117.9 %reduce-scatter.13.cloned.1.call-start = ((), (), s32[]{:S(2)}) async-start(), calls=%async_computation.11 | async-start | bytes 2293760
  12.4 0.9 copy-start.8
  62.6 5.9 %copy-start.13 = (bf16[128,1,640]{2,0,1:T(8,128)(2,1)S(1)}, bf16[128,1,640]{2,0,1:T(8,128)(2,1)}, u32[]{:S(2)}) copy-start(bf16[128,1,640]{2,0,1:T(8,128)(2,1)} %param.33) | copy-start | bytes 491524
  79.6 2.3 copy-start.10
  82.3 1.7 copy-start.9
  84.4 3.2 copy-start.2
  87.4 40.6 %copy-start.6 = (bf16[128,720]{0,1:T(8,128)(2,1)S(1)}, bf16[128,720]{0,1:T(8,128)(2,1)}, u32[]{:S(2)}) copy-start(bf16[128,720]{0,1:T(8,128)(2,1)} %param.35) | copy-start | bytes 552964
  87.4 71.3 %all-gather.11.cloned.1.call-start = ((), (), s32[]{:S(2)}) async-start(), calls=%async_computation.10 | async-start | bytes 1474560 | tf_op jit(solution)/shard_map/all_gather | solution.py:205
  132.5 29.6 %copy-start.11 = (f32[2880]{0:T(1024)S(1)}, f32[2880]{0:T(1024)}, u32[]{:S(2)}) copy-start(f32[2880]{0:T(1024)} %param.36) | copy-start | bytes 34564
  166.9 85.3 %all-to-all-start = ((bf16[8,128,2944]{2,1,0:T(8,128)(2,1)}), bf16[8,128,2944]{2,1,0:T(8,128)(2,1)}, u32[]{:S(2)}, u32[]{:S(2)}) async-start(bf16[8,128,2944]{2,1,0:T(8,128)(2,1)} %bitcast.149), calls=%async_computation | async-start | bytes 12058624 | tf_op jit(solution)/shard_map/all_to_all | solution.py:231
  171.7 43.9 %copy-start.7 = (bf16[128,720]{0,1:T(8,128)(2,1)S(1)}, bf16[128,720]{0,1:T(8,128)(2,1)}, u32[]{:S(2)}) copy-start(bf16[128,720]{0,1:T(8,128)(2,1)} %param.35) | copy-start | bytes 552964
  171.7 41.8 %reduce-scatter.15.cloned.1.call-start = ((), (), s32[]{:S(2)}) async-start(), calls=%async_computation.12 | async-start | bytes 2293760
  172.3 74.1 %all-gather.9.cloned.1.call-start = ((), (), s32[]{:S(2)}) async-start(), calls=%async_computation.9 | async-start | bytes 1474560 | tf_op jit(solution)/shard_map/all_gather | solution.py:205
  257.4 73.5 %all-to-all-start.1 = ((bf16[8,128,2944]{2,1,0:T(8,128)(2,1)}), bf16[8,128,2944]{2,1,0:T(8,128)(2,1)}, u32[]{:S(2)}, u32[]{:S(2)}) async-start(bf16[8,128,2944]{2,1,0:T(8,128)(2,1)} %bitcast.150), calls=%async_computation.1 | async-start | bytes 12058624 | tf_op jit(solution)/shard_map/all_to_all | solution.py:231
  330.9 73.8 %all-to-all-start.2 = ((bf16[8,128,2944]{2,1,0:T(8,128)(2,1)}), bf16[8,128,2944]{2,1,0:T(8,128)(2,1)}, u32[]{:S(2)}, u32[]{:S(2)}) async-start(bf16[8,128,2944]{2,1,0:T(8,128)(2,1)} %bitcast.158), calls=%async_computation.2 | async-start | bytes 12058624 | tf_op jit(solution)/shard_map/all_to_all | solution.py:251
  410.6 73.5 %all-to-all-start.3 = ((bf16[8,128,2944]{2,1,0:T(8,128)(2,1)}), bf16[8,128,2944]{2,1,0:T(8,128)(2,1)}, u32[]{:S(2)}, u32[]{:S(2)}) async-start(bf16[8,128,2944]{2,1,0:T(8,128)(2,1)} %bitcast.157), calls=%async_computation.3 | async-start | bytes 12058624 | tf_op jit(solution)/shard_map/all_to_all | solution.py:251
  415.3 83.5 %reduce-scatter.17.cloned.1.call-start = ((), (), s32[]{:S(2)}) async-start(), calls=%async_computation.13 | async-start | bytes 1843200
  417.9 111.0 %reduce-scatter.19.cloned.1.call-start = ((), (), s32[]{:S(2)}) async-start(), calls=%async_computation.14 | async-start | bytes 1843200
  495.0 36.1 %copy-start.12 = (f32[2880]{0:T(1024)S(1)}, f32[2880]{0:T(1024)}, u32[]{:S(2)}) copy-start(f32[2880]{0:T(1024)} %param.40) | copy-start | bytes 34564
  495.0 46.1 %copy-start.3 = (bf16[192,720]{1,0:T(8,128)(2,1)S(1)}, bf16[192,720]{1,0:T(8,128)(2,1)}, u32[]{:S(2)}) copy-start(bf16[192,720]{1,0:T(8,128)(2,1)} %fusion.63) | copy-start | bytes 829444
  495.0 46.1 %copy-start.4 = (bf16[192,720]{1,0:T(8,128)(2,1)S(1)}, bf16[192,720]{1,0:T(8,128)(2,1)}, u32[]{:S(2)}) copy-start(bf16[192,720]{1,0:T(8,128)(2,1)} %fusion.62) | copy-start | bytes 829444
  530.0 0.7 copy-start.5
  541.2 8.7 %copy-start.1 = (bf16[512,2880]{0,1:T(8,128)(2,1)S(1)}, bf16[512,2880]{0,1:T(8,128)(2,1)}, u32[]{:S(2)}) copy-start(bf16[512,2880]{0,1:T(8,128)(2,1)} %param.31) | copy-start | bytes 8847364
Sparse Core Ops, SparseCore 0:
  9.6 50.7 all-gather.6
  87.5 38.2 reduce-scatter.12
  129.0 29.5 all-gather.10
  174.5 38.9 reduce-scatter.14
  216.7 29.5 all-gather.8
  418.2 33.2 reduce-scatter.16
  497.8 31.0 reduce-scatter.18

commit v8 on v7

--- a/solution.py
+++ b/solution.py
@@ -183,7 +183,7 @@
     gate_weight = expert_gate_weight[0]
     up_weight = expert_up_weight[0]
     down_weight = jnp.pad(expert_down_weight[0], ((0, 0), (0, lane_pad)))
-    halves = 2 if groups % 2 == 0 else 1
+    halves = groups
     half_tokens = col_tokens // halves
     half_capacity = (groups // halves) * capacity
     counter = jnp.arange(col_tokens, dtype=jnp.int32)
@@ -229,10 +229,7 @@
             .reshape(experts, half_capacity, wide)
         )
         arrived = lax.all_to_all(outgoing, "expert", split_axis=0, concat_axis=0, tiled=True)
-        if h == 0:
-            held = arrived
-        else:
-            arrived = lax.optimization_barrier((arrived, held))[0]
+        held = arrived
         rows_in = arrived.reshape(-1, wide)[:, :width]
         gate_part = jnp.dot(rows_in, gate_weight, preferred_element_type=jnp.float32)
         up_part = jnp.dot(rows_in, up_weight, preferred_element_type=jnp.float32)

time: 567 us -> 604 us (1.065)
  waiting for transfers between devices: 346 us -> 219 us
  blocking collectives: 9.22 us -> 82.1 us
  local copies, waits for them, and re-layouts: 50.8 us -> 96.9 us
  other arithmetic: 18.9 us -> 33.8 us
  starting transfers between devices: 19.7 us -> 34.2 us
  matrix products: 97.7 us -> 111 us
    all_gather x0 -> x4, blocking collectives: none -> 72.8 us  [shards(): column_h = lax.all_gather(resid_h, 'dp', axis=1, tiled=True)]
    all_to_all x2 -> x4, waiting for transfers between devices: 104 us -> 41.4 us  [shards(): lax.all_to_all(shares_out, 'expert', split_axis=0, concat_axis=0, tiled=T...]
    all_gather x2 -> x0, waiting for transfers between devices: 45 us -> none  [shards(): column_h = lax.all_gather(resid_h, 'dp', axis=1, tiled=True)]
    unnamed x11 -> x17, waiting for transfers between devices: 108 us -> 69.3 us
    all_to_all x2 -> x4, waiting for transfers between devices: 41.6 us -> 61.5 us  [shards(): lax.all_to_all(outgoing, 'expert', split_axis=0, concat_axis=0, tiled=True)]
    unnamed x46 -> x92, local copies, waits for them, and re-layouts: 16.6 us -> 31.4 us
    dot_general x2 -> x4, matrix products: 33.6 us -> 45.3 us  [shards(): jnp.dot(activated, down_weight, preferred_element_type=jnp.float32)]
    all_to_all x2 -> x4, starting transfers between devices: 9.45 us -> 18.2 us  [shards(): lax.all_to_all(outgoing, 'expert', split_axis=0, concat_axis=0, tiled=True)]
  transfers between devices with their start and end apart: 11 -> 17, of which waited for: 9 -> 10; matrix products, arithmetic and copies ran while one was open for 19% -> 34% of each run, Pallas kernels for 0% -> 0%
where the time goes in v8:
time: 604 us; the launch traced here: 592 us
  waiting for transfers between devices  219 us (36%)
  matrix products  111 us (18%)
  local copies, waits for them, and re-layouts  96.9 us (16%)
  blocking collectives  82.1 us (14%)
  starting transfers between devices  34.2 us (6%)
  other arithmetic  33.8 us (6%)
  between operations  15.2 us (3%)
    all_gather x4, blocking collectives, shards(): column_h = lax.all_gather(resid_h, 'dp', axis=1, tiled=True)  72.8 us
    unnamed x17, waiting for transfers between devices  69.3 us
    all_to_all x4, waiting for transfers between devices, shards(): lax.all_to_all(outgoing, 'expert', split_axis=0, concat_axis=0, tiled=True)  61.5 us
    all_gather x1, waiting for transfers between devices, shards(): gathered_rows = lax.all_gather(hidden, 'dp', axis=1, tiled=True)  46.6 us
    dot_general x4, matrix products, shards(): jnp.dot(activated, down_weight, preferred_element_type=jnp.float32)  45.3 us
    all_to_all x4, waiting for transfers between devices, shards(): lax.all_to_all(shares_out, 'expert', split_axis=0, concat_axis=0, tiled=T...  41.4 us
    unnamed x92, local copies, waits for them, and re-layouts  31.4 us
    dot_general x4, matrix products, shards(): jnp.dot(rows_in, gate_weight, preferred_element_type=jnp.float32)  24.7 us
  transfers between devices with their start and end apart: 17, of which 10 were waited for; matrix products, arithmetic and copies ran while one was open for 34% of the time, Pallas kernels for 0%

profile of v8, /device:TPU:0, one launch (start us, length us, event | category | flops | bytes accessed | tf_op | source)
XLA Modules:
  0.0 592.3 jit_solution(989438346307177853)
XLA Ops:
  13.7 46.6 %all-gather.7.cloned.1.call-done = bf16[384,2880]{0,1:T(8,128)(2,1)} async-done(((bf16[384,720]{0,1:T(8,128)(2,1)}), bf16[384,2880]{0,1:T(8,128)(2,1)}) %all-gather.7.cloned.1.call-update) | async-done | bytes 2211856 | tf_op jit(solution)/shard_map/all_gather | solution.py:103
  60.4 2.2 fusion
  62.6 5.9 %fusion.20 = f32[384,640]{1,0:T(8,128)} fusion(bf16[2880,1,640]{2,0,1:T(8,128)(2,1)} %param.29, bf16[384,2880]{0,1:T(8,128)(2,1)} %all-gather.7.cloned.1.call-done, f32[2880]{0:T(1024)S(1)} %copy-done.30, f32[384]{0:T(512)S(1)} %add_rsqrt_fusion), kind=kOutput, calls=%fused_computation.45 | convolution fusion | flops 1420001280 | bytes 6894336 | tf_op jit(solution)/shard_map/dot_general | solution.py:108
  68.5 4.8 fusion.60
  73.3 2.5 copy.68
  79.6 2.3 fusion.61
  84.4 2.9 fusion.216
  88.2 23.3 %reduce-scatter.25.cloned.1.call-done = bf16[896,96]{1,0:T(8,128)(2,1)} async-done(((bf16[3584,96]{1,0:T(8,128)(2,1)}), bf16[896,96]{1,0:T(8,128)(2,1)}) %reduce-scatter.25.cloned.1.call-update) | async-done | bytes 172048
  117.5 23.3 %all-gather.1 = bf16[4,720,96]{1,2,0:T(8,128)(2,1)S(1)} all-gather(bf16[1,720,96]{1,2,0:T(8,128)(2,1)S(1)} %bitcast.251), channel_id=1, replica_groups=mesh['dp'=4,'expert'=8] {'dp'}, dimensions={0}, use_global_device_ids=true | all-gather | bytes 691200 | tf_op jit(solution)/shard_map/all_gather | solution.py:205
  141.9 2.9 scatter_custom_fusion.1
  145.0 2.6 convolution_convert_fusion.7
  147.6 4.4 all-to-all-start
  158.0 2.9 scatter_custom_fusion
  161.1 16.4 %all-gather = bf16[4,720,96]{1,2,0:T(8,128)(2,1)S(1)} all-gather(bf16[1,720,96]{1,2,0:T(8,128)(2,1)S(1)} %bitcast.252), channel_id=1, replica_groups=mesh['dp'=4,'expert'=8] {'dp'}, dimensions={0}, use_global_device_ids=true | all-gather | bytes 691200 | tf_op jit(solution)/shard_map/all_gather | solution.py:205
  178.5 10.1 %all-to-all-done = bf16[8,64,2944]{2,1,0:T(8,128)(2,1)} async-done(((bf16[8,64,2944]{2,1,0:T(8,128)(2,1)}), bf16[8,64,2944]{2,1,0:T(8,128)(2,1)}, u32[]{:S(2)}, u32[]{:S(2)}) %all-to-all-start) | async-done | bytes 3014688 | tf_op jit(solution)/shard_map/all_to_all | solution.py:231
  189.0 2.6 convolution_convert_fusion.6
  191.6 4.4 all-to-all-start.1
  196.7 5.6 fusion.15
  202.3 11.3 %convolution_convert_fusion.4 = bf16[512,2944]{1,0:T(8,128)(2,1)} fusion(bf16[720,2880]{1,0:T(8,128)(2,1)} %bitcast.279, f32[512,720]{0,1:T(8,128)S(1)} %fusion.15, bf16[1,2880,720]{1,2,0:T(8,128)(2,1)} %param.38, bf16[512,2944]{1,0:T(8,128)(2,1)} %bitcast.45), kind=kOutput, calls=%fused_computation.20 | convolution fusion | flops 4298375168 | bytes 15798272 | tf_op jit(solution)/shard_map/dot_general | solution.py:240
  213.5 19.0 %all-to-all-done.1 = bf16[8,64,2944]{2,1,0:T(8,128)(2,1)} async-done(((bf16[8,64,2944]{2,1,0:T(8,128)(2,1)}), bf16[8,64,2944]{2,1,0:T(8,128)(2,1)}, u32[]{:S(2)}, u32[]{:S(2)}) %all-to-all-start.1) | async-done | bytes 3014688 | tf_op jit(solution)/shard_map/all_to_all | solution.py:231
  232.5 3.6 all-to-all-start.2
  249.3 2.5 reduce-window.45
  260.5 3.1 scatter_custom_fusion.2
  265.4 16.4 %all-gather.2 = bf16[4,720,96]{1,2,0:T(8,128)(2,1)S(1)} all-gather(bf16[1,720,96]{1,2,0:T(8,128)(2,1)S(1)} %bitcast.253), channel_id=1, replica_groups=mesh['dp'=4,'expert'=8] {'dp'}, dimensions={0}, use_global_device_ids=true | all-gather | bytes 691200 | tf_op jit(solution)/shard_map/all_gather | solution.py:205
  283.1 2.5 reshape.778
  288.1 2.6 convolution_convert_fusion.3
  290.7 4.6 all-to-all-start.3
  296.9 6.8 %fusion.17 = f32[512,720]{0,1:T(8,128)} fusion(bf16[1,2880,720]{1,2,0:T(8,128)(2,1)} %param.37, bf16[512,2944]{1,0:T(8,128)(2,1)} %bitcast.40), kind=kOutput, calls=%fused_computation.41 | convolution fusion | flops 2123366400 | bytes 8636416 | tf_op jit(solution)/shard_map/dot_general | solution.py:234
  303.7 1.8 fusion.222
  305.6 11.5 %convolution_convert_fusion.5 = bf16[512,2944]{1,0:T(8,128)(2,1)} fusion(bf16[720,2880]{1,0:T(8,128)(2,1)} %bitcast.280, f32[512,720]{0,1:T(8,128)} %fusion.17, bf16[1,2880,720]{1,2,0:T(8,128)(2,1)} %param.38, bf16[512,2944]{1,0:T(8,128)(2,1)} %bitcast.40), kind=kOutput, calls=%fused_computation.21 | convolution fusion | flops 4298375168 | bytes 15798272 | tf_op jit(solution)/shard_map/dot_general | solution.py:240
  317.1 14.7 %all-to-all-done.3 = bf16[8,64,2944]{2,1,0:T(8,128)(2,1)} async-done(((bf16[8,64,2944]{2,1,0:T(8,128)(2,1)}), bf16[8,64,2944]{2,1,0:T(8,128)(2,1)}, u32[]{:S(2)}, u32[]{:S(2)}) %all-to-all-start.3) | async-done | bytes 3014688 | tf_op jit(solution)/shard_map/all_to_all | solution.py:231
  331.8 3.6 all-to-all-start.4
  349.2 3.1 scatter_custom_fusion.3
  354.0 16.7 %all-gather.3 = bf16[4,720,96]{1,2,0:T(8,128)(2,1)S(1)} all-gather(bf16[1,720,96]{1,2,0:T(8,128)(2,1)S(1)} %bitcast.254), channel_id=1, replica_groups=mesh['dp'=4,'expert'=8] {'dp'}, dimensions={0}, use_global_device_ids=true | all-gather | bytes 691200 | tf_op jit(solution)/shard_map/all_gather | solution.py:205
  372.1 2.5 reshape.780
  377.1 2.6 convolution_convert_fusion.1
  379.7 4.8 all-to-all-start.5
  384.8 1.9 fusion.223
  386.7 5.6 fusion.13
  392.3 11.0 %convolution_convert_fusion.2 = bf16[512,2944]{1,0:T(8,128)(2,1)} fusion(bf16[720,2880]{1,0:T(8,128)(2,1)} %bitcast.281, f32[512,720]{0,1:T(8,128)S(1)} %fusion.13, bf16[1,2880,720]{1,2,0:T(8,128)(2,1)} %param.38, bf16[512,2944]{1,0:T(8,128)(2,1)} %bitcast.54), kind=kOutput, calls=%fused_computation.18 | convolution fusion | flops 4298375168 | bytes 15798272 | tf_op jit(solution)/shard_map/dot_general | solution.py:240
  403.3 17.7 %all-to-all-done.5 = bf16[8,64,2944]{2,1,0:T(8,128)(2,1)} async-done(((bf16[8,64,2944]{2,1,0:T(8,128)(2,1)}), bf16[8,64,2944]{2,1,0:T(8,128)(2,1)}, u32[]{:S(2)}, u32[]{:S(2)}) %all-to-all-start.5) | async-done | bytes 3014688 | tf_op jit(solution)/shard_map/all_to_all | solution.py:231
  421.0 3.6 all-to-all-start.6
  424.9 6.7 %fusion.11 = f32[512,720]{0,1:T(8,128)} fusion(bf16[1,2880,720]{1,2,0:T(8,128)(2,1)} %param.37, bf16[512,2944]{1,0:T(8,128)(2,1)} %bitcast.63), kind=kOutput, calls=%fused_computation.35 | convolution fusion | flops 2123366400 | bytes 8636416 | tf_op jit(solution)/shard_map/dot_general | solution.py:234
  431.7 11.5 %convolution_convert_fusion = bf16[512,2944]{1,0:T(8,128)(2,1)} fusion(bf16[720,2880]{1,0:T(8,128)(2,1)} %bitcast.282, f32[512,720]{0,1:T(8,128)} %fusion.11, bf16[1,2880,720]{1,2,0:T(8,128)(2,1)} %param.38, bf16[512,2944]{1,0:T(8,128)(2,1)} %bitcast.63), kind=kOutput, calls=%fused_computation.16 | convolution fusion | flops 4298375168 | bytes 15798272 | tf_op jit(solution)/shard_map/dot_general | solution.py:240
  443.1 17.9 %all-to-all-done.6 = bf16[8,64,2944]{2,1,0:T(8,128)(2,1)S(1)} async-done(((bf16[8,64,2944]{2,1,0:T(8,128)(2,1)}), bf16[8,64,2944]{2,1,0:T(8,128)(2,1)S(1)}, u32[]{:S(2)}, u32[]{:S(2)}) %all-to-all-start.6) | async-done | bytes 3014688 | tf_op jit(solution)/shard_map/all_to_all | solution.py:248
  461.1 1.8 fusion.224
  462.9 3.9 all-to-all-start.7
  466.9 2.2 copy.104
  469.2 2.2 copy.106
  471.9 1.8 gather_fusion
  473.8 1.8 gather_fusion.1
  475.6 2.2 copy.108
  477.8 1.8 gather_fusion.2
  479.8 23.4 %all-to-all-done.7 = bf16[8,64,2944]{2,1,0:T(8,128)(2,1)S(1)} async-done(((bf16[8,64,2944]{2,1,0:T(8,128)(2,1)}), bf16[8,64,2944]{2,1,0:T(8,128)(2,1)S(1)}, u32[]{:S(2)}, u32[]{:S(2)}) %all-to-all-start.7) | async-done | bytes 3014688 | tf_op jit(solution)/shard_map/all_to_all | solution.py:248
  503.2 1.8 fusion.225
  505.0 1.8 gather_fusion.3
  509.6 1.7 gather_fusion.4
  511.3 1.7 gather_fusion.5
  514.8 1.7 copy.105
  516.5 1.7 gather_fusion.7
  520.0 22.2 %reduce-scatter.37.cloned.1.call-done = bf16[720,96]{1,0:T(8,128)(2,1)} async-done(((bf16[2880,96]{1,0:T(8,128)(2,1)}), bf16[720,96]{1,0:T(8,128)(2,1)}) %reduce-scatter.37.cloned.1.call-update) | async-done | bytes 138256
  543.9 22.7 %reduce-scatter.39.cloned.1.call-done = bf16[720,112]{1,0:T(8,128)(2,1)} async-done(((bf16[2880,112]{1,0:T(8,128)(2,1)}), bf16[720,112]{1,0:T(8,128)(2,1)}) %reduce-scatter.39.cloned.1.call-update) | async-done | bytes 161296
  568.2 9.3 %all-gather.4 = bf16[8,4,2880]{2,1,0:T(4,128)(2,1)S(1)} all-gather(bf16[1,4,2880]{2,1,0:T(4,128)(2,1)S(1)} %fusion.154), channel_id=1, replica_groups=mesh['dp'=4,'expert'=8] {'expert'}, dimensions={0}, use_global_device_ids=true | all-gather | bytes 207360 | tf_op jit(solution)/shard_map/all_gather | solution.py:287
  580.8 4.5 fusion.226
  (248 shorter events, 91.0 us)
Async XLA Ops:
  7.2 75.2 %copy-start = (bf16[512,2880]{0,1:T(8,128)(2,1)S(1)}, bf16[512,2880]{0,1:T(8,128)(2,1)}, u32[]{:S(2)}) copy-start(bf16[512,2880]{0,1:T(8,128)(2,1)} %param.31) | copy-start | bytes 8847364
  7.2 55.4 %copy-start.30 = (f32[2880]{0:T(1024)S(1)}, f32[2880]{0:T(1024)}, u32[]{:S(2)}) copy-start(f32[2880]{0:T(1024)} %param.28) | copy-start | bytes 34564
  7.2 53.2 %all-gather.7.cloned.1.call-start = ((), (), s32[]{:S(2)}) async-start(), calls=%async_computation.16 | async-start | bytes 2764800 | tf_op jit(solution)/shard_map/all_gather | solution.py:103
  7.9 103.6 %reduce-scatter.25.cloned.1.call-start = ((), (), s32[]{:S(2)}) async-start(), calls=%async_computation.17 | async-start | bytes 1146880
  9.4 59.1 %copy-start.20 = (s32[384]{0:T(512)}, s32[384]{0:T(512)S(1)}, u32[]{:S(2)}) copy-start(s32[384]{0:T(512)S(1)} %reduce.5) | copy-start | bytes 4612
  12.4 0.9 copy-start.17
  62.6 5.9 %copy-start.29 = (bf16[128,1,640]{2,0,1:T(8,128)(2,1)S(1)}, bf16[128,1,640]{2,0,1:T(8,128)(2,1)}, u32[]{:S(2)}) copy-start(bf16[128,1,640]{2,0,1:T(8,128)(2,1)} %param.33) | copy-start | bytes 491524
  79.6 2.3 copy-start.19
  82.4 1.7 copy-start.18
  84.4 3.2 copy-start.4
  87.4 29.9 %copy-start.5 = (bf16[128,720]{0,1:T(8,128)(2,1)S(1)}, bf16[128,720]{0,1:T(8,128)(2,1)}, u32[]{:S(2)}) copy-start(bf16[128,720]{0,1:T(8,128)(2,1)} %param.35) | copy-start | bytes 552964
  87.4 64.9 %reduce-scatter.27.cloned.1.call-start = ((), (), s32[]{:S(2)}) async-start(), calls=%async_computation.18 | async-start | bytes 1146880
  88.0 69.9 %copy-start.28 = (s32[384]{0:T(512)}, s32[384]{0:T(512)S(1)}, u32[]{:S(2)}) copy-start(s32[384]{0:T(512)S(1)} %add_select_fusion) | copy-start | bytes 4612
  88.2 72.7 %copy-start.16 = (pred[384,128]{1,0:T(32,128)(4,1)}, pred[384,128]{1,0:T(32,128)(4,1)S(1)}, u32[]{:S(2)}) copy-start(pred[384,128]{1,0:T(32,128)(4,1)S(1)} %broadcast_compare_fusion) | copy-start | bytes 147460
  88.2 56.6 %copy-start.11 = (f32[2880]{0:T(1024)S(1)}, f32[2880]{0:T(1024)}, u32[]{:S(2)}) copy-start(f32[2880]{0:T(1024)} %param.36) | copy-start | bytes 34564
  117.4 30.2 %copy-start.6 = (bf16[96,720]{1,0:T(8,128)(2,1)}, bf16[96,720]{1,0:T(8,128)(2,1)S(1)}, u32[]{:S(2)}) copy-start(bf16[96,720]{1,0:T(8,128)(2,1)S(1)} %fusion.68) | copy-start | bytes 414724
  141.7 6.0 %copy-start.2 = (bf16[2880,96]{0,1:T(8,128)(2,1)}, bf16[2880,96]{0,1:T(8,128)(2,1)S(1)}, u32[]{:S(2)}) copy-start(bf16[2880,96]{0,1:T(8,128)(2,1)S(1)} %reshape.776) | copy-start | bytes 1658884
  147.6 40.9 %all-to-all-start = ((bf16[8,64,2944]{2,1,0:T(8,128)(2,1)}), bf16[8,64,2944]{2,1,0:T(8,128)(2,1)}, u32[]{:S(2)}, u32[]{:S(2)}) async-start(bf16[8,64,2944]{2,1,0:T(8,128)(2,1)} %bitcast.38), calls=%async_computation | async-start | bytes 6029312 | tf_op jit(solution)/shard_map/all_to_all | solution.py:231
  161.1 30.5 %copy-start.7 = (bf16[96,720]{1,0:T(8,128)(2,1)}, bf16[96,720]{1,0:T(8,128)(2,1)S(1)}, u32[]{:S(2)}) copy-start(bf16[96,720]{1,0:T(8,128)(2,1)S(1)} %fusion.69) | copy-start | bytes 414724
  178.5 13.2 %copy-start.3 = (bf16[2880,96]{0,1:T(8,128)(2,1)}, bf16[2880,96]{0,1:T(8,128)(2,1)S(1)}, u32[]{:S(2)}) copy-start(bf16[2880,96]{0,1:T(8,128)(2,1)S(1)} %reshape.774) | copy-start | bytes 1658884
  191.6 40.9 %all-to-all-start.1 = ((bf16[8,64,2944]{2,1,0:T(8,128)(2,1)}), bf16[8,64,2944]{2,1,0:T(8,128)(2,1)}, u32[]{:S(2)}, u32[]{:S(2)}) async-start(bf16[8,64,2944]{2,1,0:T(8,128)(2,1)} %bitcast.39), calls=%async_computation.1 | async-start | bytes 6029312 | tf_op jit(solution)/shard_map/all_to_all | solution.py:231
  196.1 40.2 %reduce-scatter.29.cloned.1.call-start = ((), (), s32[]{:S(2)}) async-start(), calls=%async_computation.19 | async-start | bytes 1146880
  232.5 58.2 %all-to-all-start.2 = ((bf16[8,64,2944]{2,1,0:T(8,128)(2,1)}), bf16[8,64,2944]{2,1,0:T(8,128)(2,1)S(1)}, u32[]{:S(2)}, u32[]{:S(2)}) async-start(bf16[8,64,2944]{2,1,0:T(8,128)(2,1)} %bitcast.244), calls=%async_computation.2 | async-start | bytes 6029312 | tf_op jit(solution)/shard_map/all_to_all | solution.py:248
  258.9 27.9 %copy-start.12 = (f32[2880]{0:T(1024)S(1)}, f32[2880]{0:T(1024)}, u32[]{:S(2)}) copy-start(f32[2880]{0:T(1024)} %param.36) | copy-start | bytes 34564
  264.7 0.7 copy-start.8
  290.7 6.0 %copy-start.25 = (bf16[96,4]{0,1:T(4,128)(2,1)S(1)}, bf16[96,4]{0,1:T(4,128)(2,1)}, u32[]{:S(2)}) copy-start(bf16[96,4]{0,1:T(4,128)(2,1)} %get-tuple-element.50) | copy-start | bytes 2308
  290.7 41.1 %all-to-all-start.3 = ((bf16[8,64,2944]{2,1,0:T(8,128)(2,1)}), bf16[8,64,2944]{2,1,0:T(8,128)(2,1)}, u32[]{:S(2)}, u32[]{:S(2)}) async-start(bf16[8,64,2944]{2,1,0:T(8,128)(2,1)} %bitcast.222), calls=%async_computation.3 | async-start | bytes 6029312 | tf_op jit(solution)/shard_map/all_to_all | solution.py:231
  295.3 40.2 %reduce-scatter.31.cloned.1.call-start = ((), (), s32[]{:S(2)}) async-start(), calls=%async_computation.20 | async-start | bytes 1146880
  331.8 48.0 %all-to-all-start.4 = ((bf16[8,64,2944]{2,1,0:T(8,128)(2,1)}), bf16[8,64,2944]{2,1,0:T(8,128)(2,1)S(1)}, u32[]{:S(2)}, u32[]{:S(2)}) async-start(bf16[8,64,2944]{2,1,0:T(8,128)(2,1)} %bitcast.243), calls=%async_computation.4 | async-start | bytes 6029312 | tf_op jit(solution)/shard_map/all_to_all | solution.py:248
  344.2 31.6 %copy-start.13 = (f32[2880]{0:T(1024)S(1)}, f32[2880]{0:T(1024)}, u32[]{:S(2)}) copy-start(f32[2880]{0:T(1024)} %param.36) | copy-start | bytes 34564
  347.6 0.6 copy-start.22
  353.4 0.7 copy-start.9
  379.7 4.8 copy-start.14
  379.7 4.9 copy-start.24
  379.7 41.3 %all-to-all-start.5 = ((bf16[8,64,2944]{2,1,0:T(8,128)(2,1)}), bf16[8,64,2944]{2,1,0:T(8,128)(2,1)}, u32[]{:S(2)}, u32[]{:S(2)}) async-start(bf16[8,64,2944]{2,1,0:T(8,128)(2,1)} %bitcast.223), calls=%async_computation.5 | async-start | bytes 6029312 | tf_op jit(solution)/shard_map/all_to_all | solution.py:231
  403.3 21.4 %copy-start.15 = (s32[96,4]{1,0:T(8,128)S(1)}, s32[96,4]{1,0:T(8,128)}, u32[]{:S(2)}) copy-start(s32[96,4]{1,0:T(8,128)} %get-tuple-element.64) | copy-start | bytes 4612
  403.3 21.4 %copy-start.26 = (bf16[96,4]{0,1:T(4,128)(2,1)S(1)}, bf16[96,4]{0,1:T(4,128)(2,1)}, u32[]{:S(2)}) copy-start(bf16[96,4]{0,1:T(4,128)(2,1)} %get-tuple-element.54) | copy-start | bytes 2308
  421.0 40.1 %all-to-all-start.6 = ((bf16[8,64,2944]{2,1,0:T(8,128)(2,1)}), bf16[8,64,2944]{2,1,0:T(8,128)(2,1)S(1)}, u32[]{:S(2)}, u32[]{:S(2)}) async-start(bf16[8,64,2944]{2,1,0:T(8,128)(2,1)} %bitcast.245), calls=%async_computation.6 | async-start | bytes 6029312 | tf_op jit(solution)/shard_map/all_to_all | solution.py:248
  462.9 40.3 %all-to-all-start.7 = ((bf16[8,64,2944]{2,1,0:T(8,128)(2,1)}), bf16[8,64,2944]{2,1,0:T(8,128)(2,1)S(1)}, u32[]{:S(2)}, u32[]{:S(2)}) async-start(bf16[8,64,2944]{2,1,0:T(8,128)(2,1)} %bitcast.242), calls=%async_computation.7 | async-start | bytes 6029312 | tf_op jit(solution)/shard_map/all_to_all | solution.py:248
  466.8 4.7 copy-start.21
  466.8 4.9 copy-start.27
  466.8 48.0 %reduce-scatter.33.cloned.1.call-start = ((), (), s32[]{:S(2)}) async-start(), calls=%async_computation.21 | async-start | bytes 921600
  469.1 49.2 %reduce-scatter.35.cloned.1.call-start = ((), (), s32[]{:S(2)}) async-start(), calls=%async_computation.22 | async-start | bytes 921600
  471.4 70.8 %reduce-scatter.37.cloned.1.call-start = ((), (), s32[]{:S(2)}) async-start(), calls=%async_computation.23 | async-start | bytes 921600
  479.7 86.9 %reduce-scatter.39.cloned.1.call-start = ((), (), s32[]{:S(2)}) async-start(), calls=%async_computation.24 | async-start | bytes 921600
  507.3 60.8 %copy-start.23 = (f32[2880]{0:T(1024)S(1)}, f32[2880]{0:T(1024)}, u32[]{:S(2)}) copy-start(f32[2880]{0:T(1024)} %param.40) | copy-start | bytes 34564
  567.7 9.8 %copy-start.10 = (bf16[112,720]{1,0:T(8,128)(2,1)}, bf16[112,720]{1,0:T(8,128)(2,1)S(1)}, u32[]{:S(2)}) copy-start(bf16[112,720]{1,0:T(8,128)(2,1)S(1)} %copy.111) | copy-start | bytes 483844
  578.2 7.1 %copy-start.1 = (bf16[512,2880]{0,1:T(8,128)(2,1)S(1)}, bf16[512,2880]{0,1:T(8,128)(2,1)}, u32[]{:S(2)}) copy-start(bf16[512,2880]{0,1:T(8,128)(2,1)} %param.31) | copy-start | bytes 8847364
Sparse Core Ops, SparseCore 0:
  9.6 50.7 all-gather.6
  87.5 23.9 reduce-scatter.24
  113.8 32.9 reduce-scatter.26
  198.9 25.6 reduce-scatter.28
  298.1 25.9 reduce-scatter.30
  469.6 23.8 reduce-scatter.32
  495.8 22.0 reduce-scatter.34
  520.2 22.0 reduce-scatter.36
  544.5 22.0 reduce-scatter.38

commit v9 on v7

--- a/solution.py
+++ b/solution.py
@@ -53,14 +53,16 @@
     )
 
 
-def attend_heads(queries, key_heads, value_heads, segment_row, sink_row):
+def attend_heads(queries, key_heads, value_heads, segment_row, sink_row, offset):
     tokens_now, kv_now, group_now, head_dim = queries.shape
+    keys_now = key_heads.shape[0]
     scores = jnp.einsum(
         "tkgh,skh->kgts", queries, key_heads, preferred_element_type=jnp.float32
     ) * head_dim ** (-0.5)
-    counter = jnp.arange(tokens_now, dtype=jnp.int32)
-    allowed = (segment_row[:, None] == segment_row[None, :]) & (
-        counter[None, :] <= counter[:, None]
+    query_index = offset + jnp.arange(tokens_now, dtype=jnp.int32)
+    key_index = jnp.arange(keys_now, dtype=jnp.int32)
+    allowed = (segment_row[offset : offset + tokens_now, None] == segment_row[None, :keys_now]) & (
+        key_index[None, :] <= query_index[:, None]
     )
     weights = jnp.where(allowed[None, None], jnp.exp(scores), 0.0)
     totals = jnp.sum(weights, axis=-1, keepdims=True) + jnp.exp(sink_row).reshape(
@@ -130,7 +132,6 @@
     queries = queries.astype(jnp.bfloat16).reshape(col_tokens, kv_here, QUERY_GROUP, HEAD_SIZE)
     key_heads = rotate_heads(joined_projection[:, :, QUERY_GROUP], positions).astype(jnp.bfloat16)
     value_heads = joined_projection[:, :, QUERY_GROUP + 1].astype(jnp.bfloat16)
-    blended_hidden = attend_heads(queries, key_heads, value_heads, segment_row, sinks)
     share = col_tokens // groups
     quarter = hidden.shape[1]
     rank_total = output_down_maps.shape[1]
@@ -142,23 +143,39 @@
     pack_rows = lax.dynamic_update_slice_in_dim(
         jnp.zeros((col_tokens, pack_width), jnp.bfloat16), route_pack, position_dp * share, 0
     )
-    partial_out = jnp.dot(blended_hidden, attention_out_weight, preferred_element_type=jnp.float32)
-    low_local = jnp.dot(blended_hidden, output_down_maps, preferred_element_type=jnp.float32)
-    joined_send = jnp.concatenate(
-        [
-            partial_out.astype(jnp.bfloat16).reshape(col_tokens, groups, quarter),
-            jnp.broadcast_to(
-                low_local.astype(jnp.bfloat16)[:, None, :], (col_tokens, groups, rank_total)
-            ),
-            jnp.broadcast_to(pack_rows[:, None, :], (col_tokens, groups, pack_width)),
-        ],
-        axis=2,
-    ).reshape(col_tokens, -1)
+    halves = 2 if groups % 2 == 0 else 1
+    half_tokens = col_tokens // halves
+    joined_parts = []
+    for h in range(halves):
+        lo = h * half_tokens
+        hi = lo + half_tokens
+        blended_hidden = attend_heads(
+            queries[lo:hi], key_heads[:hi], value_heads[:hi], segment_row, sinks, lo
+        )
+        partial_out = jnp.dot(
+            blended_hidden, attention_out_weight, preferred_element_type=jnp.float32
+        )
+        low_local = jnp.dot(blended_hidden, output_down_maps, preferred_element_type=jnp.float32)
+        joined_parts.append(
+            jnp.concatenate(
+                [
+                    partial_out.astype(jnp.bfloat16).reshape(half_tokens, groups, quarter),
+                    jnp.broadcast_to(
+                        low_local.astype(jnp.bfloat16)[:, None, :],
+                        (half_tokens, groups, rank_total),
+                    ),
+                    jnp.broadcast_to(
+                        pack_rows[lo:hi, None, :], (half_tokens, groups, pack_width)
+                    ),
+                ],
+                axis=2,
+            ).reshape(half_tokens, -1)
+        )
     reduced_parts = []
 
     def reduce_rows(lo, rows):
         joined_back = lax.psum_scatter(
-            joined_send[lo : lo + rows], "dp", scatter_dimension=1, tiled=True
+            joined_parts[lo // rows], "dp", scatter_dimension=1, tiled=True
         )
         return joined_back
 
@@ -183,8 +200,6 @@
     gate_weight = expert_gate_weight[0]
     up_weight = expert_up_weight[0]
     down_weight = jnp.pad(expert_down_weight[0], ((0, 0), (0, lane_pad)))
-    halves = 2 if groups % 2 == 0 else 1
-    half_tokens = col_tokens // halves
     half_capacity = (groups // halves) * capacity
     counter = jnp.arange(col_tokens, dtype=jnp.int32)
     request_ids = jnp.arange(REQS, dtype=jnp.int32)

time: 567 us -> 585 us (1.032)
  local copies, waits for them, and re-layouts: 50.8 us -> 70.1 us
  waiting for transfers between devices: 346 us -> 331 us
  other arithmetic: 18.9 us -> 25.7 us
  matrix products: 97.7 us -> 104 us
    reshape x0 -> x2, local copies, waits for them, and re-layouts: none -> 7.5 us  [shards(): partial_out.astype(jnp.bfloat16).reshape(half_tokens, groups, quarter)]
    unnamed x46 -> x57, local copies, waits for them, and re-layouts: 16.6 us -> 24 us
    unnamed x11, waiting for transfers between devices: 108 us -> 101 us
    all_gather x2, waiting for transfers between devices: 45 us -> 38.2 us  [shards(): column_h = lax.all_gather(resid_h, 'dp', axis=1, tiled=True)]
  transfers between devices with their start and end apart: 11 -> 11, of which waited for: 9 -> 9; matrix products, arithmetic and copies ran while one was open for 19% -> 21% of each run, Pallas kernels for 0% -> 0%
where the time goes in v9:
time: 585 us; the launch traced here: 575 us
  waiting for transfers between devices  331 us (57%)
  matrix products  104 us (18%)
  local copies, waits for them, and re-layouts  70.1 us (12%)
  other arithmetic  25.7 us (4%)
  starting transfers between devices  20.1 us (3%)
  between operations  14.9 us (3%)
  blocking collectives  9.22 us (2%)
    all_to_all x2, waiting for transfers between devices, shards(): lax.all_to_all(shares_out, 'expert', split_axis=0, concat_axis=0, tiled=T...  105 us
    unnamed x11, waiting for transfers between devices  101 us
    all_gather x1, waiting for transfers between devices, shards(): gathered_rows = lax.all_gather(hidden, 'dp', axis=1, tiled=True)  45.1 us
    all_to_all x2, waiting for transfers between devices, shards(): lax.all_to_all(outgoing, 'expert', split_axis=0, concat_axis=0, tiled=True)  41.6 us
    all_gather x2, waiting for transfers between devices, shards(): column_h = lax.all_gather(resid_h, 'dp', axis=1, tiled=True)  38.2 us
    dot_general x2, matrix products, shards(): jnp.dot(activated, down_weight, preferred_element_type=jnp.float32)  33.6 us
    unnamed x57, local copies, waits for them, and re-layouts  24 us
    dot_general x2, matrix products, shards(): up_part = jnp.dot(rows_in, up_weight, preferred_element_type=jnp.float32)  20.7 us
  transfers between devices with their start and end apart: 11, of which 9 were waited for; matrix products, arithmetic and copies ran while one was open for 21% of the time, Pallas kernels for 0%

profile of v9, /device:TPU:0, one launch (start us, length us, event | category | flops | bytes accessed | tf_op | source)
XLA Modules:
  0.0 575.4 jit_solution(13821050495738963323)
XLA Ops:
  15.2 45.1 %all-gather.7.cloned.1.call-done = bf16[384,2880]{0,1:T(8,128)(2,1)} async-done(((bf16[384,720]{0,1:T(8,128)(2,1)}), bf16[384,2880]{0,1:T(8,128)(2,1)}) %all-gather.7.cloned.1.call-update) | async-done | bytes 2211856 | tf_op jit(solution)/shard_map/all_gather | solution.py:105
  60.4 2.2 fusion.12
  62.6 5.9 %fusion.21 = f32[384,640]{1,0:T(8,128)} fusion(bf16[2880,1,640]{2,0,1:T(8,128)(2,1)} %param.29, bf16[384,2880]{0,1:T(8,128)(2,1)} %all-gather.7.cloned.1.call-done, f32[2880]{0:T(1024)S(1)} %copy-done.18, f32[384]{0:T(512)S(1)} %add_rsqrt_fusion), kind=kOutput, calls=%fused_computation.35 | convolution fusion | flops 1420001280 | bytes 6894336 | tf_op jit(solution)/shard_map/dot_general | solution.py:110
  68.5 4.8 fusion.54
  73.3 2.5 copy.58
  77.6 1.2 slice_bitcast_fusion
  79.7 2.2 fusion.31
  83.8 2.1 convolution_convert_fusion.5
  85.9 4.1 reshape.624
  90.1 3.3 pad_maximum_fusion
  93.4 4.1 copy.82
  98.6 1.9 copy.84
  101.3 34.5 %reduce-scatter.13.cloned.1.call-done = bf16[896,192]{1,0:T(8,128)(2,1)} async-done(((bf16[3584,192]{1,0:T(8,128)(2,1)}), bf16[896,192]{1,0:T(8,128)(2,1)}) %reduce-scatter.13.cloned.1.call-update) | async-done | bytes 344080
  135.8 1.5 slice.202
  137.3 1.0 slice.200
  140.1 2.0 fusion.58
  142.8 2.5 convolution_convert_fusion.6
  145.3 1.3 fusion.133
  147.0 1.7 reduce-window.29
  150.0 1.6 fusion.106
  151.6 1.0 mul.275
  152.6 3.5 scatter_custom_fusion.1
  156.2 15.7 %all-gather.11.cloned.1.call-done = bf16[4,720,192]{1,2,0:T(8,128)(2,1)} async-done(((bf16[1,720,192]{1,2,0:T(8,128)(2,1)}), bf16[4,720,192]{1,2,0:T(8,128)(2,1)}) %all-gather.11.cloned.1.call-update) | async-done | bytes 1105936 | tf_op jit(solution)/shard_map/all_gather | solution.py:220
  171.9 3.2 copy.67
  175.1 3.5 reshape.697
  178.6 1.6 fusion.25
  180.1 1.6 fusion.27
  181.7 4.5 convolution_convert_fusion.1
  186.2 4.7 all-to-all-start
  191.0 2.2 convolution_convert_fusion.4
  193.1 3.4 reshape.628
  196.6 1.2 convolution_convert_fusion.9
  198.8 2.7 copy.83
  202.1 38.5 %reduce-scatter.15.cloned.1.call-done = bf16[896,192]{1,0:T(8,128)(2,1)} async-done(((bf16[3584,192]{1,0:T(8,128)(2,1)}), bf16[896,192]{1,0:T(8,128)(2,1)}) %reduce-scatter.15.cloned.1.call-update) | async-done | bytes 344080
  241.5 1.0 slice.204
  244.9 1.7 reduce-window.25
  247.5 3.5 scatter_custom_fusion
  251.0 22.5 %all-gather.9.cloned.1.call-done = bf16[4,720,192]{1,2,0:T(8,128)(2,1)} async-done(((bf16[1,720,192]{1,2,0:T(8,128)(2,1)}), bf16[4,720,192]{1,2,0:T(8,128)(2,1)}) %all-gather.9.cloned.1.call-update) | async-done | bytes 1105936 | tf_op jit(solution)/shard_map/all_gather | solution.py:220
  273.5 2.2 copy.64
  277.3 4.4 convolution_convert_fusion
  281.7 4.7 all-to-all-start.1
  286.5 10.4 %fusion.4 = f32[1024,720]{0,1:T(8,128)} fusion(bf16[1024,2944]{1,0:T(8,128)(2,1)} %bitcast.56, bf16[1,2880,720]{1,2,0:T(8,128)(2,1)} %param.38), kind=kOutput, calls=%fused_computation.16 | convolution fusion | flops 4246732800 | bytes 13125632 | tf_op jit(solution)/shard_map/dot_general | solution.py:253
  296.9 16.8 %convolution_convert_fusion.2 = bf16[1024,2944]{1,0:T(8,128)(2,1)} fusion(bf16[720,2880]{1,0:T(8,128)(2,1)} %bitcast.211, f32[1024,720]{0,1:T(8,128)} %fusion.4, bf16[1,2880,720]{1,2,0:T(8,128)(2,1)} %param.37, bf16[1024,2944]{1,0:T(8,128)(2,1)} %bitcast.56), kind=kOutput, calls=%fused_computation.12 | convolution fusion | flops 8596750336 | bytes 23302144 | tf_op jit(solution)/shard_map/dot_general | solution.py:258
  313.6 41.6 %all-to-all-done.1 = bf16[8,128,2944]{2,1,0:T(8,128)(2,1)} async-done(((bf16[8,128,2944]{2,1,0:T(8,128)(2,1)}), bf16[8,128,2944]{2,1,0:T(8,128)(2,1)}, u32[]{:S(2)}, u32[]{:S(2)}) %all-to-all-start.1) | async-done | bytes 6029344 | tf_op jit(solution)/shard_map/all_to_all | solution.py:246
  355.3 5.1 all-to-all-start.2
  360.9 10.4 %fusion.8 = f32[1024,720]{0,1:T(8,128)} fusion(bf16[1024,2944]{1,0:T(8,128)(2,1)} %bitcast.51, bf16[1,2880,720]{1,2,0:T(8,128)(2,1)} %param.38), kind=kOutput, calls=%fused_computation.20 | convolution fusion | flops 4246732800 | bytes 13125632 | tf_op jit(solution)/shard_map/dot_general | solution.py:253
  371.2 16.8 %convolution_convert_fusion.3 = bf16[1024,2944]{1,0:T(8,128)(2,1)} fusion(bf16[720,2880]{1,0:T(8,128)(2,1)} %bitcast.212, f32[1024,720]{0,1:T(8,128)} %fusion.8, bf16[1,2880,720]{1,2,0:T(8,128)(2,1)} %param.37, bf16[1024,2944]{1,0:T(8,128)(2,1)} %bitcast.51), kind=kOutput, calls=%fused_computation.13 | convolution fusion | flops 8596750336 | bytes 23302144 | tf_op jit(solution)/shard_map/dot_general | solution.py:258
  388.1 41.1 %all-to-all-done.2 = bf16[8,128,2944]{2,1,0:T(8,128)(2,1)} async-done(((bf16[8,128,2944]{2,1,0:T(8,128)(2,1)}), bf16[8,128,2944]{2,1,0:T(8,128)(2,1)}, u32[]{:S(2)}, u32[]{:S(2)}) %all-to-all-start.2) | async-done | bytes 6029344 | tf_op jit(solution)/shard_map/all_to_all | solution.py:266
  429.2 5.6 fusion.138
  434.7 4.7 all-to-all-start.3
  439.5 1.7 copy.78
  441.9 2.2 gather_fusion
  444.2 64.1 %all-to-all-done.3 = bf16[8,128,2944]{2,1,0:T(8,128)(2,1)} async-done(((bf16[8,128,2944]{2,1,0:T(8,128)(2,1)}), bf16[8,128,2944]{2,1,0:T(8,128)(2,1)}, u32[]{:S(2)}, u32[]{:S(2)}) %all-to-all-start.3) | async-done | bytes 6029344 | tf_op jit(solution)/shard_map/all_to_all | solution.py:266
  508.2 6.0 %fusion.139 = (bf16[192,2880]{1,0:T(8,128)(2,1)}, f32[192,2880]{1,0:T(8,128)}) fusion(bf16[192,1024]{1,0:T(8,128)(2,1)S(1)} %fusion.48, bf16[1024,2944]{1,0:T(8,128)(2,1)} %bitcast.59), kind=kOutput, calls=%fused_computation.234 | convolution fusion | flops 1133015040 | bytes 9740288 | tf_op jit(solution)/shard_map/dot_general | solution.py:276
  514.2 2.2 gather_fusion.1
  516.8 1.3 pad_maximum_fusion.2
  518.1 1.7 copy.80
  519.9 2.1 gather_fusion.2
  522.5 1.2 copy.79
  523.8 27.4 %reduce-scatter.19.cloned.1.call-done = bf16[720,208]{1,0:T(8,128)(2,1)} async-done(((bf16[2880,208]{1,0:T(8,128)(2,1)}), bf16[720,208]{1,0:T(8,128)(2,1)}) %reduce-scatter.19.cloned.1.call-update) | async-done | bytes 299536
  551.1 1.1 copy.81
  552.7 9.2 %all-gather.2 = bf16[8,4,2880]{2,1,0:T(4,128)(2,1)S(1)} all-gather(bf16[1,4,2880]{2,1,0:T(4,128)(2,1)S(1)} %fusion.104), channel_id=1, replica_groups=mesh['dp'=4,'expert'=8] {'expert'}, dimensions={0}, use_global_device_ids=true | all-gather | bytes 207360 | tf_op jit(solution)/shard_map/all_gather | solution.py:305
  562.9 1.0 copy.72
  563.9 4.5 fusion.141
  (152 shorter events, 29.7 us)
Async XLA Ops:
  7.2 76.6 %copy-start = (bf16[512,2880]{0,1:T(8,128)(2,1)S(1)}, bf16[512,2880]{0,1:T(8,128)(2,1)}, u32[]{:S(2)}) copy-start(bf16[512,2880]{0,1:T(8,128)(2,1)} %param.31) | copy-start | bytes 8847364
  7.2 55.4 %copy-start.18 = (f32[2880]{0:T(1024)S(1)}, f32[2880]{0:T(1024)}, u32[]{:S(2)}) copy-start(f32[2880]{0:T(1024)} %param.28) | copy-start | bytes 34564
  7.2 53.2 %all-gather.7.cloned.1.call-start = ((), (), s32[]{:S(2)}) async-start(), calls=%async_computation.8 | async-start | bytes 2764800 | tf_op jit(solution)/shard_map/all_gather | solution.py:105
  7.9 127.9 %reduce-scatter.13.cloned.1.call-start = ((), (), s32[]{:S(2)}) async-start(), calls=%async_computation.11 | async-start | bytes 2293760
  12.3 56.2 %copy-start.16 = (s32[128]{0:T(128)}, s32[128]{0:T(128)S(1)}, u32[]{:S(2)}) copy-start(s32[128]{0:T(128)S(1)} %and_select_fusion) | copy-start | bytes 1540
  13.2 55.3 %copy-start.15 = (s32[384]{0:T(512)}, s32[384]{0:T(512)S(1)}, u32[]{:S(2)}) copy-start(s32[384]{0:T(512)S(1)} %select_reduce_fusion.1) | copy-start | bytes 4612
  14.4 65.4 %copy-start.11 = (pred[192,384]{1,0:T(8,128)(4,1)}, pred[192,384]{1,0:T(8,128)(4,1)S(1)}, u32[]{:S(2)}) copy-start(pred[192,384]{1,0:T(8,128)(4,1)S(1)} %fusion.69) | copy-start | bytes 221188
  62.6 5.9 %copy-start.17 = (bf16[128,1,640]{2,0,1:T(8,128)(2,1)S(1)}, bf16[128,1,640]{2,0,1:T(8,128)(2,1)}, u32[]{:S(2)}) copy-start(bf16[128,1,640]{2,0,1:T(8,128)(2,1)} %param.33) | copy-start | bytes 491524
  82.6 0.9 copy-start.7
  93.4 4.3 copy-start.2
  97.4 74.5 %all-gather.11.cloned.1.call-start = ((), (), s32[]{:S(2)}) async-start(), calls=%async_computation.10 | async-start | bytes 1474560 | tf_op jit(solution)/shard_map/all_gather | solution.py:220
  98.6 41.5 %copy-start.6 = (bf16[128,720]{0,1:T(8,128)(2,1)S(1)}, bf16[128,720]{0,1:T(8,128)(2,1)}, u32[]{:S(2)}) copy-start(bf16[128,720]{0,1:T(8,128)(2,1)} %param.35) | copy-start | bytes 552964
  101.3 44.0 %copy-start.9 = (pred[384,128]{1,0:T(32,128)(4,1)}, pred[384,128]{1,0:T(32,128)(4,1)S(1)}, u32[]{:S(2)}) copy-start(pred[384,128]{1,0:T(32,128)(4,1)S(1)} %broadcast_compare_fusion) | copy-start | bytes 147460
  156.2 24.0 %copy-start.12 = (f32[2880]{0:T(1024)S(1)}, f32[2880]{0:T(1024)}, u32[]{:S(2)}) copy-start(f32[2880]{0:T(1024)} %param.36) | copy-start | bytes 34564
  186.2 90.4 %all-to-all-start = ((bf16[8,128,2944]{2,1,0:T(8,128)(2,1)}), bf16[8,128,2944]{2,1,0:T(8,128)(2,1)}, u32[]{:S(2)}, u32[]{:S(2)}) async-start(bf16[8,128,2944]{2,1,0:T(8,128)(2,1)} %bitcast.171), calls=%async_computation | async-start | bytes 12058624 | tf_op jit(solution)/shard_map/all_to_all | solution.py:246
  190.9 49.7 %reduce-scatter.15.cloned.1.call-start = ((), (), s32[]{:S(2)}) async-start(), calls=%async_computation.12 | async-start | bytes 2293760
  193.1 4.6 copy-start.8
  198.8 3.2 copy-start.5
  201.5 41.3 %copy-start.10 = (pred[384,128]{1,0:T(32,128)(4,1)S(1)}, pred[384,128]{1,0:T(32,128)(4,1)}, u32[]{:S(2)}) copy-start(pred[384,128]{1,0:T(32,128)(4,1)} %copy-done.9) | copy-start | bytes 147460
  201.5 72.0 %all-gather.9.cloned.1.call-start = ((), (), s32[]{:S(2)}) async-start(), calls=%async_computation.9 | async-start | bytes 1474560 | tf_op jit(solution)/shard_map/all_gather | solution.py:220
  281.7 73.5 %all-to-all-start.1 = ((bf16[8,128,2944]{2,1,0:T(8,128)(2,1)}), bf16[8,128,2944]{2,1,0:T(8,128)(2,1)}, u32[]{:S(2)}, u32[]{:S(2)}) async-start(bf16[8,128,2944]{2,1,0:T(8,128)(2,1)} %bitcast.172), calls=%async_computation.1 | async-start | bytes 12058624 | tf_op jit(solution)/shard_map/all_to_all | solution.py:246
  355.3 5.2 copy-start.14
  355.3 73.9 %all-to-all-start.2 = ((bf16[8,128,2944]{2,1,0:T(8,128)(2,1)}), bf16[8,128,2944]{2,1,0:T(8,128)(2,1)}, u32[]{:S(2)}, u32[]{:S(2)}) async-start(bf16[8,128,2944]{2,1,0:T(8,128)(2,1)} %bitcast.180), calls=%async_computation.2 | async-start | bytes 12058624 | tf_op jit(solution)/shard_map/all_to_all | solution.py:266
  434.7 73.5 %all-to-all-start.3 = ((bf16[8,128,2944]{2,1,0:T(8,128)(2,1)}), bf16[8,128,2944]{2,1,0:T(8,128)(2,1)}, u32[]{:S(2)}, u32[]{:S(2)}) async-start(bf16[8,128,2944]{2,1,0:T(8,128)(2,1)} %bitcast.179), calls=%async_computation.3 | async-start | bytes 12058624 | tf_op jit(solution)/shard_map/all_to_all | solution.py:266
  439.4 83.1 %reduce-scatter.17.cloned.1.call-start = ((), (), s32[]{:S(2)}) async-start(), calls=%async_computation.13 | async-start | bytes 1843200
  441.2 109.9 %reduce-scatter.19.cloned.1.call-start = ((), (), s32[]{:S(2)}) async-start(), calls=%async_computation.14 | async-start | bytes 1843200
  519.9 32.8 %copy-start.13 = (f32[2880]{0:T(1024)S(1)}, f32[2880]{0:T(1024)}, u32[]{:S(2)}) copy-start(f32[2880]{0:T(1024)} %param.40) | copy-start | bytes 34564
  519.9 42.8 %copy-start.3 = (bf16[192,720]{1,0:T(8,128)(2,1)S(1)}, bf16[192,720]{1,0:T(8,128)(2,1)}, u32[]{:S(2)}) copy-start(bf16[192,720]{1,0:T(8,128)(2,1)} %fusion.58) | copy-start | bytes 829444
  519.9 42.8 %copy-start.4 = (bf16[192,720]{1,0:T(8,128)(2,1)S(1)}, bf16[192,720]{1,0:T(8,128)(2,1)}, u32[]{:S(2)}) copy-start(bf16[192,720]{1,0:T(8,128)(2,1)} %fusion.57) | copy-start | bytes 829444
  562.9 5.6 copy-start.1
Sparse Core Ops, SparseCore 0:
  9.6 50.7 all-gather.6
  97.6 38.2 reduce-scatter.12
  142.3 29.5 all-gather.10
  201.6 38.9 reduce-scatter.14
  243.9 29.5 all-gather.8
  442.3 33.2 reduce-scatter.16
  520.0 31.0 reduce-scatter.18

commit v10 on v7

--- a/solution.py
+++ b/solution.py
@@ -157,10 +157,9 @@
     reduced_parts = []
 
     def reduce_rows(lo, rows):
-        joined_back = lax.psum_scatter(
-            joined_send[lo : lo + rows], "dp", scatter_dimension=1, tiled=True
-        )
-        return joined_back
+        pieces = joined_send[lo : lo + rows].reshape(rows, groups, -1).transpose(1, 0, 2)
+        swapped = lax.all_to_all(pieces, "dp", split_axis=0, concat_axis=0, tiled=True)
+        return jnp.sum(swapped.astype(jnp.float32), axis=0).astype(jnp.bfloat16)
 
     def resid_rows(joined_back, lo, rows):
         mine_out = joined_back[:, :quarter].astype(jnp.float32)

time: 567 us -> 581 us (1.025)
  starting transfers between devices: 19.7 us -> 26.8 us
    unnamed x11 -> x7, waiting for transfers between devices: 108 us -> 31.6 us
    all_to_all x0 -> x2, waiting for transfers between devices: none -> 32.3 us  [reduce_rows(): lax.all_to_all(pieces, 'dp', split_axis=0, concat_axis=0, tiled=True)]
    all_to_all x2, waiting for transfers between devices: 41.6 us -> 69.3 us  [shards(): lax.all_to_all(outgoing, 'expert', split_axis=0, concat_axis=0, tiled=True)]
    all_gather x2, waiting for transfers between devices: 45 us -> 66.4 us  [shards(): column_h = lax.all_gather(resid_h, 'dp', axis=1, tiled=True)]
    all_to_all x0 -> x2, starting transfers between devices: none -> 7.23 us  [reduce_rows(): lax.all_to_all(pieces, 'dp', split_axis=0, concat_axis=0, tiled=True)]
    slice x6 -> x1, local copies, waits for them, and re-layouts: 6.72 us -> 0.07 us  [the longest x1 2.94 us: reduce_rows(): joined_send[lo:lo + rows]]
    unnamed x46 -> x33, local copies, waits for them, and re-layouts: 16.6 us -> 16.1 us
  transfers between devices with their start and end apart: 11 -> 11, of which waited for: 9 -> 9; matrix products, arithmetic and copies ran while one was open for 19% -> 20% of each run, Pallas kernels for 0% -> 0%
where the time goes in v10:
time: 581 us; the launch traced here: 572 us
  waiting for transfers between devices  351 us (60%)
  matrix products  100 us (17%)
  local copies, waits for them, and re-layouts  49.7 us (9%)
  starting transfers between devices  26.8 us (5%)
  other arithmetic  20.9 us (4%)
  between operations  14.8 us (3%)
  blocking collectives  9.22 us (2%)
    all_to_all x2, waiting for transfers between devices, shards(): lax.all_to_all(shares_out, 'expert', split_axis=0, concat_axis=0, tiled=T...  104 us
    all_to_all x2, waiting for transfers between devices, shards(): lax.all_to_all(outgoing, 'expert', split_axis=0, concat_axis=0, tiled=True)  69.3 us
    all_gather x2, waiting for transfers between devices, shards(): column_h = lax.all_gather(resid_h, 'dp', axis=1, tiled=True)  66.4 us
    all_gather x1, waiting for transfers between devices, shards(): gathered_rows = lax.all_gather(hidden, 'dp', axis=1, tiled=True)  46.7 us
    dot_general x2, matrix products, shards(): jnp.dot(activated, down_weight, preferred_element_type=jnp.float32)  33.6 us
    all_to_all x2, waiting for transfers between devices, reduce_rows(): lax.all_to_all(pieces, 'dp', split_axis=0, concat_axis=0, tiled=True)  32.3 us
    unnamed x7, waiting for transfers between devices  31.6 us
    dot_general x2, matrix products, shards(): up_part = jnp.dot(rows_in, up_weight, preferred_element_type=jnp.float32)  20.7 us
  transfers between devices with their start and end apart: 11, of which 9 were waited for; matrix products, arithmetic and copies ran while one was open for 20% of the time, Pallas kernels for 0%

profile of v10, /device:TPU:0, one launch (start us, length us, event | category | flops | bytes accessed | tf_op | source)
XLA Modules:
  0.0 571.9 jit_solution(8021652707246313375)
XLA Ops:
  7.2 0.7 all-gather.7.cloned.1.call-update
  7.9 0.8 exp.21
  8.7 0.7 reduce.5
  9.4 0.8 compare_reduce_fusion
  10.8 0.7 convert_bitcast_fusion
  11.5 0.7 pad_maximum_fusion.3
  12.5 0.7 select_reduce_fusion.1
  13.7 46.7 %all-gather.7.cloned.1.call-done = bf16[384,2880]{0,1:T(8,128)(2,1)} async-done(((bf16[384,720]{0,1:T(8,128)(2,1)}), bf16[384,2880]{0,1:T(8,128)(2,1)}) %all-gather.7.cloned.1.call-update) | async-done | bytes 2211856 | tf_op jit(solution)/shard_map/all_gather | solution.py:103
  60.4 2.2 fusion.12
  62.6 5.9 %fusion.22 = f32[384,640]{1,0:T(8,128)} fusion(bf16[2880,1,640]{2,0,1:T(8,128)(2,1)} %param.29, bf16[384,2880]{0,1:T(8,128)(2,1)} %all-gather.7.cloned.1.call-done, f32[2880]{0:T(1024)S(1)} %copy-done.8, f32[384]{0:T(512)S(1)} %add_rsqrt_fusion), kind=kOutput, calls=%fused_computation.37 | convolution fusion | flops 1420001280 | bytes 6894336 | tf_op jit(solution)/shard_map/dot_general | solution.py:108
  68.5 4.8 fusion.56
  73.3 2.5 copy.77
  75.8 0.9 slice_bitcast_fusion.3
  76.7 1.2 slice_bitcast_fusion.2
  78.3 1.3 fusion.19
  79.6 2.3 fusion.59
  82.2 3.0 convolution_convert_fusion.4
  85.3 4.2 copy.80
  89.6 2.3 pad_maximum_fusion
  91.9 1.8 slice_bitcast_fusion.1
  93.6 3.7 all-to-all-start
  98.0 32.3 %all-to-all-done = bf16[4,192,896]{2,1,0:T(8,128)(2,1)S(1)} async-done(((bf16[4,192,896]{2,1,0:T(8,128)(2,1)}), bf16[4,192,896]{2,1,0:T(8,128)(2,1)S(1)}, u32[]{:S(2)}, u32[]{:S(2)}) %all-to-all-start) | async-done | bytes 1376288 | tf_op jit(solution)/shard_map/all_to_all | solution.py:161
  130.6 1.0 fusion.63
  131.7 3.6 all-to-all-start.1
  135.8 1.7 reduce-window.29
  138.6 3.4 scatter_custom_fusion.1
  141.9 40.7 %all-gather.11.cloned.1.call-done = bf16[4,720,192]{1,2,0:T(8,128)(2,1)} async-done(((bf16[1,720,192]{1,2,0:T(8,128)(2,1)}), bf16[4,720,192]{1,2,0:T(8,128)(2,1)}) %all-gather.11.cloned.1.call-update) | async-done | bytes 1105936 | tf_op jit(solution)/shard_map/all_gather | solution.py:204
  182.6 3.2 copy.99
  185.8 2.7 reshape.558
  189.2 4.5 convolution_convert_fusion.1
  193.7 4.7 all-to-all-start.2
  198.9 1.9 fusion.62
  201.5 1.7 reduce-window.25
  204.2 3.6 scatter_custom_fusion
  207.8 25.8 %all-gather.9.cloned.1.call-done = bf16[4,720,192]{1,2,0:T(8,128)(2,1)} async-done(((bf16[1,720,192]{1,2,0:T(8,128)(2,1)}), bf16[4,720,192]{1,2,0:T(8,128)(2,1)}) %all-gather.9.cloned.1.call-update) | async-done | bytes 1105936 | tf_op jit(solution)/shard_map/all_gather | solution.py:204
  233.6 3.2 copy.93
  236.8 2.7 reshape.556
  239.6 27.6 %all-to-all-done.2 = bf16[8,128,2944]{2,1,0:T(8,128)(2,1)} async-done(((bf16[8,128,2944]{2,1,0:T(8,128)(2,1)}), bf16[8,128,2944]{2,1,0:T(8,128)(2,1)}, u32[]{:S(2)}, u32[]{:S(2)}) %all-to-all-start.2) | async-done | bytes 6029344 | tf_op jit(solution)/shard_map/all_to_all | solution.py:230
  267.9 4.4 convolution_convert_fusion
  272.3 4.7 all-to-all-start.3
  277.0 10.4 %fusion.4 = f32[1024,720]{0,1:T(8,128)} fusion(bf16[1024,2944]{1,0:T(8,128)(2,1)} %bitcast.45, bf16[1,2880,720]{1,2,0:T(8,128)(2,1)} %param.38), kind=kOutput, calls=%fused_computation.16 | convolution fusion | flops 4246732800 | bytes 13125632 | tf_op jit(solution)/shard_map/dot_general | solution.py:237
  287.4 16.8 %convolution_convert_fusion.2 = bf16[1024,2944]{1,0:T(8,128)(2,1)} fusion(bf16[720,2880]{1,0:T(8,128)(2,1)} %bitcast.171, f32[1024,720]{0,1:T(8,128)} %fusion.4, bf16[1,2880,720]{1,2,0:T(8,128)(2,1)} %param.37, bf16[1024,2944]{1,0:T(8,128)(2,1)} %bitcast.45), kind=kOutput, calls=%fused_computation.12 | convolution fusion | flops 8596750336 | bytes 23302144 | tf_op jit(solution)/shard_map/dot_general | solution.py:242
  304.2 41.6 %all-to-all-done.3 = bf16[8,128,2944]{2,1,0:T(8,128)(2,1)} async-done(((bf16[8,128,2944]{2,1,0:T(8,128)(2,1)}), bf16[8,128,2944]{2,1,0:T(8,128)(2,1)}, u32[]{:S(2)}, u32[]{:S(2)}) %all-to-all-start.3) | async-done | bytes 6029344 | tf_op jit(solution)/shard_map/all_to_all | solution.py:230
  345.8 5.0 all-to-all-start.4
  351.4 10.4 %fusion.8 = f32[1024,720]{0,1:T(8,128)} fusion(bf16[1024,2944]{1,0:T(8,128)(2,1)} %bitcast.40, bf16[1,2880,720]{1,2,0:T(8,128)(2,1)} %param.38), kind=kOutput, calls=%fused_computation.20 | convolution fusion | flops 4246732800 | bytes 13125632 | tf_op jit(solution)/shard_map/dot_general | solution.py:237
  361.7 16.8 %convolution_convert_fusion.3 = bf16[1024,2944]{1,0:T(8,128)(2,1)} fusion(bf16[720,2880]{1,0:T(8,128)(2,1)} %bitcast.172, f32[1024,720]{0,1:T(8,128)} %fusion.8, bf16[1,2880,720]{1,2,0:T(8,128)(2,1)} %param.37, bf16[1024,2944]{1,0:T(8,128)(2,1)} %bitcast.40), kind=kOutput, calls=%fused_computation.13 | convolution fusion | flops 8596750336 | bytes 23302144 | tf_op jit(solution)/shard_map/dot_general | solution.py:242
  378.6 41.1 %all-to-all-done.4 = bf16[8,128,2944]{2,1,0:T(8,128)(2,1)} async-done(((bf16[8,128,2944]{2,1,0:T(8,128)(2,1)}), bf16[8,128,2944]{2,1,0:T(8,128)(2,1)}, u32[]{:S(2)}, u32[]{:S(2)}) %all-to-all-start.4) | async-done | bytes 6029344 | tf_op jit(solution)/shard_map/all_to_all | solution.py:250
  419.6 5.8 %fusion.138 = (bf16[192,2880]{1,0:T(8,128)(2,1)}, f32[192,2880]{1,0:T(8,128)}) fusion(bf16[192,1024]{1,0:T(8,128)(2,1)S(1)} %fusion.51, bf16[1024,2944]{1,0:T(8,128)(2,1)} %bitcast.47), kind=kOutput, calls=%fused_computation.219 | convolution fusion | flops 1133015040 | bytes 9740288 | tf_op jit(solution)/shard_map/dot_general | solution.py:260
  425.5 4.7 all-to-all-start.5
  430.3 2.5 copy.104
  433.5 2.2 gather_fusion
  435.8 63.2 %all-to-all-done.5 = bf16[8,128,2944]{2,1,0:T(8,128)(2,1)} async-done(((bf16[8,128,2944]{2,1,0:T(8,128)(2,1)}), bf16[8,128,2944]{2,1,0:T(8,128)(2,1)}, u32[]{:S(2)}, u32[]{:S(2)}) %all-to-all-start.5) | async-done | bytes 6029344 | tf_op jit(solution)/shard_map/all_to_all | solution.py:250
  499.0 6.0 %fusion.139 = (bf16[192,2880]{1,0:T(8,128)(2,1)}, f32[192,2880]{1,0:T(8,128)}) fusion(bf16[192,1024]{1,0:T(8,128)(2,1)S(1)} %fusion.50, bf16[1024,2944]{1,0:T(8,128)(2,1)} %bitcast.48), kind=kOutput, calls=%fused_computation.220 | convolution fusion | flops 1133015040 | bytes 9740288 | tf_op jit(solution)/shard_map/dot_general | solution.py:260
  505.0 2.2 gather_fusion.1
  507.6 2.4 pad_maximum_fusion.1
  509.9 2.5 copy.106
  513.7 1.9 copy.105
  515.5 30.8 %reduce-scatter.9.cloned.1.call-done = bf16[720,208]{1,0:T(8,128)(2,1)} async-done(((bf16[2880,208]{1,0:T(8,128)(2,1)}), bf16[720,208]{1,0:T(8,128)(2,1)}) %reduce-scatter.9.cloned.1.call-update) | async-done | bytes 299536
  546.3 1.1 copy.107
  547.9 9.2 %all-gather.2 = bf16[8,4,2880]{2,1,0:T(4,128)(2,1)S(1)} all-gather(bf16[1,4,2880]{2,1,0:T(4,128)(2,1)S(1)} %fusion.108), channel_id=1, replica_groups=mesh['dp'=4,'expert'=8] {'expert'}, dimensions={0}, use_global_device_ids=true | all-gather | bytes 207360 | tf_op jit(solution)/shard_map/all_gather | solution.py:289
  557.2 0.8 reshape.560
  557.9 1.5 add_convert_fusion
  559.5 1.0 copy.102
  560.5 4.5 fusion.140
  (116 shorter events, 11.4 us)
Async XLA Ops:
  7.2 75.1 %copy-start = (bf16[512,2880]{0,1:T(8,128)(2,1)S(1)}, bf16[512,2880]{0,1:T(8,128)(2,1)}, u32[]{:S(2)}) copy-start(bf16[512,2880]{0,1:T(8,128)(2,1)} %param.31) | copy-start | bytes 8847364
  7.2 55.4 %copy-start.8 = (f32[2880]{0:T(1024)S(1)}, f32[2880]{0:T(1024)}, u32[]{:S(2)}) copy-start(f32[2880]{0:T(1024)} %param.28) | copy-start | bytes 34564
  7.2 53.2 %all-gather.7.cloned.1.call-start = ((), (), s32[]{:S(2)}) async-start(), calls=%async_computation.8 | async-start | bytes 2764800 | tf_op jit(solution)/shard_map/all_gather | solution.py:103
  79.6 2.3 copy-start.4
  91.8 5.7 copy-start.2
  93.6 37.0 %copy-start.7 = (bf16[128,720]{0,1:T(8,128)(2,1)S(1)}, bf16[128,720]{0,1:T(8,128)(2,1)}, u32[]{:S(2)}) copy-start(bf16[128,720]{0,1:T(8,128)(2,1)} %param.35) | copy-start | bytes 552964
  93.6 36.6 %all-to-all-start = ((bf16[4,192,896]{2,1,0:T(8,128)(2,1)}), bf16[4,192,896]{2,1,0:T(8,128)(2,1)S(1)}, u32[]{:S(2)}, u32[]{:S(2)}) async-start(bf16[4,192,896]{2,1,0:T(8,128)(2,1)} %get-tuple-element.24), calls=%async_computation | async-start | bytes 2752512 | tf_op jit(solution)/shard_map/all_to_all | solution.py:161
  97.3 85.3 %all-gather.11.cloned.1.call-start = ((), (), s32[]{:S(2)}) async-start(), calls=%async_computation.10 | async-start | bytes 1474560 | tf_op jit(solution)/shard_map/all_gather | solution.py:204
  131.7 62.0 %all-to-all-start.1 = ((bf16[4,192,896]{2,1,0:T(8,128)(2,1)}), bf16[4,192,896]{2,1,0:T(8,128)(2,1)S(1)}, u32[]{:S(2)}, u32[]{:S(2)}) async-start(bf16[4,192,896]{2,1,0:T(8,128)(2,1)} %get-tuple-element.25), calls=%async_computation.1 | async-start | bytes 2752512 | tf_op jit(solution)/shard_map/all_to_all | solution.py:161
  138.4 50.5 %copy-start.5 = (f32[2880]{0:T(1024)S(1)}, f32[2880]{0:T(1024)}, u32[]{:S(2)}) copy-start(f32[2880]{0:T(1024)} %param.36) | copy-start | bytes 34564
  193.7 73.5 %all-to-all-start.2 = ((bf16[8,128,2944]{2,1,0:T(8,128)(2,1)}), bf16[8,128,2944]{2,1,0:T(8,128)(2,1)}, u32[]{:S(2)}, u32[]{:S(2)}) async-start(bf16[8,128,2944]{2,1,0:T(8,128)(2,1)} %bitcast.145), calls=%async_computation.2 | async-start | bytes 12058624 | tf_op jit(solution)/shard_map/all_to_all | solution.py:230
  198.4 35.2 %all-gather.9.cloned.1.call-start = ((), (), s32[]{:S(2)}) async-start(), calls=%async_computation.9 | async-start | bytes 1474560 | tf_op jit(solution)/shard_map/all_gather | solution.py:204
  272.3 73.5 %all-to-all-start.3 = ((bf16[8,128,2944]{2,1,0:T(8,128)(2,1)}), bf16[8,128,2944]{2,1,0:T(8,128)(2,1)}, u32[]{:S(2)}, u32[]{:S(2)}) async-start(bf16[8,128,2944]{2,1,0:T(8,128)(2,1)} %bitcast.146), calls=%async_computation.3 | async-start | bytes 12058624 | tf_op jit(solution)/shard_map/all_to_all | solution.py:230
  345.8 73.8 %all-to-all-start.4 = ((bf16[8,128,2944]{2,1,0:T(8,128)(2,1)}), bf16[8,128,2944]{2,1,0:T(8,128)(2,1)}, u32[]{:S(2)}, u32[]{:S(2)}) async-start(bf16[8,128,2944]{2,1,0:T(8,128)(2,1)} %bitcast.152), calls=%async_computation.4 | async-start | bytes 12058624 | tf_op jit(solution)/shard_map/all_to_all | solution.py:250
  425.5 73.5 %all-to-all-start.5 = ((bf16[8,128,2944]{2,1,0:T(8,128)(2,1)}), bf16[8,128,2944]{2,1,0:T(8,128)(2,1)}, u32[]{:S(2)}, u32[]{:S(2)}) async-start(bf16[8,128,2944]{2,1,0:T(8,128)(2,1)} %bitcast.151), calls=%async_computation.5 | async-start | bytes 12058624 | tf_op jit(solution)/shard_map/all_to_all | solution.py:250
  430.2 83.4 %reduce-scatter.7.cloned.1.call-start = ((), (), s32[]{:S(2)}) async-start(), calls=%async_computation.11 | async-start | bytes 1843200
  432.8 113.5 %reduce-scatter.9.cloned.1.call-start = ((), (), s32[]{:S(2)}) async-start(), calls=%async_computation.12 | async-start | bytes 1843200
  509.9 37.9 %copy-start.6 = (f32[2880]{0:T(1024)S(1)}, f32[2880]{0:T(1024)}, u32[]{:S(2)}) copy-start(f32[2880]{0:T(1024)} %param.40) | copy-start | bytes 34564
  547.5 9.7 %copy-start.3 = (bf16[208,720]{1,0:T(8,128)(2,1)}, bf16[208,720]{1,0:T(8,128)(2,1)S(1)}, u32[]{:S(2)}) copy-start(bf16[208,720]{1,0:T(8,128)(2,1)S(1)} %copy.107) | copy-start | bytes 898564
  557.9 7.0 %copy-start.1 = (bf16[512,2880]{0,1:T(8,128)(2,1)S(1)}, bf16[512,2880]{0,1:T(8,128)(2,1)}, u32[]{:S(2)}) copy-start(bf16[512,2880]{0,1:T(8,128)(2,1)} %param.31) | copy-start | bytes 8847364
Sparse Core Ops, SparseCore 0:
  9.6 50.7 all-gather.6
  131.8 50.7 all-gather.10
  201.0 32.5 all-gather.8
  433.1 35.9 reduce-scatter.6
  512.6 33.7 reduce-scatter.8

commit v11 on v7

--- a/solution.py
+++ b/solution.py
@@ -183,9 +183,8 @@
     gate_weight = expert_gate_weight[0]
     up_weight = expert_up_weight[0]
     down_weight = jnp.pad(expert_down_weight[0], ((0, 0), (0, lane_pad)))
-    halves = 2 if groups % 2 == 0 else 1
-    half_tokens = col_tokens // halves
-    half_capacity = (groups // halves) * capacity
+    chunk_blocks = [groups - groups // 2] + [1] * (groups // 2)
+    halves = len(chunk_blocks)
     counter = jnp.arange(col_tokens, dtype=jnp.int32)
     request_ids = jnp.arange(REQS, dtype=jnp.int32)
     last_index = jnp.max(
@@ -198,7 +197,9 @@
     held = None
     pending = None
     for h in range(halves):
-        lo = h * half_tokens
+        lo = sum(chunk_blocks[:h]) * share
+        half_tokens = chunk_blocks[h] * share
+        half_capacity = chunk_blocks[h] * capacity
         joined_h = reduce_rows(lo, half_tokens)
         resid_h, pack_h = resid_rows(joined_h, lo, half_tokens)
         reduced_parts.append(resid_h)

time: 567 us -> 607 us (1.071)
  waiting for transfers between devices: 346 us -> 305 us
  blocking collectives: 9.22 us -> 41.7 us
  local copies, waits for them, and re-layouts: 50.8 us -> 72.8 us
  matrix products: 97.7 us -> 107 us
  starting transfers between devices: 19.7 us -> 28.6 us
  other arithmetic: 18.9 us -> 27 us
    all_gather x2 -> x1, waiting for transfers between devices: 45 us -> 8.72 us  [shards(): column_h = lax.all_gather(resid_h, 'dp', axis=1, tiled=True)]
    all_gather x0 -> x2, blocking collectives: none -> 32.4 us  [shards(): column_h = lax.all_gather(resid_h, 'dp', axis=1, tiled=True)]
    all_to_all x2 -> x3, waiting for transfers between devices: 41.6 us -> 21.3 us  [shards(): lax.all_to_all(outgoing, 'expert', split_axis=0, concat_axis=0, tiled=True)]
    dot_general x0 -> x2, matrix products: none -> 12.3 us  [shards(): jnp.dot(rows_in, gate_weight, preferred_element_type=jnp.float32)]
    unnamed x11 -> x14, waiting for transfers between devices: 108 us -> 119 us
    dot_general x2 -> x1, matrix products: 20.7 us -> 10.3 us  [shards(): up_part = jnp.dot(rows_in, up_weight, preferred_element_type=jnp.float32)]
    unnamed x46 -> x63, local copies, waits for them, and re-layouts: 16.6 us -> 23.3 us
    dot_general x2 -> x3, matrix products: 33.6 us -> 39.3 us  [shards(): jnp.dot(activated, down_weight, preferred_element_type=jnp.float32)]
  transfers between devices with their start and end apart: 11 -> 14, of which waited for: 9 -> 12; matrix products, arithmetic and copies ran while one was open for 19% -> 24% of each run, Pallas kernels for 0% -> 0%
where the time goes in v11:
time: 607 us; the launch traced here: 597 us
  waiting for transfers between devices  305 us (50%)
  matrix products  107 us (18%)
  local copies, waits for them, and re-layouts  72.8 us (12%)
  blocking collectives  41.7 us (7%)
  starting transfers between devices  28.6 us (5%)
  other arithmetic  27 us (4%)
  between operations  15.3 us (3%)
    unnamed x14, waiting for transfers between devices  119 us
    all_to_all x3, waiting for transfers between devices, shards(): lax.all_to_all(shares_out, 'expert', split_axis=0, concat_axis=0, tiled=T...  110 us
    all_gather x1, waiting for transfers between devices, shards(): gathered_rows = lax.all_gather(hidden, 'dp', axis=1, tiled=True)  46.6 us
    dot_general x3, matrix products, shards(): jnp.dot(activated, down_weight, preferred_element_type=jnp.float32)  39.3 us
    all_gather x2, blocking collectives, shards(): column_h = lax.all_gather(resid_h, 'dp', axis=1, tiled=True)  32.4 us
    unnamed x63, local copies, waits for them, and re-layouts  23.3 us
    all_to_all x3, waiting for transfers between devices, shards(): lax.all_to_all(outgoing, 'expert', split_axis=0, concat_axis=0, tiled=True)  21.3 us
    all_to_all x3, starting transfers between devices, shards(): lax.all_to_all(shares_out, 'expert', split_axis=0, concat_axis=0, tiled=T...  14.1 us
  transfers between devices with their start and end apart: 14, of which 12 were waited for; matrix products, arithmetic and copies ran while one was open for 24% of the time, Pallas kernels for 0%

profile of v11, /device:TPU:0, one launch (start us, length us, event | category | flops | bytes accessed | tf_op | source)
XLA Modules:
  0.0 597.0 jit_solution(7627861749963668997)
XLA Ops:
  13.7 46.6 %all-gather.7.cloned.1.call-done = bf16[384,2880]{0,1:T(8,128)(2,1)} async-done(((bf16[384,720]{0,1:T(8,128)(2,1)}), bf16[384,2880]{0,1:T(8,128)(2,1)}) %all-gather.7.cloned.1.call-update) | async-done | bytes 2211856 | tf_op jit(solution)/shard_map/all_gather | solution.py:103
  60.4 2.2 fusion.6
  62.6 5.9 fusion.20
  68.5 4.8 fusion.58
  73.3 2.5 copy.66
  79.6 2.2 fusion.60
  82.4 1.7 convolution_convert_fusion.6
  87.1 1.8 copy.102
  89.7 34.5 %reduce-scatter.19.cloned.1.call-done = bf16[896,192]{1,0:T(8,128)(2,1)} async-done(((bf16[3584,192]{1,0:T(8,128)(2,1)}), bf16[896,192]{1,0:T(8,128)(2,1)}) %reduce-scatter.19.cloned.1.call-update) | async-done | bytes 344080
  124.2 1.5 slice.234
  125.7 1.7 slice.232
  127.5 1.8 copy.103
  130.3 2.1 fusion.63
  137.7 4.1 reduce-window.35
  141.8 1.4 slice.246
  147.2 1.6 fusion.132
  149.8 3.5 scatter_custom_fusion.1
  153.4 8.7 %all-gather.9.cloned.1.call-done = bf16[4,720,192]{1,2,0:T(8,128)(2,1)} async-done(((bf16[1,720,192]{1,2,0:T(8,128)(2,1)}), bf16[4,720,192]{1,2,0:T(8,128)(2,1)}) %all-gather.9.cloned.1.call-update) | async-done | bytes 1105936 | tf_op jit(solution)/shard_map/all_gather | solution.py:206
  162.1 3.2 copy.77
  165.3 3.5 reshape.691
  168.8 1.6 fusion.36
  170.4 1.6 fusion.38
  172.0 4.5 convolution_convert_fusion
  176.4 4.7 all-to-all-start
  181.2 1.9 fusion.180
  184.2 24.5 %reduce-scatter.21.cloned.1.call-done = bf16[896,96]{1,0:T(8,128)(2,1)} async-done(((bf16[3584,96]{1,0:T(8,128)(2,1)}), bf16[896,96]{1,0:T(8,128)(2,1)}) %reduce-scatter.21.cloned.1.call-update) | async-done | bytes 172048
  210.4 24.5 %reduce-scatter.23.cloned.1.call-done = bf16[896,96]{1,0:T(8,128)(2,1)} async-done(((bf16[3584,96]{1,0:T(8,128)(2,1)}), bf16[896,96]{1,0:T(8,128)(2,1)}) %reduce-scatter.23.cloned.1.call-update) | async-done | bytes 172048
  239.9 16.3 %all-gather.2 = bf16[4,720,96]{1,2,0:T(8,128)(2,1)S(1)} all-gather(bf16[1,720,96]{1,2,0:T(8,128)(2,1)S(1)} %bitcast.212), channel_id=1, replica_groups=mesh['dp'=4,'expert'=8] {'dp'}, dimensions={0}, use_global_device_ids=true | all-gather | bytes 691200 | tf_op jit(solution)/shard_map/all_gather | solution.py:206
  257.5 16.0 %all-gather = bf16[4,720,96]{1,2,0:T(8,128)(2,1)S(1)} all-gather(bf16[1,720,96]{1,2,0:T(8,128)(2,1)S(1)} %bitcast.213), channel_id=1, replica_groups=mesh['dp'=4,'expert'=8] {'dp'}, dimensions={0}, use_global_device_ids=true | all-gather | bytes 691200 | tf_op jit(solution)/shard_map/all_gather | solution.py:206
  274.5 2.9 scatter_custom_fusion
  278.2 2.6 convolution_convert_fusion.5
  280.8 4.4 all-to-all-start.1
  285.2 10.3 %fusion.2 = f32[1024,720]{0,1:T(8,128)} fusion(bf16[1024,2944]{1,0:T(8,128)(2,1)} %bitcast.45, bf16[1,2880,720]{1,2,0:T(8,128)(2,1)} %param.38), kind=kOutput, calls=%fused_computation.15 | convolution fusion | flops 4246732800 | bytes 13125632 | tf_op jit(solution)/shard_map/dot_general | solution.py:239
  295.5 16.8 %convolution_convert_fusion.1 = bf16[1024,2944]{1,0:T(8,128)(2,1)} fusion(bf16[720,2880]{1,0:T(8,128)(2,1)} %bitcast.234, f32[1024,720]{0,1:T(8,128)} %fusion.2, bf16[1,2880,720]{1,2,0:T(8,128)(2,1)} %param.37, bf16[1024,2944]{1,0:T(8,128)(2,1)} %bitcast.45), kind=kOutput, calls=%fused_computation.12 | convolution fusion | flops 8596750336 | bytes 23302144 | tf_op jit(solution)/shard_map/dot_general | solution.py:244
  312.3 9.4 %all-to-all-done.1 = bf16[8,64,2944]{2,1,0:T(8,128)(2,1)} async-done(((bf16[8,64,2944]{2,1,0:T(8,128)(2,1)}), bf16[8,64,2944]{2,1,0:T(8,128)(2,1)}, u32[]{:S(2)}, u32[]{:S(2)}) %all-to-all-start.1) | async-done | bytes 3014688 | tf_op jit(solution)/shard_map/all_to_all | solution.py:232
  321.7 4.9 all-to-all-start.2
  329.2 2.9 scatter_custom_fusion.2
  332.1 2.6 convolution_convert_fusion.3
  334.7 60.7 %all-to-all-done.2 = bf16[8,128,2944]{2,1,0:T(8,128)(2,1)} async-done(((bf16[8,128,2944]{2,1,0:T(8,128)(2,1)}), bf16[8,128,2944]{2,1,0:T(8,128)(2,1)}, u32[]{:S(2)}, u32[]{:S(2)}) %all-to-all-start.2) | async-done | bytes 6029344 | tf_op jit(solution)/shard_map/all_to_all | solution.py:252
  395.4 4.6 all-to-all-start.3
  400.5 6.7 %fusion.17 = f32[512,720]{0,1:T(8,128)} fusion(bf16[1,2880,720]{1,2,0:T(8,128)(2,1)} %param.37, bf16[512,2944]{1,0:T(8,128)(2,1)} %bitcast.40), kind=kOutput, calls=%fused_computation.36 | convolution fusion | flops 2123366400 | bytes 8636416 | tf_op jit(solution)/shard_map/dot_general | solution.py:238
  407.3 11.5 %convolution_convert_fusion.4 = bf16[512,2944]{1,0:T(8,128)(2,1)} fusion(bf16[720,2880]{1,0:T(8,128)(2,1)} %bitcast.235, f32[512,720]{0,1:T(8,128)} %fusion.17, bf16[1,2880,720]{1,2,0:T(8,128)(2,1)} %param.38, bf16[512,2944]{1,0:T(8,128)(2,1)} %bitcast.40), kind=kOutput, calls=%fused_computation.23 | convolution fusion | flops 4298375168 | bytes 15798272 | tf_op jit(solution)/shard_map/dot_general | solution.py:244
  418.7 5.9 fusion.185
  424.6 11.8 %all-to-all-done.3 = bf16[8,64,2944]{2,1,0:T(8,128)(2,1)} async-done(((bf16[8,64,2944]{2,1,0:T(8,128)(2,1)}), bf16[8,64,2944]{2,1,0:T(8,128)(2,1)}, u32[]{:S(2)}, u32[]{:S(2)}) %all-to-all-start.3) | async-done | bytes 3014688 | tf_op jit(solution)/shard_map/all_to_all | solution.py:232
  436.5 4.7 all-to-all-start.4
  441.5 5.6 fusion.14
  447.1 11.0 %convolution_convert_fusion.2 = bf16[512,2944]{1,0:T(8,128)(2,1)} fusion(bf16[720,2880]{1,0:T(8,128)(2,1)} %bitcast.236, f32[512,720]{0,1:T(8,128)S(1)} %fusion.14, bf16[1,2880,720]{1,2,0:T(8,128)(2,1)} %param.38, bf16[512,2944]{1,0:T(8,128)(2,1)} %bitcast.54), kind=kOutput, calls=%fused_computation.21 | convolution fusion | flops 4298375168 | bytes 15798272 | tf_op jit(solution)/shard_map/dot_general | solution.py:244
  458.1 19.6 %all-to-all-done.4 = bf16[8,64,2944]{2,1,0:T(8,128)(2,1)} async-done(((bf16[8,64,2944]{2,1,0:T(8,128)(2,1)}), bf16[8,64,2944]{2,1,0:T(8,128)(2,1)}, u32[]{:S(2)}, u32[]{:S(2)}) %all-to-all-start.4) | async-done | bytes 3014688 | tf_op jit(solution)/shard_map/all_to_all | solution.py:252
  477.7 2.5 fusion.186
  480.2 4.5 all-to-all-start.5
  484.7 2.5 copy.96
  487.7 2.2 gather_fusion
  491.8 29.4 %all-to-all-done.5 = bf16[8,64,2944]{2,1,0:T(8,128)(2,1)} async-done(((bf16[8,64,2944]{2,1,0:T(8,128)(2,1)}), bf16[8,64,2944]{2,1,0:T(8,128)(2,1)}, u32[]{:S(2)}, u32[]{:S(2)}) %all-to-all-start.5) | async-done | bytes 3014688 | tf_op jit(solution)/shard_map/all_to_all | solution.py:252
  521.1 3.5 fusion.187
  524.6 1.8 gather_fusion.3
  528.1 2.0 gather_fusion.1
  531.3 1.9 copy.97
  533.2 11.1 %reduce-scatter.27.cloned.1.call-done = bf16[720,96]{1,0:T(8,128)(2,1)} async-done(((bf16[2880,96]{1,0:T(8,128)(2,1)}), bf16[720,96]{1,0:T(8,128)(2,1)}) %reduce-scatter.27.cloned.1.call-update) | async-done | bytes 138256
  544.3 1.7 copy.99
  546.0 22.8 %reduce-scatter.29.cloned.1.call-done = bf16[720,112]{1,0:T(8,128)(2,1)} async-done(((bf16[2880,112]{1,0:T(8,128)(2,1)}), bf16[720,112]{1,0:T(8,128)(2,1)}) %reduce-scatter.29.cloned.1.call-update) | async-done | bytes 161296
  570.9 9.3 %all-gather.3 = bf16[8,4,2880]{2,1,0:T(4,128)(2,1)S(1)} all-gather(bf16[1,4,2880]{2,1,0:T(4,128)(2,1)S(1)} %fusion.131), channel_id=1, replica_groups=mesh['dp'=4,'expert'=8] {'expert'}, dimensions={0}, use_global_device_ids=true | all-gather | bytes 207360 | tf_op jit(solution)/shard_map/all_gather | solution.py:291
  581.0 2.2 add_convert_fusion
  583.2 2.1 copy.85
  585.3 4.5 fusion.188
  (185 shorter events, 47.7 us)
Async XLA Ops:
  7.2 75.2 %copy-start = (bf16[512,2880]{0,1:T(8,128)(2,1)S(1)}, bf16[512,2880]{0,1:T(8,128)(2,1)}, u32[]{:S(2)}) copy-start(bf16[512,2880]{0,1:T(8,128)(2,1)} %param.31) | copy-start | bytes 8847364
  7.2 55.4 %copy-start.19 = (f32[2880]{0:T(1024)S(1)}, f32[2880]{0:T(1024)}, u32[]{:S(2)}) copy-start(f32[2880]{0:T(1024)} %param.28) | copy-start | bytes 34564
  7.2 53.2 %all-gather.7.cloned.1.call-start = ((), (), s32[]{:S(2)}) async-start(), calls=%async_computation.12 | async-start | bytes 2764800 | tf_op jit(solution)/shard_map/all_gather | solution.py:103
  7.9 116.3 %reduce-scatter.19.cloned.1.call-start = ((), (), s32[]{:S(2)}) async-start(), calls=%async_computation.14 | async-start | bytes 2293760
  12.4 0.9 copy-start.8
  12.4 56.1 %copy-start.16 = (s32[128]{0:T(128)}, s32[128]{0:T(128)S(1)}, u32[]{:S(2)}) copy-start(s32[128]{0:T(128)S(1)} %and_select_fusion) | copy-start | bytes 1540
  13.3 55.2 %copy-start.14 = (s32[384]{0:T(512)}, s32[384]{0:T(512)S(1)}, u32[]{:S(2)}) copy-start(s32[384]{0:T(512)S(1)} %select_reduce_fusion.1) | copy-start | bytes 4612
  62.6 5.9 copy-start.18
  79.6 2.3 copy-start.10
  82.3 1.7 copy-start.9
  84.4 1.9 copy-start.2
  84.4 4.6 copy-start.15
  84.4 4.5 copy-start.17
  85.8 44.4 %copy-start.4 = (bf16[128,720]{0,1:T(8,128)(2,1)S(1)}, bf16[128,720]{0,1:T(8,128)(2,1)}, u32[]{:S(2)}) copy-start(bf16[128,720]{0,1:T(8,128)(2,1)} %param.35) | copy-start | bytes 552964
  85.8 76.3 %all-gather.9.cloned.1.call-start = ((), (), s32[]{:S(2)}) async-start(), calls=%async_computation.13 | async-start | bytes 1474560 | tf_op jit(solution)/shard_map/all_gather | solution.py:206
  148.8 21.6 %copy-start.11 = (f32[2880]{0:T(1024)S(1)}, f32[2880]{0:T(1024)}, u32[]{:S(2)}) copy-start(f32[2880]{0:T(1024)} %param.36) | copy-start | bytes 34564
  176.4 100.9 %all-to-all-start = ((bf16[8,128,2944]{2,1,0:T(8,128)(2,1)}), bf16[8,128,2944]{2,1,0:T(8,128)(2,1)}, u32[]{:S(2)}, u32[]{:S(2)}) async-start(bf16[8,128,2944]{2,1,0:T(8,128)(2,1)} %bitcast.188), calls=%async_computation | async-start | bytes 12058624 | tf_op jit(solution)/shard_map/all_to_all | solution.py:232
  181.2 27.5 %reduce-scatter.21.cloned.1.call-start = ((), (), s32[]{:S(2)}) async-start(), calls=%async_computation.15 | async-start | bytes 1146880
  183.1 56.6 %copy-start.7 = (pred[384,128]{1,0:T(32,128)(4,1)S(1)}, pred[384,128]{1,0:T(32,128)(4,1)}, u32[]{:S(2)}) copy-start(pred[384,128]{1,0:T(32,128)(4,1)} %broadcast_compare_fusion) | copy-start | bytes 147460
  183.1 51.8 %reduce-scatter.23.cloned.1.call-start = ((), (), s32[]{:S(2)}) async-start(), calls=%async_computation.16 | async-start | bytes 1146880
  280.8 40.9 %all-to-all-start.1 = ((bf16[8,64,2944]{2,1,0:T(8,128)(2,1)}), bf16[8,64,2944]{2,1,0:T(8,128)(2,1)}, u32[]{:S(2)}, u32[]{:S(2)}) async-start(bf16[8,64,2944]{2,1,0:T(8,128)(2,1)} %bitcast.190), calls=%async_computation.1 | async-start | bytes 6029312 | tf_op jit(solution)/shard_map/all_to_all | solution.py:232
  321.7 73.7 %all-to-all-start.2 = ((bf16[8,128,2944]{2,1,0:T(8,128)(2,1)}), bf16[8,128,2944]{2,1,0:T(8,128)(2,1)}, u32[]{:S(2)}, u32[]{:S(2)}) async-start(bf16[8,128,2944]{2,1,0:T(8,128)(2,1)} %bitcast.199), calls=%async_computation.2 | async-start | bytes 12058624 | tf_op jit(solution)/shard_map/all_to_all | solution.py:252
  395.4 4.6 copy-start.6
  395.4 4.7 copy-start.13
  395.4 41.1 %all-to-all-start.3 = ((bf16[8,64,2944]{2,1,0:T(8,128)(2,1)}), bf16[8,64,2944]{2,1,0:T(8,128)(2,1)}, u32[]{:S(2)}, u32[]{:S(2)}) async-start(bf16[8,64,2944]{2,1,0:T(8,128)(2,1)} %bitcast.189), calls=%async_computation.3 | async-start | bytes 6029312 | tf_op jit(solution)/shard_map/all_to_all | solution.py:232
  436.5 41.2 %all-to-all-start.4 = ((bf16[8,64,2944]{2,1,0:T(8,128)(2,1)}), bf16[8,64,2944]{2,1,0:T(8,128)(2,1)}, u32[]{:S(2)}, u32[]{:S(2)}) async-start(bf16[8,64,2944]{2,1,0:T(8,128)(2,1)} %bitcast.207), calls=%async_computation.4 | async-start | bytes 6029312 | tf_op jit(solution)/shard_map/all_to_all | solution.py:252
  480.2 41.0 %all-to-all-start.5 = ((bf16[8,64,2944]{2,1,0:T(8,128)(2,1)}), bf16[8,64,2944]{2,1,0:T(8,128)(2,1)}, u32[]{:S(2)}, u32[]{:S(2)}) async-start(bf16[8,64,2944]{2,1,0:T(8,128)(2,1)} %bitcast.206), calls=%async_computation.5 | async-start | bytes 6029312 | tf_op jit(solution)/shard_map/all_to_all | solution.py:252
  484.6 46.6 %reduce-scatter.25.cloned.1.call-start = ((), (), s32[]{:S(2)}) async-start(), calls=%async_computation.17 | async-start | bytes 1843200
  487.2 57.1 %reduce-scatter.27.cloned.1.call-start = ((), (), s32[]{:S(2)}) async-start(), calls=%async_computation.18 | async-start | bytes 921600
  491.7 77.0 %reduce-scatter.29.cloned.1.call-start = ((), (), s32[]{:S(2)}) async-start(), calls=%async_computation.19 | async-start | bytes 921600
  526.7 44.1 %copy-start.12 = (f32[2880]{0:T(1024)S(1)}, f32[2880]{0:T(1024)}, u32[]{:S(2)}) copy-start(f32[2880]{0:T(1024)} %param.40) | copy-start | bytes 34564
  526.8 54.1 %copy-start.3 = (bf16[192,720]{1,0:T(8,128)(2,1)S(1)}, bf16[192,720]{1,0:T(8,128)(2,1)}, u32[]{:S(2)}) copy-start(bf16[192,720]{1,0:T(8,128)(2,1)} %fusion.63) | copy-start | bytes 829444
  569.8 0.7 copy-start.5
  581.0 8.8 %copy-start.1 = (bf16[512,2880]{0,1:T(8,128)(2,1)S(1)}, bf16[512,2880]{0,1:T(8,128)(2,1)}, u32[]{:S(2)}) copy-start(bf16[512,2880]{0,1:T(8,128)(2,1)} %param.31) | copy-start | bytes 8847364
Sparse Core Ops, SparseCore 0:
  9.6 50.7 all-gather.6
  86.0 38.2 reduce-scatter.18
  132.5 29.5 all-gather.8
  184.0 24.6 reduce-scatter.20
  210.9 24.0 reduce-scatter.22
  487.5 32.5 reduce-scatter.24
  522.5 21.7 reduce-scatter.26
  546.7 22.0 reduce-scatter.28

commit v12 on v7

--- a/solution.py
+++ b/solution.py
@@ -249,6 +249,8 @@
             moe_rows.append(lax.psum_scatter(pending, "dp", scatter_dimension=1, tiled=True))
             pending = None
         answers = lax.all_to_all(shares_out, "expert", split_axis=0, concat_axis=0, tiled=True)
+        if moe_rows:
+            answers, moe_rows[-1] = lax.optimization_barrier((answers, moe_rows[-1]))
         slot_ids = jnp.arange(experts * half_capacity, dtype=jnp.int32)
         combine = jnp.sum(
             jnp.where(
@@ -275,15 +277,21 @@
             pending = mixture.astype(jnp.bfloat16)
         else:
             last_mix = sum(last_parts).reshape(REQS * groups, quarter)
-            moe_send = jnp.concatenate(
-                [mixture, jnp.tile(last_mix, (1, groups))], axis=0
-            ).astype(jnp.bfloat16)
+            extra_back = lax.psum_scatter(
+                jnp.tile(last_mix, (1, groups)).astype(jnp.bfloat16),
+                "dp",
+                scatter_dimension=1,
+                tiled=True,
+            )
+            moe_send, extra_back = lax.optimization_barrier(
+                (mixture.astype(jnp.bfloat16), extra_back)
+            )
             moe_rows.append(lax.psum_scatter(moe_send, "dp", scatter_dimension=1, tiled=True))
     moe_back = jnp.concatenate(moe_rows, axis=0)
-    moe_rounded = moe_back[:col_tokens].astype(jnp.float32).astype(jnp.bfloat16)
+    moe_rounded = moe_back.astype(jnp.float32).astype(jnp.bfloat16)
     resid = jnp.concatenate(reduced_parts, axis=0)
     hidden_out = (resid.astype(jnp.float32) + moe_rounded.astype(jnp.float32)).astype(jnp.bfloat16)
-    last_moe = moe_back[col_tokens:].reshape(REQS, width)
+    last_moe = extra_back.reshape(REQS, width)
     last_resid = sum(part.astype(jnp.float32) for part in last_resid_parts)
     last_hidden = (last_resid + last_moe.astype(jnp.float32)).astype(jnp.bfloat16)
     ends = rms_scale(last_hidden.astype(jnp.float32), closing_gain).astype(jnp.bfloat16)

time: 567 us -> 573 us (1.011)
  waiting for transfers between devices: 346 us -> 353 us
    unnamed x11 -> x13, waiting for transfers between devices: 108 us -> 148 us
    all_to_all x2, waiting for transfers between devices: 104 us -> 71.8 us  [shards(): lax.all_to_all(shares_out, 'expert', split_axis=0, concat_axis=0, tiled=T...]
    unnamed x46 -> x44, local copies, waits for them, and re-layouts: 16.6 us -> 14.8 us
  transfers between devices with their start and end apart: 11 -> 12, of which waited for: 9 -> 11; matrix products, arithmetic and copies ran while one was open for 19% -> 18% of each run, Pallas kernels for 0% -> 0%
where the time goes in v12:
time: 573 us; the launch traced here: 563 us
  waiting for transfers between devices  353 us (62%)
  matrix products  97.7 us (17%)
  local copies, waits for them, and re-layouts  52.8 us (9%)
  starting transfers between devices  19.7 us (3%)
  other arithmetic  16.4 us (3%)
  between operations  14.9 us (3%)
  blocking collectives  9.15 us (2%)
    unnamed x13, waiting for transfers between devices  148 us
    all_to_all x2, waiting for transfers between devices, shards(): lax.all_to_all(shares_out, 'expert', split_axis=0, concat_axis=0, tiled=T...  71.8 us
    all_gather x1, waiting for transfers between devices, shards(): gathered_rows = lax.all_gather(hidden, 'dp', axis=1, tiled=True)  46.6 us
    all_gather x2, waiting for transfers between devices, shards(): column_h = lax.all_gather(resid_h, 'dp', axis=1, tiled=True)  44.8 us
    all_to_all x2, waiting for transfers between devices, shards(): lax.all_to_all(outgoing, 'expert', split_axis=0, concat_axis=0, tiled=True)  41.6 us
    dot_general x2, matrix products, shards(): jnp.dot(activated, down_weight, preferred_element_type=jnp.float32)  33.6 us
    dot_general x2, matrix products, shards(): up_part = jnp.dot(rows_in, up_weight, preferred_element_type=jnp.float32)  20.7 us
    unnamed x44, local copies, waits for them, and re-layouts  14.8 us
  transfers between devices with their start and end apart: 12, of which 11 were waited for; matrix products, arithmetic and copies ran while one was open for 18% of the time, Pallas kernels for 0%

profile of v12, /device:TPU:0, one launch (start us, length us, event | category | flops | bytes accessed | tf_op | source)
XLA Modules:
  0.0 563.4 jit_solution(12358124955838175695)
XLA Ops:
  8.0 0.8 exp.21
  9.4 0.8 compare_reduce_fusion
  13.7 46.6 %all-gather.7.cloned.1.call-done = bf16[384,2880]{0,1:T(8,128)(2,1)} async-done(((bf16[384,720]{0,1:T(8,128)(2,1)}), bf16[384,2880]{0,1:T(8,128)(2,1)}) %all-gather.7.cloned.1.call-update) | async-done | bytes 2211856 | tf_op jit(solution)/shard_map/all_gather | solution.py:103
  60.4 2.2 fusion.12
  62.6 5.9 %fusion.22 = f32[384,640]{1,0:T(8,128)} fusion(bf16[2880,1,640]{2,0,1:T(8,128)(2,1)} %param.29, bf16[384,2880]{0,1:T(8,128)(2,1)} %all-gather.7.cloned.1.call-done, f32[2880]{0:T(1024)S(1)} %copy-done.13, f32[384]{0:T(512)S(1)} %add_rsqrt_fusion), kind=kOutput, calls=%fused_computation.37 | convolution fusion | flops 1420001280 | bytes 6894336 | tf_op jit(solution)/shard_map/dot_general | solution.py:108
  68.5 4.8 fusion.56
  73.3 2.5 copy.64
  75.8 0.9 slice_bitcast_fusion.1
  76.7 1.2 slice_bitcast_fusion
  78.3 1.3 fusion.19
  79.6 2.2 fusion.59
  82.3 1.7 convolution_convert_fusion.4
  84.4 2.9 fusion.136
  88.1 37.7 %reduce-scatter.16.cloned.1.call-done = bf16[896,192]{1,0:T(8,128)(2,1)} async-done(((bf16[3584,192]{1,0:T(8,128)(2,1)}), bf16[896,192]{1,0:T(8,128)(2,1)}) %reduce-scatter.16.cloned.1.call-update) | async-done | bytes 344080
  125.8 0.8 slice.170
  126.6 1.0 slice.168
  127.9 1.0 fusion.63
  128.9 0.8 fusion.138
  130.1 1.7 reduce-window.29
  132.7 3.4 scatter_custom_fusion.1
  136.0 22.6 %all-gather.11.cloned.1.call-done = bf16[4,720,192]{1,2,0:T(8,128)(2,1)} async-done(((bf16[1,720,192]{1,2,0:T(8,128)(2,1)}), bf16[4,720,192]{1,2,0:T(8,128)(2,1)}) %all-gather.11.cloned.1.call-update) | async-done | bytes 1105936 | tf_op jit(solution)/shard_map/all_gather | solution.py:205
  158.6 2.2 copy.75
  160.8 1.0 reshape.555
  162.5 4.5 convolution_convert_fusion.1
  166.9 4.7 all-to-all-start
  172.5 41.0 %reduce-scatter.18.cloned.1.call-done = bf16[896,192]{1,0:T(8,128)(2,1)} async-done(((bf16[3584,192]{1,0:T(8,128)(2,1)}), bf16[896,192]{1,0:T(8,128)(2,1)}) %reduce-scatter.18.cloned.1.call-update) | async-done | bytes 344080
  213.5 0.8 slice.174
  214.4 1.0 slice.172
  215.6 1.0 fusion.62
  216.6 0.8 fusion.139
  217.8 1.7 reduce-window.25
  220.4 3.8 scatter_custom_fusion
  224.2 22.2 %all-gather.9.cloned.1.call-done = bf16[4,720,192]{1,2,0:T(8,128)(2,1)} async-done(((bf16[1,720,192]{1,2,0:T(8,128)(2,1)}), bf16[4,720,192]{1,2,0:T(8,128)(2,1)}) %all-gather.9.cloned.1.call-update) | async-done | bytes 1105936 | tf_op jit(solution)/shard_map/all_gather | solution.py:205
  246.4 3.2 copy.72
  249.6 2.7 reshape.553
  253.0 4.4 convolution_convert_fusion
  257.4 4.7 all-to-all-start.1
  262.1 10.4 %fusion.4 = f32[1024,720]{0,1:T(8,128)} fusion(bf16[1024,2944]{1,0:T(8,128)(2,1)} %bitcast.45, bf16[1,2880,720]{1,2,0:T(8,128)(2,1)} %param.38), kind=kOutput, calls=%fused_computation.16 | convolution fusion | flops 4246732800 | bytes 13125632 | tf_op jit(solution)/shard_map/dot_general | solution.py:238
  272.5 16.8 %convolution_convert_fusion.2 = bf16[1024,2944]{1,0:T(8,128)(2,1)} fusion(bf16[720,2880]{1,0:T(8,128)(2,1)} %bitcast.189, f32[1024,720]{0,1:T(8,128)} %fusion.4, bf16[1,2880,720]{1,2,0:T(8,128)(2,1)} %param.37, bf16[1024,2944]{1,0:T(8,128)(2,1)} %bitcast.45), kind=kOutput, calls=%fused_computation.12 | convolution fusion | flops 8596750336 | bytes 23302144 | tf_op jit(solution)/shard_map/dot_general | solution.py:243
  289.3 41.6 %all-to-all-done.1 = bf16[8,128,2944]{2,1,0:T(8,128)(2,1)} async-done(((bf16[8,128,2944]{2,1,0:T(8,128)(2,1)}), bf16[8,128,2944]{2,1,0:T(8,128)(2,1)}, u32[]{:S(2)}, u32[]{:S(2)}) %all-to-all-start.1) | async-done | bytes 6029344 | tf_op jit(solution)/shard_map/all_to_all | solution.py:231
  330.9 4.9 all-to-all-start.2
  336.4 10.4 %fusion.8 = f32[1024,720]{0,1:T(8,128)} fusion(bf16[1024,2944]{1,0:T(8,128)(2,1)} %bitcast.40, bf16[1,2880,720]{1,2,0:T(8,128)(2,1)} %param.38), kind=kOutput, calls=%fused_computation.20 | convolution fusion | flops 4246732800 | bytes 13125632 | tf_op jit(solution)/shard_map/dot_general | solution.py:238
  346.8 16.8 %convolution_convert_fusion.3 = bf16[1024,2944]{1,0:T(8,128)(2,1)} fusion(bf16[720,2880]{1,0:T(8,128)(2,1)} %bitcast.190, f32[1024,720]{0,1:T(8,128)} %fusion.8, bf16[1,2880,720]{1,2,0:T(8,128)(2,1)} %param.37, bf16[1024,2944]{1,0:T(8,128)(2,1)} %bitcast.40), kind=kOutput, calls=%fused_computation.13 | convolution fusion | flops 8596750336 | bytes 23302144 | tf_op jit(solution)/shard_map/dot_general | solution.py:243
  363.6 41.1 %all-to-all-done.2 = bf16[8,128,2944]{2,1,0:T(8,128)(2,1)} async-done(((bf16[8,128,2944]{2,1,0:T(8,128)(2,1)}), bf16[8,128,2944]{2,1,0:T(8,128)(2,1)}, u32[]{:S(2)}, u32[]{:S(2)}) %all-to-all-start.2) | async-done | bytes 6029344 | tf_op jit(solution)/shard_map/all_to_all | solution.py:251
  404.7 5.9 %fusion.140 = (bf16[192,2880]{1,0:T(8,128)(2,1)}, f32[192,2880]{1,0:T(8,128)}) fusion(bf16[192,1024]{1,0:T(8,128)(2,1)S(1)} %fusion.51, bf16[1024,2944]{1,0:T(8,128)(2,1)} %bitcast.47), kind=kOutput, calls=%fused_computation.215 | convolution fusion | flops 1133015040 | bytes 9740288 | tf_op jit(solution)/shard_map/dot_general | solution.py:263
  410.5 4.7 all-to-all-start.3
  415.3 2.5 copy.88
  418.6 2.2 gather_fusion
  420.8 30.6 %reduce-scatter.20.cloned.1.call-done = bf16[720,192]{1,0:T(8,128)(2,1)} async-done(((bf16[2880,192]{1,0:T(8,128)(2,1)}), bf16[720,192]{1,0:T(8,128)(2,1)}) %reduce-scatter.20.cloned.1.call-update) | async-done | bytes 276496
  451.4 1.8 copy.89
  453.3 30.8 %all-to-all-done.3 = bf16[8,128,2944]{2,1,0:T(8,128)(2,1)} async-done(((bf16[8,128,2944]{2,1,0:T(8,128)(2,1)}), bf16[8,128,2944]{2,1,0:T(8,128)(2,1)}, u32[]{:S(2)}, u32[]{:S(2)}) %all-to-all-start.3) | async-done | bytes 6029344 | tf_op jit(solution)/shard_map/all_to_all | solution.py:251
  484.0 5.8 %fusion.141 = (bf16[192,2880]{1,0:T(8,128)(2,1)}, f32[192,2880]{1,0:T(8,128)}) fusion(bf16[192,1024]{1,0:T(8,128)(2,1)S(1)} %fusion.50, bf16[1024,2944]{1,0:T(8,128)(2,1)} %bitcast.48), kind=kOutput, calls=%fused_computation.216 | convolution fusion | flops 1133015040 | bytes 9740288 | tf_op jit(solution)/shard_map/dot_general | solution.py:263
  489.9 2.2 gather_fusion.1
  492.5 1.0 tile.2.clone
  493.5 20.4 %reduce-scatter.22.cloned.1.call-done = bf16[720,16]{1,0:T(8,128)(2,1)} async-done(((bf16[2880,16]{1,0:T(8,128)(2,1)}), bf16[720,16]{1,0:T(8,128)(2,1)}) %reduce-scatter.22.cloned.1.call-update) | async-done | bytes 23056
  513.9 1.0 copy.91
  514.9 2.5 copy.92
  519.0 9.2 %all-gather.2 = bf16[8,4,2880]{2,1,0:T(4,128)(2,1)S(1)} all-gather(bf16[1,4,2880]{2,1,0:T(4,128)(2,1)S(1)} %fusion.108), channel_id=1, replica_groups=mesh['dp'=4,'expert'=8] {'expert'}, dimensions={0}, use_global_device_ids=true | all-gather | bytes 207360 | tf_op jit(solution)/shard_map/all_gather | solution.py:298
  528.2 0.8 reshape.557
  528.9 4.6 fusion.142
  533.6 16.8 %reduce-scatter.24.cloned.1.call-done = bf16[720,192]{1,0:T(8,128)(2,1)} async-done(((bf16[2880,192]{1,0:T(8,128)(2,1)}), bf16[720,192]{1,0:T(8,128)(2,1)}) %reduce-scatter.24.cloned.1.call-update) | async-done | bytes 276496
  550.4 1.9 copy.93
  552.3 2.0 add_convert_fusion
  554.3 2.1 copy.80
  (129 shorter events, 15.2 us)
Async XLA Ops:
  7.2 75.2 %copy-start = (bf16[512,2880]{0,1:T(8,128)(2,1)S(1)}, bf16[512,2880]{0,1:T(8,128)(2,1)}, u32[]{:S(2)}) copy-start(bf16[512,2880]{0,1:T(8,128)(2,1)} %param.31) | copy-start | bytes 8847364
  7.2 55.4 %copy-start.13 = (f32[2880]{0:T(1024)S(1)}, f32[2880]{0:T(1024)}, u32[]{:S(2)}) copy-start(f32[2880]{0:T(1024)} %param.28) | copy-start | bytes 34564
  7.2 53.2 %all-gather.7.cloned.1.call-start = ((), (), s32[]{:S(2)}) async-start(), calls=%async_computation.9 | async-start | bytes 2764800 | tf_op jit(solution)/shard_map/all_gather | solution.py:103
  7.9 117.9 %reduce-scatter.16.cloned.1.call-start = ((), (), s32[]{:S(2)}) async-start(), calls=%async_computation.12 | async-start | bytes 2293760
  12.4 0.9 copy-start.7
  62.6 5.9 %copy-start.12 = (bf16[128,1,640]{2,0,1:T(8,128)(2,1)S(1)}, bf16[128,1,640]{2,0,1:T(8,128)(2,1)}, u32[]{:S(2)}) copy-start(bf16[128,1,640]{2,0,1:T(8,128)(2,1)} %param.33) | copy-start | bytes 491524
  79.6 2.3 copy-start.9
  82.3 1.7 copy-start.8
  84.4 3.2 copy-start.2
  87.4 40.6 %copy-start.5 = (bf16[128,720]{0,1:T(8,128)(2,1)S(1)}, bf16[128,720]{0,1:T(8,128)(2,1)}, u32[]{:S(2)}) copy-start(bf16[128,720]{0,1:T(8,128)(2,1)} %param.35) | copy-start | bytes 552964
  87.4 71.3 %all-gather.11.cloned.1.call-start = ((), (), s32[]{:S(2)}) async-start(), calls=%async_computation.11 | async-start | bytes 1474560 | tf_op jit(solution)/shard_map/all_gather | solution.py:205
  132.5 29.6 %copy-start.10 = (f32[2880]{0:T(1024)S(1)}, f32[2880]{0:T(1024)}, u32[]{:S(2)}) copy-start(f32[2880]{0:T(1024)} %param.36) | copy-start | bytes 34564
  166.9 85.4 %all-to-all-start = ((bf16[8,128,2944]{2,1,0:T(8,128)(2,1)}), bf16[8,128,2944]{2,1,0:T(8,128)(2,1)}, u32[]{:S(2)}, u32[]{:S(2)}) async-start(bf16[8,128,2944]{2,1,0:T(8,128)(2,1)} %bitcast.153), calls=%async_computation | async-start | bytes 12058624 | tf_op jit(solution)/shard_map/all_to_all | solution.py:231
  171.7 44.0 %copy-start.6 = (bf16[128,720]{0,1:T(8,128)(2,1)S(1)}, bf16[128,720]{0,1:T(8,128)(2,1)}, u32[]{:S(2)}) copy-start(bf16[128,720]{0,1:T(8,128)(2,1)} %param.35) | copy-start | bytes 552964
  171.7 41.8 %reduce-scatter.18.cloned.1.call-start = ((), (), s32[]{:S(2)}) async-start(), calls=%async_computation.13 | async-start | bytes 2293760
  172.3 74.1 %all-gather.9.cloned.1.call-start = ((), (), s32[]{:S(2)}) async-start(), calls=%async_computation.10 | async-start | bytes 1474560 | tf_op jit(solution)/shard_map/all_gather | solution.py:205
  257.4 73.5 %all-to-all-start.1 = ((bf16[8,128,2944]{2,1,0:T(8,128)(2,1)}), bf16[8,128,2944]{2,1,0:T(8,128)(2,1)}, u32[]{:S(2)}, u32[]{:S(2)}) async-start(bf16[8,128,2944]{2,1,0:T(8,128)(2,1)} %bitcast.154), calls=%async_computation.1 | async-start | bytes 12058624 | tf_op jit(solution)/shard_map/all_to_all | solution.py:231
  330.9 73.7 %all-to-all-start.2 = ((bf16[8,128,2944]{2,1,0:T(8,128)(2,1)}), bf16[8,128,2944]{2,1,0:T(8,128)(2,1)}, u32[]{:S(2)}, u32[]{:S(2)}) async-start(bf16[8,128,2944]{2,1,0:T(8,128)(2,1)} %bitcast.162), calls=%async_computation.2 | async-start | bytes 12058624 | tf_op jit(solution)/shard_map/all_to_all | solution.py:251
  410.5 73.5 %all-to-all-start.3 = ((bf16[8,128,2944]{2,1,0:T(8,128)(2,1)}), bf16[8,128,2944]{2,1,0:T(8,128)(2,1)}, u32[]{:S(2)}, u32[]{:S(2)}) async-start(bf16[8,128,2944]{2,1,0:T(8,128)(2,1)} %bitcast.161), calls=%async_computation.3 | async-start | bytes 12058624 | tf_op jit(solution)/shard_map/all_to_all | solution.py:251
  415.3 36.2 %reduce-scatter.20.cloned.1.call-start = ((), (), s32[]{:S(2)}) async-start(), calls=%async_computation.14 | async-start | bytes 1843200
  417.8 96.0 %reduce-scatter.22.cloned.1.call-start = ((), (), s32[]{:S(2)}) async-start(), calls=%async_computation.15 | async-start | bytes 921600
  493.4 25.5 %copy-start.11 = (f32[2880]{0:T(1024)S(1)}, f32[2880]{0:T(1024)}, u32[]{:S(2)}) copy-start(f32[2880]{0:T(1024)} %param.40) | copy-start | bytes 34564
  493.5 56.9 %reduce-scatter.24.cloned.1.call-start = ((), (), s32[]{:S(2)}) async-start(), calls=%async_computation.16 | async-start | bytes 1843200
  528.2 24.1 %copy-start.3 = (bf16[192,720]{1,0:T(8,128)(2,1)S(1)}, bf16[192,720]{1,0:T(8,128)(2,1)}, u32[]{:S(2)}) copy-start(bf16[192,720]{1,0:T(8,128)(2,1)} %fusion.63) | copy-start | bytes 829444
  528.2 24.1 %copy-start.4 = (bf16[192,720]{1,0:T(8,128)(2,1)S(1)}, bf16[192,720]{1,0:T(8,128)(2,1)}, u32[]{:S(2)}) copy-start(bf16[192,720]{1,0:T(8,128)(2,1)} %fusion.62) | copy-start | bytes 829444
  528.9 27.4 %copy-start.1 = (bf16[512,2880]{0,1:T(8,128)(2,1)S(1)}, bf16[512,2880]{0,1:T(8,128)(2,1)}, u32[]{:S(2)}) copy-start(bf16[512,2880]{0,1:T(8,128)(2,1)} %param.31) | copy-start | bytes 8847364
Sparse Core Ops, SparseCore 0:
  9.6 50.7 all-gather.6
  87.5 38.2 reduce-scatter.15
  129.0 29.5 all-gather.10
  174.5 38.9 reduce-scatter.17
  216.8 29.5 all-gather.8
  418.1 33.2 reduce-scatter.19
  493.6 20.2 reduce-scatter.21
  517.6 32.8 reduce-scatter.23

commit v13 on v7

--- a/solution.py
+++ b/solution.py
@@ -202,7 +202,11 @@
         joined_h = reduce_rows(lo, half_tokens)
         resid_h, pack_h = resid_rows(joined_h, lo, half_tokens)
         reduced_parts.append(resid_h)
-        column_h = lax.all_gather(resid_h, "dp", axis=1, tiled=True)
+        column_h = (
+            lax.all_gather(resid_h, "dp", axis=0, tiled=False)
+            .transpose(1, 0, 2)
+            .reshape(half_tokens, groups * quarter)
+        )
         if held is not None:
             column_h, held = lax.optimization_barrier((column_h, held))
         moe_in = rms_scale(column_h.astype(jnp.float32), expert_norm_gain).astype(jnp.bfloat16)

time: 567 us -> 571 us (level)
    transpose x0 -> x2, local copies, waits for them, and re-layouts: none -> 6.42 us  [shards(): column_h = lax.all_gather(resid_h, 'dp', axis=0, tiled=False).transpose(1...]
    unnamed x46 -> x44, local copies, waits for them, and re-layouts: 16.6 us -> 12.9 us
where the time goes in v13:
time: 571 us; the launch traced here: 561 us
  waiting for transfers between devices  346 us (61%)
  matrix products  97.7 us (17%)
  local copies, waits for them, and re-layouts  53.6 us (9%)
  other arithmetic  20.2 us (4%)
  starting transfers between devices  19.7 us (3%)
  between operations  15.2 us (3%)
  blocking collectives  9.25 us (2%)
    unnamed x11, waiting for transfers between devices  108 us
    all_to_all x2, waiting for transfers between devices, shards(): lax.all_to_all(shares_out, 'expert', split_axis=0, concat_axis=0, tiled=T...  104 us
    all_gather x1, waiting for transfers between devices, shards(): gathered_rows = lax.all_gather(hidden, 'dp', axis=1, tiled=True)  46.6 us
    all_gather x2, waiting for transfers between devices, shards(): lax.all_gather(resid_h, 'dp', axis=0, tiled=False).transpose(1, 0, 2)  45 us
    all_to_all x2, waiting for transfers between devices, shards(): lax.all_to_all(outgoing, 'expert', split_axis=0, concat_axis=0, tiled=True)  41.6 us
    dot_general x2, matrix products, shards(): jnp.dot(activated, down_weight, preferred_element_type=jnp.float32)  33.6 us
    dot_general x2, matrix products, shards(): up_part = jnp.dot(rows_in, up_weight, preferred_element_type=jnp.float32)  20.7 us
    unnamed x44, local copies, waits for them, and re-layouts  12.9 us
  transfers between devices with their start and end apart: 11, of which 9 were waited for; matrix products, arithmetic and copies ran while one was open for 19% of the time, Pallas kernels for 0%

profile of v13, /device:TPU:0, one launch (start us, length us, event | category | flops | bytes accessed | tf_op | source)
XLA Modules:
  0.0 561.3 jit_solution(1387218645051442600)
XLA Ops:
  8.0 0.8 exp.21
  9.4 0.8 compare_reduce_fusion
  12.5 0.7 select_reduce_fusion.1
  13.7 46.6 %all-gather.7.cloned.1.call-done = bf16[384,2880]{0,1:T(8,128)(2,1)} async-done(((bf16[384,720]{0,1:T(8,128)(2,1)}), bf16[384,2880]{0,1:T(8,128)(2,1)}) %all-gather.7.cloned.1.call-update) | async-done | bytes 2211856 | tf_op jit(solution)/shard_map/all_gather | solution.py:103
  60.4 2.2 fusion.12
  62.6 5.9 %fusion.22 = f32[384,640]{1,0:T(8,128)} fusion(bf16[2880,1,640]{2,0,1:T(8,128)(2,1)} %param.29, bf16[384,2880]{0,1:T(8,128)(2,1)} %all-gather.7.cloned.1.call-done, f32[2880]{0:T(1024)S(1)} %copy-done.14, f32[384]{0:T(512)S(1)} %add_rsqrt_fusion), kind=kOutput, calls=%fused_computation.37 | convolution fusion | flops 1420001280 | bytes 6894336 | tf_op jit(solution)/shard_map/dot_general | solution.py:108
  68.5 4.8 fusion.53
  73.3 2.5 copy.66
  75.8 0.9 slice_bitcast_fusion.1
  76.7 1.2 slice_bitcast_fusion
  78.3 1.3 fusion.19
  79.6 2.2 fusion.56
  82.4 1.7 convolution_convert_fusion.4
  84.4 2.9 fusion.133
  88.1 37.7 %reduce-scatter.13.cloned.1.call-done = bf16[896,192]{1,0:T(8,128)(2,1)} async-done(((bf16[3584,192]{1,0:T(8,128)(2,1)}), bf16[896,192]{1,0:T(8,128)(2,1)}) %reduce-scatter.13.cloned.1.call-update) | async-done | bytes 344080
  125.8 0.8 slice.178
  126.6 1.0 slice.176
  127.9 1.0 fusion.60
  128.9 0.8 fusion.135
  130.1 1.7 reduce-window.29
  132.7 3.4 scatter_custom_fusion.1
  136.1 22.6 %all-gather.11.cloned.1.call-done = bf16[768,720]{1,0:T(8,128)(2,1)} async-done(((bf16[192,720]{1,0:T(8,128)(2,1)}), bf16[768,720]{1,0:T(8,128)(2,1)}) %all-gather.11.cloned.1.call-update) | async-done | bytes 1105936 | tf_op jit(solution)/shard_map/all_gather | solution.py:206
  158.7 1.6 multiply_reduce_fusion
  160.3 3.2 copy.77
  163.5 2.7 reshape.496
  166.6 4.5 convolution_convert_fusion.1
  171.0 4.7 all-to-all-start
  176.6 41.0 %reduce-scatter.15.cloned.1.call-done = bf16[896,192]{1,0:T(8,128)(2,1)} async-done(((bf16[3584,192]{1,0:T(8,128)(2,1)}), bf16[896,192]{1,0:T(8,128)(2,1)}) %reduce-scatter.15.cloned.1.call-update) | async-done | bytes 344080
  217.6 0.8 slice.182
  218.4 1.0 slice.180
  219.7 1.0 fusion.59
  220.7 0.8 fusion.136
  221.9 1.7 reduce-window.25
  224.4 3.6 scatter_custom_fusion
  228.0 22.4 %all-gather.9.cloned.1.call-done = bf16[768,720]{1,0:T(8,128)(2,1)} async-done(((bf16[192,720]{1,0:T(8,128)(2,1)}), bf16[768,720]{1,0:T(8,128)(2,1)}) %all-gather.9.cloned.1.call-update) | async-done | bytes 1105936 | tf_op jit(solution)/shard_map/all_gather | solution.py:206
  250.5 3.2 copy.74
  253.6 2.7 reshape.494
  257.1 4.4 convolution_convert_fusion
  261.5 4.7 all-to-all-start.1
  266.2 10.4 %fusion.4 = f32[1024,720]{0,1:T(8,128)} fusion(bf16[1024,2944]{1,0:T(8,128)(2,1)} %bitcast.44, bf16[1,2880,720]{1,2,0:T(8,128)(2,1)} %param.38), kind=kOutput, calls=%fused_computation.16 | convolution fusion | flops 4246732800 | bytes 13125632 | tf_op jit(solution)/shard_map/dot_general | solution.py:242
  276.6 16.8 %convolution_convert_fusion.2 = bf16[1024,2944]{1,0:T(8,128)(2,1)} fusion(bf16[720,2880]{1,0:T(8,128)(2,1)} %bitcast.172, f32[1024,720]{0,1:T(8,128)} %fusion.4, bf16[1,2880,720]{1,2,0:T(8,128)(2,1)} %param.37, bf16[1024,2944]{1,0:T(8,128)(2,1)} %bitcast.44), kind=kOutput, calls=%fused_computation.12 | convolution fusion | flops 8596750336 | bytes 23302144 | tf_op jit(solution)/shard_map/dot_general | solution.py:247
  293.4 41.6 %all-to-all-done.1 = bf16[8,128,2944]{2,1,0:T(8,128)(2,1)} async-done(((bf16[8,128,2944]{2,1,0:T(8,128)(2,1)}), bf16[8,128,2944]{2,1,0:T(8,128)(2,1)}, u32[]{:S(2)}, u32[]{:S(2)}) %all-to-all-start.1) | async-done | bytes 6029344 | tf_op jit(solution)/shard_map/all_to_all | solution.py:235
  335.0 5.0 all-to-all-start.2
  340.5 10.4 %fusion.8 = f32[1024,720]{0,1:T(8,128)} fusion(bf16[1024,2944]{1,0:T(8,128)(2,1)} %bitcast.39, bf16[1,2880,720]{1,2,0:T(8,128)(2,1)} %param.38), kind=kOutput, calls=%fused_computation.20 | convolution fusion | flops 4246732800 | bytes 13125632 | tf_op jit(solution)/shard_map/dot_general | solution.py:242
  350.9 16.8 %convolution_convert_fusion.3 = bf16[1024,2944]{1,0:T(8,128)(2,1)} fusion(bf16[720,2880]{1,0:T(8,128)(2,1)} %bitcast.173, f32[1024,720]{0,1:T(8,128)} %fusion.8, bf16[1,2880,720]{1,2,0:T(8,128)(2,1)} %param.37, bf16[1024,2944]{1,0:T(8,128)(2,1)} %bitcast.39), kind=kOutput, calls=%fused_computation.13 | convolution fusion | flops 8596750336 | bytes 23302144 | tf_op jit(solution)/shard_map/dot_general | solution.py:247
  367.8 41.1 %all-to-all-done.2 = bf16[8,128,2944]{2,1,0:T(8,128)(2,1)} async-done(((bf16[8,128,2944]{2,1,0:T(8,128)(2,1)}), bf16[8,128,2944]{2,1,0:T(8,128)(2,1)}, u32[]{:S(2)}, u32[]{:S(2)}) %all-to-all-start.2) | async-done | bytes 6029344 | tf_op jit(solution)/shard_map/all_to_all | solution.py:255
  408.8 5.8 %fusion.137 = (bf16[192,2880]{1,0:T(8,128)(2,1)}, f32[192,2880]{1,0:T(8,128)}) fusion(bf16[192,1024]{1,0:T(8,128)(2,1)S(1)} %fusion.48, bf16[1024,2944]{1,0:T(8,128)(2,1)} %bitcast.46), kind=kOutput, calls=%fused_computation.215 | convolution fusion | flops 1133015040 | bytes 9740288 | tf_op jit(solution)/shard_map/dot_general | solution.py:265
  414.7 4.7 all-to-all-start.3
  419.5 2.5 copy.90
  422.7 2.2 gather_fusion
  425.0 63.2 %all-to-all-done.3 = bf16[8,128,2944]{2,1,0:T(8,128)(2,1)} async-done(((bf16[8,128,2944]{2,1,0:T(8,128)(2,1)}), bf16[8,128,2944]{2,1,0:T(8,128)(2,1)}, u32[]{:S(2)}, u32[]{:S(2)}) %all-to-all-start.3) | async-done | bytes 6029344 | tf_op jit(solution)/shard_map/all_to_all | solution.py:255
  488.2 6.0 %fusion.138 = (bf16[192,2880]{1,0:T(8,128)(2,1)}, f32[192,2880]{1,0:T(8,128)}) fusion(bf16[192,1024]{1,0:T(8,128)(2,1)S(1)} %fusion.47, bf16[1024,2944]{1,0:T(8,128)(2,1)} %bitcast.47), kind=kOutput, calls=%fused_computation.216 | convolution fusion | flops 1133015040 | bytes 9740288 | tf_op jit(solution)/shard_map/dot_general | solution.py:265
  494.2 2.2 gather_fusion.1
  496.8 2.4 pad_maximum_fusion.1
  499.1 2.6 copy.92
  502.9 1.9 copy.91
  504.8 28.2 %reduce-scatter.19.cloned.1.call-done = bf16[720,208]{1,0:T(8,128)(2,1)} async-done(((bf16[2880,208]{1,0:T(8,128)(2,1)}), bf16[720,208]{1,0:T(8,128)(2,1)}) %reduce-scatter.19.cloned.1.call-update) | async-done | bytes 299536
  533.0 1.1 copy.93
  534.1 0.7 copy-done.5
  535.3 9.3 %all-gather.2 = bf16[8,4,2880]{2,1,0:T(4,128)(2,1)S(1)} all-gather(bf16[1,4,2880]{2,1,0:T(4,128)(2,1)S(1)} %fusion.105), channel_id=1, replica_groups=mesh['dp'=4,'expert'=8] {'expert'}, dimensions={0}, use_global_device_ids=true | all-gather | bytes 207360 | tf_op jit(solution)/shard_map/all_gather | solution.py:294
  544.5 0.8 reshape.562
  545.3 2.2 add_convert_fusion
  547.5 2.1 copy.82
  549.5 4.5 fusion.139
  (129 shorter events, 14.0 us)
Async XLA Ops:
  7.2 75.2 %copy-start = (bf16[512,2880]{0,1:T(8,128)(2,1)S(1)}, bf16[512,2880]{0,1:T(8,128)(2,1)}, u32[]{:S(2)}) copy-start(bf16[512,2880]{0,1:T(8,128)(2,1)} %param.31) | copy-start | bytes 8847364
  7.2 55.4 %copy-start.14 = (f32[2880]{0:T(1024)S(1)}, f32[2880]{0:T(1024)}, u32[]{:S(2)}) copy-start(f32[2880]{0:T(1024)} %param.28) | copy-start | bytes 34564
  7.2 53.2 %all-gather.7.cloned.1.call-start = ((), (), s32[]{:S(2)}) async-start(), calls=%async_computation.8 | async-start | bytes 2764800 | tf_op jit(solution)/shard_map/all_gather | solution.py:103
  7.9 117.9 %reduce-scatter.13.cloned.1.call-start = ((), (), s32[]{:S(2)}) async-start(), calls=%async_computation.11 | async-start | bytes 2293760
  12.4 0.9 copy-start.8
  62.6 5.9 %copy-start.13 = (bf16[128,1,640]{2,0,1:T(8,128)(2,1)S(1)}, bf16[128,1,640]{2,0,1:T(8,128)(2,1)}, u32[]{:S(2)}) copy-start(bf16[128,1,640]{2,0,1:T(8,128)(2,1)} %param.33) | copy-start | bytes 491524
  79.6 2.3 copy-start.10
  82.3 1.7 copy-start.9
  84.4 3.2 copy-start.2
  87.4 40.6 %copy-start.6 = (bf16[128,720]{0,1:T(8,128)(2,1)S(1)}, bf16[128,720]{0,1:T(8,128)(2,1)}, u32[]{:S(2)}) copy-start(bf16[128,720]{0,1:T(8,128)(2,1)} %param.35) | copy-start | bytes 552964
  87.4 71.3 %all-gather.11.cloned.1.call-start = ((), (), s32[]{:S(2)}) async-start(), calls=%async_computation.10 | async-start | bytes 1474560 | tf_op jit(solution)/shard_map/all_gather | solution.py:206
  132.6 33.6 %copy-start.11 = (f32[2880]{0:T(1024)S(1)}, f32[2880]{0:T(1024)}, u32[]{:S(2)}) copy-start(f32[2880]{0:T(1024)} %param.36) | copy-start | bytes 34564
  171.0 85.3 %all-to-all-start = ((bf16[8,128,2944]{2,1,0:T(8,128)(2,1)}), bf16[8,128,2944]{2,1,0:T(8,128)(2,1)}, u32[]{:S(2)}, u32[]{:S(2)}) async-start(bf16[8,128,2944]{2,1,0:T(8,128)(2,1)} %bitcast.141), calls=%async_computation | async-start | bytes 12058624 | tf_op jit(solution)/shard_map/all_to_all | solution.py:235
  175.8 43.9 %copy-start.7 = (bf16[128,720]{0,1:T(8,128)(2,1)S(1)}, bf16[128,720]{0,1:T(8,128)(2,1)}, u32[]{:S(2)}) copy-start(bf16[128,720]{0,1:T(8,128)(2,1)} %param.35) | copy-start | bytes 552964
  175.8 41.8 %reduce-scatter.15.cloned.1.call-start = ((), (), s32[]{:S(2)}) async-start(), calls=%async_computation.12 | async-start | bytes 2293760
  176.4 74.1 %all-gather.9.cloned.1.call-start = ((), (), s32[]{:S(2)}) async-start(), calls=%async_computation.9 | async-start | bytes 1474560 | tf_op jit(solution)/shard_map/all_gather | solution.py:206
  261.5 73.5 %all-to-all-start.1 = ((bf16[8,128,2944]{2,1,0:T(8,128)(2,1)}), bf16[8,128,2944]{2,1,0:T(8,128)(2,1)}, u32[]{:S(2)}, u32[]{:S(2)}) async-start(bf16[8,128,2944]{2,1,0:T(8,128)(2,1)} %bitcast.142), calls=%async_computation.1 | async-start | bytes 12058624 | tf_op jit(solution)/shard_map/all_to_all | solution.py:235
  335.0 73.8 %all-to-all-start.2 = ((bf16[8,128,2944]{2,1,0:T(8,128)(2,1)}), bf16[8,128,2944]{2,1,0:T(8,128)(2,1)}, u32[]{:S(2)}, u32[]{:S(2)}) async-start(bf16[8,128,2944]{2,1,0:T(8,128)(2,1)} %bitcast.146), calls=%async_computation.2 | async-start | bytes 12058624 | tf_op jit(solution)/shard_map/all_to_all | solution.py:255
  414.7 73.5 %all-to-all-start.3 = ((bf16[8,128,2944]{2,1,0:T(8,128)(2,1)}), bf16[8,128,2944]{2,1,0:T(8,128)(2,1)}, u32[]{:S(2)}, u32[]{:S(2)}) async-start(bf16[8,128,2944]{2,1,0:T(8,128)(2,1)} %bitcast.145), calls=%async_computation.3 | async-start | bytes 12058624 | tf_op jit(solution)/shard_map/all_to_all | solution.py:255
  419.4 83.5 %reduce-scatter.17.cloned.1.call-start = ((), (), s32[]{:S(2)}) async-start(), calls=%async_computation.13 | async-start | bytes 1843200
  422.0 111.0 %reduce-scatter.19.cloned.1.call-start = ((), (), s32[]{:S(2)}) async-start(), calls=%async_computation.14 | async-start | bytes 1843200
  499.1 36.1 %copy-start.12 = (f32[2880]{0:T(1024)S(1)}, f32[2880]{0:T(1024)}, u32[]{:S(2)}) copy-start(f32[2880]{0:T(1024)} %param.40) | copy-start | bytes 34564
  499.1 46.2 %copy-start.3 = (bf16[192,720]{1,0:T(8,128)(2,1)S(1)}, bf16[192,720]{1,0:T(8,128)(2,1)}, u32[]{:S(2)}) copy-start(bf16[192,720]{1,0:T(8,128)(2,1)} %fusion.60) | copy-start | bytes 829444
  499.1 46.2 %copy-start.4 = (bf16[192,720]{1,0:T(8,128)(2,1)S(1)}, bf16[192,720]{1,0:T(8,128)(2,1)}, u32[]{:S(2)}) copy-start(bf16[192,720]{1,0:T(8,128)(2,1)} %fusion.59) | copy-start | bytes 829444
  534.1 0.7 copy-start.5
  545.3 8.7 %copy-start.1 = (bf16[512,2880]{0,1:T(8,128)(2,1)S(1)}, bf16[512,2880]{0,1:T(8,128)(2,1)}, u32[]{:S(2)}) copy-start(bf16[512,2880]{0,1:T(8,128)(2,1)} %param.31) | copy-start | bytes 8847364
Sparse Core Ops, SparseCore 0:
  9.6 50.7 all-gather.6
  87.5 38.2 reduce-scatter.12
  129.0 29.5 all-gather.10
  178.6 38.9 reduce-scatter.14
  220.8 29.5 all-gather.8
  422.3 33.3 reduce-scatter.16
  501.9 31.0 reduce-scatter.18

commit v14 on v7

--- a/solution.py
+++ b/solution.py
@@ -244,11 +244,11 @@
             .astype(jnp.bfloat16)
             .reshape(experts, half_capacity, wide)
         )
+        answers = lax.all_to_all(shares_out, "expert", split_axis=0, concat_axis=0, tiled=True)
         if pending is not None:
-            shares_out, pending = lax.optimization_barrier((shares_out, pending))
             moe_rows.append(lax.psum_scatter(pending, "dp", scatter_dimension=1, tiled=True))
+            answers, moe_rows[-1] = lax.optimization_barrier((answers, moe_rows[-1]))
             pending = None
-        answers = lax.all_to_all(shares_out, "expert", split_axis=0, concat_axis=0, tiled=True)
         slot_ids = jnp.arange(experts * half_capacity, dtype=jnp.int32)
         combine = jnp.sum(
             jnp.where(

time: 567 us -> 559 us (0.986)
  waiting for transfers between devices: 346 us -> 339 us
    all_to_all x2, waiting for transfers between devices: 104 us -> 66.1 us  [shards(): lax.all_to_all(shares_out, 'expert', split_axis=0, concat_axis=0, tiled=T...]
    unnamed x11, waiting for transfers between devices: 108 us -> 139 us
    unnamed x46 -> x49, local copies, waits for them, and re-layouts: 16.6 us -> 12.3 us
  transfers between devices with their start and end apart: 11 -> 11, of which waited for: 9 -> 10; matrix products, arithmetic and copies ran while one was open for 19% -> 18% of each run, Pallas kernels for 0% -> 0%
where the time goes in v14:
time: 559 us; the launch traced here: 550 us
  waiting for transfers between devices  339 us (61%)
  matrix products  97.4 us (17%)
  local copies, waits for them, and re-layouts  50.3 us (9%)
  starting transfers between devices  19.6 us (4%)
  other arithmetic  19.2 us (3%)
  between operations  15.2 us (3%)
  blocking collectives  9.25 us (2%)
    unnamed x11, waiting for transfers between devices  139 us
    all_to_all x2, waiting for transfers between devices, shards(): lax.all_to_all(shares_out, 'expert', split_axis=0, concat_axis=0, tiled=T...  66.1 us
    all_gather x1, waiting for transfers between devices, shards(): gathered_rows = lax.all_gather(hidden, 'dp', axis=1, tiled=True)  46.6 us
    all_gather x2, waiting for transfers between devices, shards(): column_h = lax.all_gather(resid_h, 'dp', axis=1, tiled=True)  45 us
    all_to_all x2, waiting for transfers between devices, shards(): lax.all_to_all(outgoing, 'expert', split_axis=0, concat_axis=0, tiled=True)  41.6 us
    dot_general x2, matrix products, shards(): jnp.dot(activated, down_weight, preferred_element_type=jnp.float32)  33.7 us
    dot_general x2, matrix products, shards(): up_part = jnp.dot(rows_in, up_weight, preferred_element_type=jnp.float32)  20.7 us
    unnamed x49, local copies, waits for them, and re-layouts  12.3 us
  transfers between devices with their start and end apart: 11, of which 10 were waited for; matrix products, arithmetic and copies ran while one was open for 18% of the time, Pallas kernels for 0%

profile of v14, /device:TPU:0, one launch (start us, length us, event | category | flops | bytes accessed | tf_op | source)
XLA Modules:
  0.0 549.8 jit_solution(267624168265766925)
XLA Ops:
  9.4 0.8 compare_reduce_fusion
  13.7 46.6 %all-gather.7.cloned.1.call-done = bf16[384,2880]{0,1:T(8,128)(2,1)} async-done(((bf16[384,720]{0,1:T(8,128)(2,1)}), bf16[384,2880]{0,1:T(8,128)(2,1)}) %all-gather.7.cloned.1.call-update) | async-done | bytes 2211856 | tf_op jit(solution)/shard_map/all_gather | solution.py:103
  60.4 2.2 fusion.12
  62.6 5.9 %fusion.22 = f32[384,640]{1,0:T(8,128)} fusion(bf16[2880,1,640]{2,0,1:T(8,128)(2,1)} %param.29, bf16[384,2880]{0,1:T(8,128)(2,1)} %all-gather.7.cloned.1.call-done, f32[2880]{0:T(1024)S(1)} %copy-done.16, f32[384]{0:T(512)S(1)} %add_rsqrt_fusion), kind=kOutput, calls=%fused_computation.37 | convolution fusion | flops 1420001280 | bytes 6894336 | tf_op jit(solution)/shard_map/dot_general | solution.py:108
  68.5 4.8 fusion.56
  73.3 2.5 copy.64
  75.8 0.9 slice_bitcast_fusion.1
  76.7 1.2 slice_bitcast_fusion
  78.3 1.3 fusion.19
  79.6 2.2 fusion.59
  82.4 1.7 convolution_convert_fusion.4
  84.4 2.9 fusion.136
  88.1 37.7 %reduce-scatter.13.cloned.1.call-done = bf16[896,192]{1,0:T(8,128)(2,1)} async-done(((bf16[3584,192]{1,0:T(8,128)(2,1)}), bf16[896,192]{1,0:T(8,128)(2,1)}) %reduce-scatter.13.cloned.1.call-update) | async-done | bytes 344080
  125.8 0.8 slice.178
  126.6 1.0 slice.176
  127.9 1.0 fusion.63
  128.9 0.8 fusion.138
  130.1 1.7 reduce-window.29
  132.7 3.4 scatter_custom_fusion.1
  136.1 22.6 %all-gather.11.cloned.1.call-done = bf16[4,720,192]{1,2,0:T(8,128)(2,1)} async-done(((bf16[1,720,192]{1,2,0:T(8,128)(2,1)}), bf16[4,720,192]{1,2,0:T(8,128)(2,1)}) %all-gather.11.cloned.1.call-update) | async-done | bytes 1105936 | tf_op jit(solution)/shard_map/all_gather | solution.py:205
  158.7 2.2 copy.75
  160.8 1.0 reshape.554
  162.5 4.5 convolution_convert_fusion.1
  166.9 4.7 all-to-all-start
  172.5 41.0 %reduce-scatter.15.cloned.1.call-done = bf16[896,192]{1,0:T(8,128)(2,1)} async-done(((bf16[3584,192]{1,0:T(8,128)(2,1)}), bf16[896,192]{1,0:T(8,128)(2,1)}) %reduce-scatter.15.cloned.1.call-update) | async-done | bytes 344080
  213.5 0.8 slice.182
  214.3 1.0 slice.180
  215.6 1.0 fusion.62
  216.6 0.8 fusion.139
  217.8 1.7 reduce-window.25
  220.3 3.6 scatter_custom_fusion
  223.9 22.4 %all-gather.9.cloned.1.call-done = bf16[4,720,192]{1,2,0:T(8,128)(2,1)} async-done(((bf16[1,720,192]{1,2,0:T(8,128)(2,1)}), bf16[4,720,192]{1,2,0:T(8,128)(2,1)}) %all-gather.9.cloned.1.call-update) | async-done | bytes 1105936 | tf_op jit(solution)/shard_map/all_gather | solution.py:205
  246.4 3.2 copy.72
  249.6 2.7 reshape.552
  253.0 4.4 convolution_convert_fusion
  257.4 4.7 all-to-all-start.1
  262.1 10.4 %fusion.4 = f32[1024,720]{0,1:T(8,128)} fusion(bf16[1024,2944]{1,0:T(8,128)(2,1)} %bitcast.45, bf16[1,2880,720]{1,2,0:T(8,128)(2,1)} %param.38), kind=kOutput, calls=%fused_computation.16 | convolution fusion | flops 4246732800 | bytes 13125632 | tf_op jit(solution)/shard_map/dot_general | solution.py:238
  272.5 16.8 %convolution_convert_fusion.2 = bf16[1024,2944]{1,0:T(8,128)(2,1)} fusion(bf16[720,2880]{1,0:T(8,128)(2,1)} %bitcast.183, f32[1024,720]{0,1:T(8,128)} %fusion.4, bf16[1,2880,720]{1,2,0:T(8,128)(2,1)} %param.37, bf16[1024,2944]{1,0:T(8,128)(2,1)} %bitcast.45), kind=kOutput, calls=%fused_computation.12 | convolution fusion | flops 8596750336 | bytes 23302144 | tf_op jit(solution)/shard_map/dot_general | solution.py:243
  289.3 41.6 %all-to-all-done.1 = bf16[8,128,2944]{2,1,0:T(8,128)(2,1)} async-done(((bf16[8,128,2944]{2,1,0:T(8,128)(2,1)}), bf16[8,128,2944]{2,1,0:T(8,128)(2,1)}, u32[]{:S(2)}, u32[]{:S(2)}) %all-to-all-start.1) | async-done | bytes 6029344 | tf_op jit(solution)/shard_map/all_to_all | solution.py:231
  330.9 5.0 all-to-all-start.3
  335.9 10.4 %fusion.8 = f32[1024,720]{0,1:T(8,128)} fusion(bf16[1024,2944]{1,0:T(8,128)(2,1)} %bitcast.40, bf16[1,2880,720]{1,2,0:T(8,128)(2,1)} %param.38), kind=kOutput, calls=%fused_computation.20 | convolution fusion | flops 4246732800 | bytes 13125632 | tf_op jit(solution)/shard_map/dot_general | solution.py:238
  346.2 16.8 %convolution_convert_fusion.3 = bf16[1024,2944]{1,0:T(8,128)(2,1)} fusion(bf16[720,2880]{1,0:T(8,128)(2,1)} %bitcast.184, f32[1024,720]{0,1:T(8,128)} %fusion.8, bf16[1,2880,720]{1,2,0:T(8,128)(2,1)} %param.37, bf16[1024,2944]{1,0:T(8,128)(2,1)} %bitcast.40), kind=kOutput, calls=%fused_computation.13 | convolution fusion | flops 8596750336 | bytes 23302144 | tf_op jit(solution)/shard_map/dot_general | solution.py:243
  363.1 41.6 %all-to-all-done.3 = bf16[8,128,2944]{2,1,0:T(8,128)(2,1)} async-done(((bf16[8,128,2944]{2,1,0:T(8,128)(2,1)}), bf16[8,128,2944]{2,1,0:T(8,128)(2,1)}, u32[]{:S(2)}, u32[]{:S(2)}) %all-to-all-start.3) | async-done | bytes 6029344 | tf_op jit(solution)/shard_map/all_to_all | solution.py:247
  404.7 4.7 all-to-all-start.2
  410.0 5.8 %fusion.140 = (bf16[192,2880]{1,0:T(8,128)(2,1)}, f32[192,2880]{1,0:T(8,128)}) fusion(bf16[192,1024]{1,0:T(8,128)(2,1)S(1)} %fusion.51, bf16[1024,2944]{1,0:T(8,128)(2,1)} %bitcast.47), kind=kOutput, calls=%fused_computation.218 | convolution fusion | flops 1133015040 | bytes 9740288 | tf_op jit(solution)/shard_map/dot_general | solution.py:261
  415.8 2.5 copy.88
  419.1 2.2 gather_fusion
  421.3 30.4 %reduce-scatter.17.cloned.1.call-done = bf16[720,192]{1,0:T(8,128)(2,1)} async-done(((bf16[2880,192]{1,0:T(8,128)(2,1)}), bf16[720,192]{1,0:T(8,128)(2,1)}) %reduce-scatter.17.cloned.1.call-update) | async-done | bytes 276496
  451.8 1.8 copy.89
  453.6 24.6 %all-to-all-done.2 = bf16[8,128,2944]{2,1,0:T(8,128)(2,1)} async-done(((bf16[8,128,2944]{2,1,0:T(8,128)(2,1)}), bf16[8,128,2944]{2,1,0:T(8,128)(2,1)}, u32[]{:S(2)}, u32[]{:S(2)}) %all-to-all-start.2) | async-done | bytes 6029344 | tf_op jit(solution)/shard_map/all_to_all | solution.py:247
  478.2 5.8 %fusion.141 = (bf16[192,2880]{1,0:T(8,128)(2,1)}, f32[192,2880]{1,0:T(8,128)}) fusion(bf16[192,1024]{1,0:T(8,128)(2,1)S(1)} %fusion.50, bf16[1024,2944]{1,0:T(8,128)(2,1)} %bitcast.48), kind=kOutput, calls=%fused_computation.219 | convolution fusion | flops 1133015040 | bytes 9740288 | tf_op jit(solution)/shard_map/dot_general | solution.py:261
  484.0 2.2 gather_fusion.1
  486.7 2.4 pad_maximum_fusion.1
  489.0 2.6 copy.90
  491.6 1.2 gather_fusion.2
  492.8 1.2 gather_fusion.3
  494.0 28.9 %reduce-scatter.19.cloned.1.call-done = bf16[720,208]{1,0:T(8,128)(2,1)} async-done(((bf16[2880,208]{1,0:T(8,128)(2,1)}), bf16[720,208]{1,0:T(8,128)(2,1)}) %reduce-scatter.19.cloned.1.call-update) | async-done | bytes 299536
  522.9 1.1 copy.91
  524.7 1.1 add_convert_fusion
  525.8 1.0 copy.80
  526.8 0.9 reshape.498
  527.8 1.0 fusion.91
  528.8 9.2 %all-gather.2 = bf16[8,4,2880]{2,1,0:T(4,128)(2,1)S(1)} all-gather(bf16[1,4,2880]{2,1,0:T(4,128)(2,1)S(1)} %fusion.108), channel_id=1, replica_groups=mesh['dp'=4,'expert'=8] {'expert'}, dimensions={0}, use_global_device_ids=true | all-gather | bytes 207360 | tf_op jit(solution)/shard_map/all_gather | solution.py:290
  538.2 4.4 fusion.142
  (133 shorter events, 15.1 us)
Async XLA Ops:
  7.2 75.2 %copy-start = (bf16[512,2880]{0,1:T(8,128)(2,1)S(1)}, bf16[512,2880]{0,1:T(8,128)(2,1)}, u32[]{:S(2)}) copy-start(bf16[512,2880]{0,1:T(8,128)(2,1)} %param.31) | copy-start | bytes 8847364
  7.2 55.4 %copy-start.16 = (f32[2880]{0:T(1024)S(1)}, f32[2880]{0:T(1024)}, u32[]{:S(2)}) copy-start(f32[2880]{0:T(1024)} %param.28) | copy-start | bytes 34564
  7.2 53.2 %all-gather.7.cloned.1.call-start = ((), (), s32[]{:S(2)}) async-start(), calls=%async_computation.8 | async-start | bytes 2764800 | tf_op jit(solution)/shard_map/all_gather | solution.py:103
  7.9 117.9 %reduce-scatter.13.cloned.1.call-start = ((), (), s32[]{:S(2)}) async-start(), calls=%async_computation.11 | async-start | bytes 2293760
  12.4 0.9 copy-start.7
  62.6 5.9 %copy-start.15 = (bf16[128,1,640]{2,0,1:T(8,128)(2,1)S(1)}, bf16[128,1,640]{2,0,1:T(8,128)(2,1)}, u32[]{:S(2)}) copy-start(bf16[128,1,640]{2,0,1:T(8,128)(2,1)} %param.33) | copy-start | bytes 491524
  79.6 2.3 copy-start.9
  82.3 1.7 copy-start.8
  84.4 3.2 copy-start.2
  87.4 40.6 %copy-start.5 = (bf16[128,720]{0,1:T(8,128)(2,1)S(1)}, bf16[128,720]{0,1:T(8,128)(2,1)}, u32[]{:S(2)}) copy-start(bf16[128,720]{0,1:T(8,128)(2,1)} %param.35) | copy-start | bytes 552964
  87.4 71.3 %all-gather.11.cloned.1.call-start = ((), (), s32[]{:S(2)}) async-start(), calls=%async_computation.10 | async-start | bytes 1474560 | tf_op jit(solution)/shard_map/all_gather | solution.py:205
  132.5 29.6 %copy-start.10 = (f32[2880]{0:T(1024)S(1)}, f32[2880]{0:T(1024)}, u32[]{:S(2)}) copy-start(f32[2880]{0:T(1024)} %param.36) | copy-start | bytes 34564
  166.9 85.3 %all-to-all-start = ((bf16[8,128,2944]{2,1,0:T(8,128)(2,1)}), bf16[8,128,2944]{2,1,0:T(8,128)(2,1)}, u32[]{:S(2)}, u32[]{:S(2)}) async-start(bf16[8,128,2944]{2,1,0:T(8,128)(2,1)} %bitcast.149), calls=%async_computation | async-start | bytes 12058624 | tf_op jit(solution)/shard_map/all_to_all | solution.py:231
  171.7 43.9 %copy-start.6 = (bf16[128,720]{0,1:T(8,128)(2,1)S(1)}, bf16[128,720]{0,1:T(8,128)(2,1)}, u32[]{:S(2)}) copy-start(bf16[128,720]{0,1:T(8,128)(2,1)} %param.35) | copy-start | bytes 552964
  171.7 41.8 %reduce-scatter.15.cloned.1.call-start = ((), (), s32[]{:S(2)}) async-start(), calls=%async_computation.12 | async-start | bytes 2293760
  172.3 74.1 %all-gather.9.cloned.1.call-start = ((), (), s32[]{:S(2)}) async-start(), calls=%async_computation.9 | async-start | bytes 1474560 | tf_op jit(solution)/shard_map/all_gather | solution.py:205
  257.4 73.5 %all-to-all-start.1 = ((bf16[8,128,2944]{2,1,0:T(8,128)(2,1)}), bf16[8,128,2944]{2,1,0:T(8,128)(2,1)}, u32[]{:S(2)}, u32[]{:S(2)}) async-start(bf16[8,128,2944]{2,1,0:T(8,128)(2,1)} %bitcast.150), calls=%async_computation.1 | async-start | bytes 12058624 | tf_op jit(solution)/shard_map/all_to_all | solution.py:231
  330.9 73.8 %all-to-all-start.3 = ((bf16[8,128,2944]{2,1,0:T(8,128)(2,1)}), bf16[8,128,2944]{2,1,0:T(8,128)(2,1)}, u32[]{:S(2)}, u32[]{:S(2)}) async-start(bf16[8,128,2944]{2,1,0:T(8,128)(2,1)} %bitcast.158), calls=%async_computation.3 | async-start | bytes 12058624 | tf_op jit(solution)/shard_map/all_to_all | solution.py:247
  404.7 73.5 %all-to-all-start.2 = ((bf16[8,128,2944]{2,1,0:T(8,128)(2,1)}), bf16[8,128,2944]{2,1,0:T(8,128)(2,1)}, u32[]{:S(2)}, u32[]{:S(2)}) async-start(bf16[8,128,2944]{2,1,0:T(8,128)(2,1)} %bitcast.157), calls=%async_computation.2 | async-start | bytes 12058624 | tf_op jit(solution)/shard_map/all_to_all | solution.py:247
  409.4 42.4 %reduce-scatter.17.cloned.1.call-start = ((), (), s32[]{:S(2)}) async-start(), calls=%async_computation.13 | async-start | bytes 1843200
  418.4 104.5 %reduce-scatter.19.cloned.1.call-start = ((), (), s32[]{:S(2)}) async-start(), calls=%async_computation.14 | async-start | bytes 1843200
  418.6 67.7 %copy-start.12 = (pred[4]{0:T(512)(128)(4,1)}, pred[4]{0:T(512)(128)(4,1)S(1)}, u32[]{:S(2)}) copy-start(pred[4]{0:T(512)(128)(4,1)S(1)} %get-tuple-element.42) | copy-start | bytes 16
  418.6 67.7 %copy-start.13 = (pred[4]{0:T(512)(128)(4,1)}, pred[4]{0:T(512)(128)(4,1)S(1)}, u32[]{:S(2)}) copy-start(pred[4]{0:T(512)(128)(4,1)S(1)} %get-tuple-element.43) | copy-start | bytes 16
  418.6 67.7 %copy-start.14 = (pred[4]{0:T(512)(128)(4,1)}, pred[4]{0:T(512)(128)(4,1)S(1)}, u32[]{:S(2)}) copy-start(pred[4]{0:T(512)(128)(4,1)S(1)} %get-tuple-element.44) | copy-start | bytes 16
  489.0 35.6 %copy-start.3 = (bf16[192,720]{1,0:T(8,128)(2,1)S(1)}, bf16[192,720]{1,0:T(8,128)(2,1)}, u32[]{:S(2)}) copy-start(bf16[192,720]{1,0:T(8,128)(2,1)} %fusion.63) | copy-start | bytes 829444
  489.0 35.6 %copy-start.4 = (bf16[192,720]{1,0:T(8,128)(2,1)S(1)}, bf16[192,720]{1,0:T(8,128)(2,1)}, u32[]{:S(2)}) copy-start(bf16[192,720]{1,0:T(8,128)(2,1)} %fusion.62) | copy-start | bytes 829444
  491.6 37.1 %copy-start.11 = (f32[2880]{0:T(1024)S(1)}, f32[2880]{0:T(1024)}, u32[]{:S(2)}) copy-start(f32[2880]{0:T(1024)} %param.40) | copy-start | bytes 34564
  525.8 16.8 %copy-start.1 = (bf16[512,2880]{0,1:T(8,128)(2,1)S(1)}, bf16[512,2880]{0,1:T(8,128)(2,1)}, u32[]{:S(2)}) copy-start(bf16[512,2880]{0,1:T(8,128)(2,1)} %param.31) | copy-start | bytes 8847364
Sparse Core Ops, SparseCore 0:
  9.6 50.7 all-gather.6
  87.5 38.2 reduce-scatter.12
  129.0 29.5 all-gather.10
  174.5 38.9 reduce-scatter.14
  216.7 29.5 all-gather.8
  418.5 33.2 reduce-scatter.16
  491.7 31.0 reduce-scatter.18
